TPU v7x, 512 devices: a whole 4x8x8 slice. The times are simulated.
512 devices in a mesh: chan: 4 (over x), tile: 128 (over z, y, core).
Axes of the slice: x: 4, y: 8, z: 8, core: 2. Of those that a mesh axis runs over, the one named last changes fastest.
Arguments:
- visibilities: bfloat16 [131072, 1024], P('tile', 'chan'), parts along dimension 1, may hold values from -6 to 6
- send_list: int32 [65536, 8], P(('chan', 'tile')), parts along dimension 0, may hold values from -1 to 1023, as said below
- pixels: int32 [2, 524288], P(None, ('chan', 'tile')), parts along dimension 1, may hold values from 0 to 31
- offsets: int32 [2, 524288], P(None, ('chan', 'tile')), parts along dimension 1, may hold values from 0 to 15
- taper: float32 [8, 16], replicated, may hold values from 0.1 to 0.6
Outputs:
- tiles: float32 [128, 32, 32, 1024], P('tile', None, None, 'chan'), parts along dimension 3
There are 4 independent parts, one for each index of `chan`. A program takes and returns all parts, laid end to end along the dimension named above; an argument that names none is the same for every part. Nothing has to cross between parts.
Inputs may be any that keep to these rules, and one draw needn't show every extreme that they name: `send_list`: for every sender and tile the live entries come first and are distinct local row indices; no row is listed twice by one sender; the rest are -1. One tile, drawn from the seed, gets 8 live slots from every sender, and every sender lists its last row.
All inputs are finite; a program needn't handle non-finite values.
Results may differ from a plain program's by a relative error of at most 0.0029.
Values may be sent and summed in bfloat16 or wider, within the bound.
No kernel may reach another device: no remote copies, remote signals or barrier semaphores. Data moves between devices by JAX's collectives and lax.ppermute only.
A program may use at most 64 MiB of HBM per device.

v0:
```python
import jax
import jax.numpy as jnp
from jax import lax
from jax.sharding import PartitionSpec as P

TS = 32
TILES_Y = 8


def passed_along(value, axis, by):
    count = lax.axis_size(axis)
    pairs = [(i, i + by) for i in range(count) if 0 <= i + by < count]
    return lax.ppermute(value, axis, pairs)


def spread(kernel, pixel, padded_side):
    cell_index = jnp.arange(padded_side, dtype=jnp.int32)[:, None] - pixel[None, :]
    tap_index = jnp.arange(kernel.shape[0], dtype=jnp.int32)[:, None, None]
    return jnp.sum(jnp.where(cell_index[None] == tap_index, kernel[:, None, :], 0.0), axis=0)


def place_block(block_rows, block_meta, taper, padded_side):
    levels = jnp.arange(taper.shape[1], dtype=jnp.int32)[:, None]
    select_u = (levels == block_meta[2][None, :]).astype(jnp.float32)
    select_v = (levels == block_meta[3][None, :]).astype(jnp.float32)
    kernel_u = jnp.dot(
        taper, select_u, precision=lax.Precision.HIGHEST, preferred_element_type=jnp.float32
    )
    kernel_v = jnp.dot(
        taper, select_v, precision=lax.Precision.HIGHEST, preferred_element_type=jnp.float32
    )
    spread_u = spread(kernel_u, block_meta[0], padded_side)
    spread_v = spread(kernel_v, block_meta[1], padded_side)
    weights = (spread_u[:, None, :] * spread_v[None, :, :]).astype(jnp.bfloat16)
    weights = weights.reshape(padded_side * padded_side, -1)
    return jnp.dot(weights, block_rows, preferred_element_type=jnp.float32)


def grid_blocks(slot_rows, slot_meta, taper, padded_side, block_size, block_count):
    width = slot_rows.shape[1]

    def one_block(index, running):
        start = index * block_size
        block_rows = lax.dynamic_slice_in_dim(slot_rows, start, block_size, 0)
        block_meta = lax.dynamic_slice_in_dim(slot_meta, start, block_size, 1)
        return running + place_block(block_rows, block_meta, taper, padded_side)

    initial = jnp.zeros((padded_side * padded_side, width), jnp.float32)
    return lax.fori_loop(0, block_count, one_block, initial)


def body(visibilities, send_list, pixels, offsets, taper):
    tile_count = lax.axis_size("tile")
    tiles_x = tile_count // TILES_Y
    slot_cap = send_list.shape[1]
    components = visibilities.shape[1]
    padded_side = TS + 8
    slot_total = tile_count * slot_cap
    block_size = min(512, slot_total)
    is_live = send_list >= 0
    picked = jnp.where(is_live, send_list, 0).reshape(-1)
    gathered = jnp.take(visibilities, picked, axis=0).reshape(tile_count, slot_cap, components)
    outgoing = jnp.where(is_live[:, :, None], gathered, jnp.zeros_like(gathered))
    live_flag = is_live.reshape(1, -1)
    slot_meta = jnp.concatenate(
        [
            jnp.take(pixels, picked, axis=1),
            jnp.take(offsets, picked, axis=1),
            live_flag.astype(jnp.int32),
        ],
        0,
    )
    slot_meta = (
        jnp.where(live_flag, slot_meta, 0).reshape(5, tile_count, slot_cap).transpose(1, 0, 2)
    )
    arrived_meta = lax.all_to_all(slot_meta, "tile", split_axis=0, concat_axis=0, tiled=True)
    meta_rows = arrived_meta.transpose(1, 0, 2).reshape(5, slot_total)
    arrived = lax.all_to_all(outgoing, "tile", split_axis=0, concat_axis=0, tiled=True)
    padded_grid = grid_blocks(
        arrived.reshape(slot_total, components),
        meta_rows,
        taper,
        padded_side,
        block_size,
        slot_total // block_size,
    )
    padded_grid = padded_grid.reshape(padded_side, padded_side, components)
    tile_row = lax.axis_index("tile") % TILES_Y
    source_start = {-1: TS + 4, 0: 4, 1: 0}
    target_start = {-1: 0, 0: 0, 1: TS - 4}
    span = {-1: 4, 0: TS, 1: 4}
    result = padded_grid[4 : TS + 4, 4 : TS + 4]
    for step_x in (-1, 0, 1):
        for step_y in (-1, 0, 1):
            if step_x == 0 and step_y == 0 or (step_x != 0 and tiles_x == 1):
                continue
            piece = padded_grid[
                source_start[step_x] : source_start[step_x] + span[step_x],
                source_start[step_y] : source_start[step_y] + span[step_y],
            ]
            incoming = passed_along(piece, "tile", -(step_x * TILES_Y + step_y))
            inside = (tile_row + step_y >= 0) & (tile_row + step_y < TILES_Y)
            incoming = jnp.where(inside, incoming, 0.0)
            result = result.at[
                target_start[step_x] : target_start[step_x] + span[step_x],
                target_start[step_y] : target_start[step_y] + span[step_y],
            ].add(incoming)
    return result[None]


def solution(mesh):
    placed = (
        P("tile", "chan"),
        P(("chan", "tile"), None),
        P(None, ("chan", "tile")),
        P(None, ("chan", "tile")),
        P(),
    )
    return jax.shard_map(
        body, mesh=mesh, in_specs=placed, out_specs=P("tile", None, None, "chan"), check_vma=False
    )
```

profile of v0, /device:TPU:76, one launch (start us, length us, event | category | flops | bytes accessed | tf_op | source)
XLA Modules:
  0.0 124.5 jit_solution(2578457371777047928)
XLA Ops:
  0.0 0.8 compare_and_fusion.1
  0.8 0.1 copy.49
  0.9 0.1 reshape.405
  1.0 0.9 copy.50
  1.9 0.9 copy.51
  2.8 2.8 %gather_fusion.1 = s32[1024,2]{1,0:T(8,128)S(1)} fusion(s32[2,1024]{0,1:T(8,128)S(1)} %copy.50, s32[1024]{0:T(1024)S(1)} %fusion.13), kind=kCustom, calls=%fused_computation.clone | custom fusion | bytes 20480 | tf_op jit(solution)/shard_map/jit(_take)/gather | solution.py:67
  5.6 2.8 %gather_fusion.2 = s32[1024,2]{1,0:T(8,128)S(1)} fusion(s32[2,1024]{0,1:T(8,128)S(1)} %copy.51, s32[1024]{0:T(1024)S(1)} %fusion.13), kind=kCustom, calls=%fused_computation.1.clone | custom fusion | bytes 20480 | tf_op jit(solution)/shard_map/jit(_take)/gather | solution.py:68
  8.5 0.2 select_bitcast_fusion.1
  8.7 0.2 copy.53
  8.9 0.2 copy.52
  9.1 1.0 copy.54
  10.1 16.5 %all-to-all-start = ((s32[128,5,8]{2,1,0:T(8,128)}), s32[128,5,8]{2,1,0:T(8,128)S(1)}, u32[]{:S(2)}, u32[]{:S(2)}) async-start(s32[128,5,8]{2,1,0:T(8,128)} %copy.54), calls=%async_computation | async-start | bytes 1048576 | tf_op jit(solution)/shard_map/all_to_all | solution.py:76
  26.6 0.1 reshape.407
  26.7 0.1 copy.56
  26.9 0.1 copy.57
  27.0 3.9 %gather_fusion = bf16[1024,256]{1,0:T(8,128)(2,1)S(1)} fusion(bf16[1024,256]{1,0:T(8,128)(2,1)S(1)} %copy-done, s32[1024]{0:T(1024)S(1)} %broadcast_clamp_fusion), kind=kCustom, calls=%fused_computation.2 | custom fusion | bytes 1052672 | tf_op jit(solution)/shard_map/jit(_take)/gather | solution.py:62
  30.9 0.0 copy-start.3
  31.0 0.0 copy-start.2
  31.0 1.2 fusion.4
  32.1 13.9 %all-to-all-done = s32[128,5,8]{2,1,0:T(8,128)S(1)} async-done(((s32[128,5,8]{2,1,0:T(8,128)}), s32[128,5,8]{2,1,0:T(8,128)S(1)}, u32[]{:S(2)}, u32[]{:S(2)}) %all-to-all-start) | async-done | bytes 20512 | tf_op jit(solution)/shard_map/all_to_all | solution.py:76
  46.0 6.6 %all-to-all-start.1 = ((bf16[128,8,256]{2,1,0:T(8,128)(2,1)}), bf16[128,8,256]{2,1,0:T(8,128)(2,1)S(1)}, u32[]{:S(2)}, u32[]{:S(2)}) async-start(bf16[128,8,256]{2,1,0:T(8,128)(2,1)} %fusion.4), calls=%async_computation.1 | async-start | bytes 1048576 | tf_op jit(solution)/shard_map/all_to_all | solution.py:78
  52.6 0.6 fusion.17
  53.3 0.8 and_reduce_fusion
  54.0 0.1 copy.55
  54.1 0.2 reshape.406
  54.3 17.7 %all-to-all-done.1 = bf16[128,8,256]{2,1,0:T(8,128)(2,1)S(1)} async-done(((bf16[128,8,256]{2,1,0:T(8,128)(2,1)}), bf16[128,8,256]{2,1,0:T(8,128)(2,1)S(1)}, u32[]{:S(2)}, u32[]{:S(2)}) %all-to-all-start.1) | async-done | bytes 524320 | tf_op jit(solution)/shard_map/all_to_all | solution.py:78
  72.0 6.9 %while.22 = (s32[]{:T(128)}, f32[1600,256]{1,0:T(8,128)}, s32[5,1024]{1,0:T(8,128)S(1)}, f32[8,16]{1,0:T(8,128)S(1)}, bf16[1024,256]{1,0:T(8,128)(2,1)S(1)}, /*i...) while((s32[]{:T(128)}, f32[1600,256]{1,0:T(8,128)}, ...), condition=%wide.region_3.5_spmd.clone, body=%wide.region_0.4_spmd.clone.sunk | while | flops 424460288 | bytes 7562477 | solution.py:49
  72.0 0.1 constant_dynamic-slice_fusion.2
  72.1 0.1 convolution_bitcast_fusion.4
  72.2 0.1 convolution_bitcast_fusion.5
  72.4 0.1 select_reduce_fusion.3
  72.5 0.4 multiply_convert_fusion.2
  72.9 1.8 %convolution_add_fusion.2 = f32[1600,256]{1,0:T(8,128)} fusion(bf16[1600,512]{1,0:T(8,128)(2,1)S(1)} %bitcast.61, f32[1600,256]{1,0:T(8,128)} %get-tuple-element.304, pred[]{:T(512)S(6)} %compare.54, bf16[1024,256]{1,0:T(8,128)(2,1)S(1)} %get-tuple-element.319, s32[]{:T(128)S(6)} %select_n.193), kind=kOutput, calls=%fused_computation.4.clone.1 | convolution fusion | flops 420249600 | bytes 5177349 | tf_op jit(solution)/shard_map/while/body/eval_jaxpr/dot_general | solution.py:36
  74.7 0.1 constant_dynamic-slice_fusion.2
  74.8 0.1 convolution_bitcast_fusion.4
  75.0 0.1 convolution_bitcast_fusion.5
  75.1 0.1 select_reduce_fusion.3
  75.2 0.4 multiply_convert_fusion.2
  75.6 3.2 %convolution_add_fusion.2 = f32[1600,256]{1,0:T(8,128)} fusion(bf16[1600,512]{1,0:T(8,128)(2,1)S(1)} %bitcast.61, f32[1600,256]{1,0:T(8,128)} %get-tuple-element.304, pred[]{:T(512)S(6)} %compare.54, bf16[1024,256]{1,0:T(8,128)(2,1)S(1)} %get-tuple-element.319, s32[]{:T(128)S(6)} %select_n.193), kind=kOutput, calls=%fused_computation.4.clone.1 | convolution fusion | flops 420249600 | bytes 5177349 | tf_op jit(solution)/shard_map/while/body/eval_jaxpr/dot_general | solution.py:36
  78.9 0.8 fusion.14
  79.7 1.1 fusion.16
  80.8 3.6 %collective-permute-start = (f32[4,4,256]{2,1,0:T(4,128)S(1)}, f32[4,4,256]{2,1,0:T(4,128)S(1)}, u32[]{:S(2)}, u32[]{:S(2)}) collective-permute-start(f32[4,4,256]{2,1,0:T(4,128)S(1)} %get-tuple-element.239), channel_id=1, source_target_pairs={{0,9},{1,10},{2,11},{3,12},{4,13},{5,14},{6,15},{7,16},{8,17},{9,1... | collective-permute-start | bytes 49160 | tf_op jit(solution)/shard_map/ppermute | solution.py:13
  84.3 1.0 fusion.15
  85.4 1.5 %slice.304 = f32[32,32,256]{2,1,0:T(8,128)S(1)} slice(f32[40,40,256]{2,1,0:T(8,128)} %bitcast.65), slice={[4:36], [4:36], [0:256]} | slice | bytes 2097152 | tf_op jit(solution)/shard_map/slice | solution.py:92
  86.8 6.0 %collective-permute-start.1 = (f32[4,32,256]{2,1,0:T(8,128)S(1)}, f32[4,32,256]{2,1,0:T(8,128)S(1)}, u32[]{:S(2)}, u32[]{:S(2)}) collective-permute-start(f32[4,32,256]{2,1,0:T(8,128)S(1)} %get-tuple-element.241), channel_id=1, source_target_pairs={{0,8},{1,9},{2,10},{3,11},{4,12},{5,13},{6,14},{7,15},{8,16},{9,17... | collective-permute-start | bytes 393224 | tf_op jit(solution)/shard_map/ppermute | solution.py:13
  92.8 2.5 %collective-permute-start.2 = (f32[4,4,256]{2,1,0:T(4,128)S(1)}, f32[4,4,256]{2,1,0:T(4,128)S(1)}, u32[]{:S(2)}, u32[]{:S(2)}) collective-permute-start(f32[4,4,256]{2,1,0:T(4,128)S(1)} %get-tuple-element.238), channel_id=1, source_target_pairs={{0,7},{1,8},{2,9},{3,10},{4,11},{5,12},{6,13},{7,14},{8,15},{9,16}... | collective-permute-start | bytes 49160 | tf_op jit(solution)/shard_map/ppermute | solution.py:13
  95.3 3.5 %collective-permute-start.3 = (f32[32,4,256]{2,1,0:T(4,128)S(1)}, f32[32,4,256]{2,1,0:T(4,128)S(1)}, u32[]{:S(2)}, u32[]{:S(2)}) collective-permute-start(f32[32,4,256]{2,1,0:T(4,128)S(1)} %get-tuple-element.243), channel_id=1, source_target_pairs={{0,1},{1,2},{2,3},{3,4},{4,5},{5,6},{6,7},{7,8},{8,9},{9,10},{10,1... | collective-permute-start | bytes 393224 | tf_op jit(solution)/shard_map/ppermute | solution.py:13
  98.8 2.1 %collective-permute-start.4 = (f32[32,4,256]{2,1,0:T(4,128)S(1)}, f32[32,4,256]{2,1,0:T(4,128)S(1)}, u32[]{:S(2)}, u32[]{:S(2)}) collective-permute-start(f32[32,4,256]{2,1,0:T(4,128)S(1)} %get-tuple-element.242), channel_id=1, source_target_pairs={{1,0},{2,1},{3,2},{4,3},{5,4},{6,5},{7,6},{8,7},{9,8},{10,9},{11,1... | collective-permute-start | bytes 393224 | tf_op jit(solution)/shard_map/ppermute | solution.py:13
  100.9 0.0 collective-permute-done
  100.9 6.6 %collective-permute-start.5 = (f32[4,4,256]{2,1,0:T(4,128)S(1)}, f32[4,4,256]{2,1,0:T(4,128)S(1)}, u32[]{:S(2)}, u32[]{:S(2)}) collective-permute-start(f32[4,4,256]{2,1,0:T(4,128)S(1)} %get-tuple-element.237), channel_id=1, source_target_pairs={{7,0},{8,1},{9,2},{10,3},{11,4},{12,5},{13,6},{14,7},{15,8},{16,9}... | collective-permute-start | bytes 49160 | tf_op jit(solution)/shard_map/ppermute | solution.py:13
  107.6 0.8 fusion.12
  108.3 3.8 %collective-permute-start.6 = (f32[4,32,256]{2,1,0:T(8,128)S(1)}, f32[4,32,256]{2,1,0:T(8,128)S(1)}, u32[]{:S(2)}, u32[]{:S(2)}) collective-permute-start(f32[4,32,256]{2,1,0:T(8,128)S(1)} %get-tuple-element.240), channel_id=1, source_target_pairs={{8,0},{9,1},{10,2},{11,3},{12,4},{13,5},{14,6},{15,7},{16,8},{17,9... | collective-permute-start | bytes 393224 | tf_op jit(solution)/shard_map/ppermute | solution.py:13
  112.2 0.0 collective-permute-done.2
  112.2 1.9 %collective-permute-start.7 = (f32[4,4,256]{2,1,0:T(4,128)S(1)}, f32[4,4,256]{2,1,0:T(4,128)S(1)}, u32[]{:S(2)}, u32[]{:S(2)}) collective-permute-start(f32[4,4,256]{2,1,0:T(4,128)S(1)} %get-tuple-element.236), channel_id=1, source_target_pairs={{9,0},{10,1},{11,2},{12,3},{13,4},{14,5},{15,6},{16,7},{17,8},{18,... | collective-permute-start | bytes 49160 | tf_op jit(solution)/shard_map/ppermute | solution.py:13
  114.1 1.9 %add_select_fusion = f32[4,4,256]{2,1,0:T(4,128)S(1)} fusion(f32[4,4,256]{2,1,0:T(4,128)S(1)} %collective-permute-done.2, f32[32,32,256]{2,1,0:T(8,128)S(1)} %fusion.7, s32[]{:T(128)} %bitcast.11, s32[]{:T(128)} %bitcast.12, pred[]{:T(512)S(6)} %and.64, pred[]{:T(512)} %and_reduce_fusion), kind=kLoop, calls=%fused_computation.32 | loop fusion | flops 12288 | bytes 49162 | tf_op jit(solution)/shard_map/select.10
  116.0 1.4 %scatter-add.30 = f32[32,32,256]{2,1,0:T(8,128)S(1)} dynamic-update-slice(f32[32,32,256]{2,1,0:T(8,128)S(1)} %fusion.7, f32[4,4,256]{2,1,0:T(4,128)S(1)} %add_select_fusion, s32[]{:T(128)} %bitcast.11, s32[]{:T(128)} %bitcast.12, s32[]{:T(128)} %constant.294.clone.1) | dynamic-update-slice | bytes 32772 | tf_op jit(solution)/shard_map/scatter-add | solution.py:107
  117.4 0.0 collective-permute-done.3
  117.4 0.1 fusion.6
  117.5 0.1 fusion.5
  117.6 0.1 copy.71
  117.7 5.2 %collective-permute-done.6 = f32[4,32,256]{2,1,0:T(8,128)S(1)} collective-permute-done((f32[4,32,256]{2,1,0:T(8,128)S(1)}, f32[4,32,256]{2,1,0:T(8,128)S(1)}, u32[]{:S(2)}, u32[]{:S(2)}) %collective-permute-start.6) | collective-permute-done | bytes 131104 | tf_op jit(solution)/shard_map/ppermute | solution.py:13
  122.9 0.0 copy-start.1
  122.9 0.9 copy-done.1
  123.9 0.6 fusion.10
  (23 shorter events, 0.2 us)
Async XLA Ops:
  0.0 27.0 %copy-start = (bf16[1024,256]{1,0:T(8,128)(2,1)S(1)}, bf16[1024,256]{1,0:T(8,128)(2,1)}, u32[]{:S(2)}) copy-start(bf16[1024,256]{1,0:T(8,128)(2,1)} %param.25) | copy-start | bytes 1572868
  10.1 35.9 %all-to-all-start = ((s32[128,5,8]{2,1,0:T(8,128)}), s32[128,5,8]{2,1,0:T(8,128)S(1)}, u32[]{:S(2)}, u32[]{:S(2)}) async-start(s32[128,5,8]{2,1,0:T(8,128)} %copy.54), calls=%async_computation | async-start | bytes 1048576 | tf_op jit(solution)/shard_map/all_to_all | solution.py:76
  30.9 22.3 %copy-start.3 = (s32[3]{0:T(128)S(1)}, s32[3]{0:T(128)}, u32[]{:S(2)}) copy-start(s32[3]{0:T(128)} %constant.306.clone.1) | copy-start | bytes 40
  31.0 41.0 %copy-start.2 = (f32[8,16]{1,0:T(8,128)S(1)}, f32[8,16]{1,0:T(8,128)}, u32[]{:S(2)}) copy-start(f32[8,16]{1,0:T(8,128)} %param.29) | copy-start | bytes 1540
  46.0 26.0 %all-to-all-start.1 = ((bf16[128,8,256]{2,1,0:T(8,128)(2,1)}), bf16[128,8,256]{2,1,0:T(8,128)(2,1)S(1)}, u32[]{:S(2)}, u32[]{:S(2)}) async-start(bf16[128,8,256]{2,1,0:T(8,128)(2,1)} %fusion.4), calls=%async_computation.1 | async-start | bytes 1048576 | tf_op jit(solution)/shard_map/all_to_all | solution.py:78
  80.8 20.1 %collective-permute-start = (f32[4,4,256]{2,1,0:T(4,128)S(1)}, f32[4,4,256]{2,1,0:T(4,128)S(1)}, u32[]{:S(2)}, u32[]{:S(2)}) collective-permute-start(f32[4,4,256]{2,1,0:T(4,128)S(1)} %get-tuple-element.239), channel_id=1, source_target_pairs={{0,9},{1,10},{2,11},{3,12},{4,13},{5,14},{6,15},{7,16},{8,17},{9,1... | collective-permute-start | bytes 49160 | tf_op jit(solution)/shard_map/ppermute | solution.py:13
  86.8 21.5 %collective-permute-start.1 = (f32[4,32,256]{2,1,0:T(8,128)S(1)}, f32[4,32,256]{2,1,0:T(8,128)S(1)}, u32[]{:S(2)}, u32[]{:S(2)}) collective-permute-start(f32[4,32,256]{2,1,0:T(8,128)S(1)} %get-tuple-element.241), channel_id=1, source_target_pairs={{0,8},{1,9},{2,10},{3,11},{4,12},{5,13},{6,14},{7,15},{8,16},{9,17... | collective-permute-start | bytes 393224 | tf_op jit(solution)/shard_map/ppermute | solution.py:13
  92.8 19.4 %collective-permute-start.2 = (f32[4,4,256]{2,1,0:T(4,128)S(1)}, f32[4,4,256]{2,1,0:T(4,128)S(1)}, u32[]{:S(2)}, u32[]{:S(2)}) collective-permute-start(f32[4,4,256]{2,1,0:T(4,128)S(1)} %get-tuple-element.238), channel_id=1, source_target_pairs={{0,7},{1,8},{2,9},{3,10},{4,11},{5,12},{6,13},{7,14},{8,15},{9,16}... | collective-permute-start | bytes 49160 | tf_op jit(solution)/shard_map/ppermute | solution.py:13
  95.3 22.1 %collective-permute-start.3 = (f32[32,4,256]{2,1,0:T(4,128)S(1)}, f32[32,4,256]{2,1,0:T(4,128)S(1)}, u32[]{:S(2)}, u32[]{:S(2)}) collective-permute-start(f32[32,4,256]{2,1,0:T(4,128)S(1)} %get-tuple-element.243), channel_id=1, source_target_pairs={{0,1},{1,2},{2,3},{3,4},{4,5},{5,6},{6,7},{7,8},{8,9},{9,10},{10,1... | collective-permute-start | bytes 393224 | tf_op jit(solution)/shard_map/ppermute | solution.py:13
  98.8 18.7 %collective-permute-start.4 = (f32[32,4,256]{2,1,0:T(4,128)S(1)}, f32[32,4,256]{2,1,0:T(4,128)S(1)}, u32[]{:S(2)}, u32[]{:S(2)}) collective-permute-start(f32[32,4,256]{2,1,0:T(4,128)S(1)} %get-tuple-element.242), channel_id=1, source_target_pairs={{1,0},{2,1},{3,2},{4,3},{5,4},{6,5},{7,6},{8,7},{9,8},{10,9},{11,1... | collective-permute-start | bytes 393224 | tf_op jit(solution)/shard_map/ppermute | solution.py:13
  100.9 16.7 %collective-permute-start.5 = (f32[4,4,256]{2,1,0:T(4,128)S(1)}, f32[4,4,256]{2,1,0:T(4,128)S(1)}, u32[]{:S(2)}, u32[]{:S(2)}) collective-permute-start(f32[4,4,256]{2,1,0:T(4,128)S(1)} %get-tuple-element.237), channel_id=1, source_target_pairs={{7,0},{8,1},{9,2},{10,3},{11,4},{12,5},{13,6},{14,7},{15,8},{16,9}... | collective-permute-start | bytes 49160 | tf_op jit(solution)/shard_map/ppermute | solution.py:13
  108.3 14.5 %collective-permute-start.6 = (f32[4,32,256]{2,1,0:T(8,128)S(1)}, f32[4,32,256]{2,1,0:T(8,128)S(1)}, u32[]{:S(2)}, u32[]{:S(2)}) collective-permute-start(f32[4,32,256]{2,1,0:T(8,128)S(1)} %get-tuple-element.240), channel_id=1, source_target_pairs={{8,0},{9,1},{10,2},{11,3},{12,4},{13,5},{14,6},{15,7},{16,8},{17,9... | collective-permute-start | bytes 393224 | tf_op jit(solution)/shard_map/ppermute | solution.py:13
  112.2 10.7 %collective-permute-start.7 = (f32[4,4,256]{2,1,0:T(4,128)S(1)}, f32[4,4,256]{2,1,0:T(4,128)S(1)}, u32[]{:S(2)}, u32[]{:S(2)}) collective-permute-start(f32[4,4,256]{2,1,0:T(4,128)S(1)} %get-tuple-element.236), channel_id=1, source_target_pairs={{9,0},{10,1},{11,2},{12,3},{13,4},{14,5},{15,6},{16,7},{17,8},{18,... | collective-permute-start | bytes 49160 | tf_op jit(solution)/shard_map/ppermute | solution.py:13
  122.9 1.0 copy-start.1
where the time goes:
time: 125 us; the launch traced here: 124 us
  starting transfers between devices  53 us (42%)
  waiting for transfers between devices  36.8 us (29%)
  local copies, waits for them, and re-layouts  21.3 us (17%)
  other arithmetic  7.5 us (6%)
  matrix products  5.54 us (4%)
    ppermute x8, starting transfers between devices, passed_along(): return lax.ppermute(value, axis, pairs)  29.9 us
    all_to_all x1, waiting for transfers between devices, body(): lax.all_to_all(outgoing, 'tile', split_axis=0, concat_axis=0, tiled=True)  17.7 us
    all_to_all x1, starting transfers between devices, body(): lax.all_to_all(slot_meta, 'tile', split_axis=0, concat_axis=0, tiled=True)  16.5 us
    all_to_all x1, waiting for transfers between devices, body(): lax.all_to_all(slot_meta, 'tile', split_axis=0, concat_axis=0, tiled=True)  13.9 us
    all_to_all x1, starting transfers between devices, body(): lax.all_to_all(outgoing, 'tile', split_axis=0, concat_axis=0, tiled=True)  6.55 us
    ppermute x8, waiting for transfers between devices, passed_along(): return lax.ppermute(value, axis, pairs)  5.22 us
    dot_general x2, matrix products, place_block(): return jnp.dot(weights, block_rows, preferred_element_type=jnp.float32)  5.01 us
    gather x1, local copies, waits for them, and re-layouts, body(): jnp.take(visibilities, picked, axis=0)  3.94 us
  transfers between devices with their start and end apart: 10, of which 3 were waited for; matrix products, arithmetic and copies ran while one was open for 11% of the time, Pallas kernels for 0%

commit v1 on v0

--- a/solution.py
+++ b/solution.py
@@ -5,6 +5,7 @@
 
 TS = 32
 TILES_Y = 8
+META = 4
 
 
 def passed_along(value, axis, by):
@@ -51,60 +52,59 @@
 
 def body(visibilities, send_list, pixels, offsets, taper):
     tile_count = lax.axis_size("tile")
-    tiles_x = tile_count // TILES_Y
     slot_cap = send_list.shape[1]
-    components = visibilities.shape[1]
+    rows_dev, components = visibilities.shape
     padded_side = TS + 8
     slot_total = tile_count * slot_cap
     block_size = min(512, slot_total)
-    is_live = send_list >= 0
-    picked = jnp.where(is_live, send_list, 0).reshape(-1)
-    gathered = jnp.take(visibilities, picked, axis=0).reshape(tile_count, slot_cap, components)
-    outgoing = jnp.where(is_live[:, :, None], gathered, jnp.zeros_like(gathered))
-    live_flag = is_live.reshape(1, -1)
-    slot_meta = jnp.concatenate(
+
+    listed = send_list.reshape(-1)
+    row_ids = jnp.arange(rows_dev, dtype=jnp.int32)
+    chosen = (listed[:, None] == row_ids[None, :]).astype(jnp.bfloat16)
+    outgoing = jnp.dot(chosen, visibilities, preferred_element_type=jnp.float32)
+    outgoing = outgoing.astype(jnp.bfloat16)
+    meta_src = jnp.concatenate([pixels, offsets], 0).astype(jnp.bfloat16)
+    slot_meta = lax.dot_general(
+        chosen, meta_src, (((1,), (1,)), ((), ())), preferred_element_type=jnp.float32
+    ).astype(jnp.bfloat16)
+    packed = jnp.concatenate(
         [
-            jnp.take(pixels, picked, axis=1),
-            jnp.take(offsets, picked, axis=1),
-            live_flag.astype(jnp.int32),
+            outgoing.reshape(tile_count, slot_cap * components),
+            slot_meta.reshape(tile_count, slot_cap * META),
         ],
-        0,
+        1,
     )
-    slot_meta = (
-        jnp.where(live_flag, slot_meta, 0).reshape(5, tile_count, slot_cap).transpose(1, 0, 2)
+    arrived = lax.all_to_all(packed, "tile", split_axis=0, concat_axis=0, tiled=True)
+    arrived_rows = arrived[:, : slot_cap * components].reshape(slot_total, components)
+    meta_rows = (
+        arrived[:, slot_cap * components :]
+        .reshape(slot_total, META)
+        .astype(jnp.int32)
+        .transpose(1, 0)
     )
-    arrived_meta = lax.all_to_all(slot_meta, "tile", split_axis=0, concat_axis=0, tiled=True)
-    meta_rows = arrived_meta.transpose(1, 0, 2).reshape(5, slot_total)
-    arrived = lax.all_to_all(outgoing, "tile", split_axis=0, concat_axis=0, tiled=True)
     padded_grid = grid_blocks(
-        arrived.reshape(slot_total, components),
+        arrived_rows,
         meta_rows,
         taper,
         padded_side,
         block_size,
         slot_total // block_size,
     )
-    padded_grid = padded_grid.reshape(padded_side, padded_side, components)
+    grid = padded_grid.reshape(padded_side, padded_side, components)
+
+    from_below = passed_along(grid[0:4], "tile", -TILES_Y)
+    from_above = passed_along(grid[TS + 4 : TS + 8], "tile", TILES_Y)
+    grid = grid.at[TS : TS + 4].add(from_below)
+    grid = grid.at[4:8].add(from_above)
     tile_row = lax.axis_index("tile") % TILES_Y
-    source_start = {-1: TS + 4, 0: 4, 1: 0}
-    target_start = {-1: 0, 0: 0, 1: TS - 4}
-    span = {-1: 4, 0: TS, 1: 4}
-    result = padded_grid[4 : TS + 4, 4 : TS + 4]
-    for step_x in (-1, 0, 1):
-        for step_y in (-1, 0, 1):
-            if step_x == 0 and step_y == 0 or (step_x != 0 and tiles_x == 1):
-                continue
-            piece = padded_grid[
-                source_start[step_x] : source_start[step_x] + span[step_x],
-                source_start[step_y] : source_start[step_y] + span[step_y],
-            ]
-            incoming = passed_along(piece, "tile", -(step_x * TILES_Y + step_y))
-            inside = (tile_row + step_y >= 0) & (tile_row + step_y < TILES_Y)
-            incoming = jnp.where(inside, incoming, 0.0)
-            result = result.at[
-                target_start[step_x] : target_start[step_x] + span[step_x],
-                target_start[step_y] : target_start[step_y] + span[step_y],
-            ].add(incoming)
+    inner = grid[4 : TS + 4]
+    from_next = passed_along(inner[:, 0:4], "tile", -1)
+    from_prev = passed_along(inner[:, TS + 4 : TS + 8], "tile", 1)
+    from_next = jnp.where(tile_row + 1 < TILES_Y, from_next, 0.0)
+    from_prev = jnp.where(tile_row >= 1, from_prev, 0.0)
+    result = inner[:, 4 : TS + 4]
+    result = result.at[:, TS - 4 : TS].add(from_next)
+    result = result.at[:, 0:4].add(from_prev)
     return result[None]
 
 

time: 125 us -> 94.5 us (0.76)
  the two profiles are of different devices: /device:TPU:76 before, /device:TPU:132 now
where the time goes in v1:
time: 94.5 us; the launch traced here: 94 us
  waiting for transfers between devices  37 us (39%)
  starting transfers between devices  29.8 us (32%)
  local copies, waits for them, and re-layouts  12 us (13%)
  other arithmetic  7.59 us (8%)
  matrix products  7.29 us (8%)
    all_to_all x1, waiting for transfers between devices, body(): lax.all_to_all(packed, 'tile', split_axis=0, concat_axis=0, tiled=True)  19.2 us
    ppermute x4, waiting for transfers between devices, passed_along(): return lax.ppermute(value, axis, pairs)  17.7 us
    all_to_all x1, starting transfers between devices, body(): lax.all_to_all(packed, 'tile', split_axis=0, concat_axis=0, tiled=True)  15.8 us
    ppermute x4, starting transfers between devices, passed_along(): return lax.ppermute(value, axis, pairs)  14.1 us
    dot_general x2, matrix products, place_block(): return jnp.dot(weights, block_rows, preferred_element_type=jnp.float32)  4.99 us
    unnamed x10, local copies, waits for them, and re-layouts  4.35 us
    all_to_all x2, local copies, waits for them, and re-layouts, body(): lax.all_to_all(packed, 'tile', split_axis=0, concat_axis=0, tiled=True)  1.99 us
  transfers between devices with their start and end apart: 5, of which 4 were waited for; matrix products, arithmetic and copies ran while one was open for 4% of the time, Pallas kernels for 0%

profile of v1, /device:TPU:132, one launch (start us, length us, event | category | flops | bytes accessed | tf_op | source)
XLA Modules:
  0.0 94.0 jit_solution(8558255049578933418)
XLA Ops:
  0.0 0.0 copy-start
  0.0 0.8 copy.29
  0.8 0.1 eq.141
  0.9 0.7 convert.9
  1.6 0.7 convert.8
  2.3 0.9 fusion.9
  3.3 0.2 copy.30
  3.5 0.2 reshape.205
  3.7 0.1 copy.32
  3.7 0.0 copy-done
  3.7 0.9 fusion.8
  4.6 0.2 reshape.204
  4.9 0.3 copy.31
  5.2 0.5 broadcast.109
  5.7 1.0 %reduce.8 = bf16[128,2080]{0,1:T(8,128)(2,1)S(1)} reduce(bf16[128,1,2080]{0,2,1:T(8,128)(2,1)S(1)} %maximum_bitcast_fusion, bf16[]{:T(256)} %broadcast.109), dimensions={1}, to_apply=%copy.33.reduce_sub_computation | reduce | bytes 1064962 | tf_op jit(solution)/shard_map/all_to_all | solution.py:77
  6.7 0.3 copy.38
  7.0 1.4 %reshape.210 = bf16[128,2,1040]{2,1,0:T(2,128)(2,1)} reshape(bf16[128,2080]{1,0:T(8,128)(2,1)S(1)} %copy.38) | data formatting | bytes 1064960
  8.4 15.8 %all-to-all-start = ((bf16[128,2,1040]{2,1,0:T(2,128)(2,1)}), bf16[128,2,1040]{2,1,0:T(2,128)(2,1)S(1)}, u32[]{:S(2)}, u32[]{:S(2)}) async-start(bf16[128,2,1040]{2,1,0:T(2,128)(2,1)} %reshape.210), calls=%async_computation | async-start | bytes 1179648 | tf_op jit(solution)/shard_map/all_to_all | solution.py:77
  24.2 19.2 %all-to-all-done = bf16[128,2,1040]{2,1,0:T(2,128)(2,1)S(1)} async-done(((bf16[128,2,1040]{2,1,0:T(2,128)(2,1)}), bf16[128,2,1040]{2,1,0:T(2,128)(2,1)S(1)}, u32[]{:S(2)}, u32[]{:S(2)}) %all-to-all-start) | async-done | bytes 532512 | tf_op jit(solution)/shard_map/all_to_all | solution.py:77
  43.4 0.6 reshape.211
  44.1 1.5 %copy.34 = bf16[128,1,2080]{0,2,1:T(8,128)(2,1)S(1)} copy(bf16[128,1,2080]{2,1,0:T(2,128)(2,1)S(1)} %reshape.211) | data formatting | bytes 1064960 | tf_op jit(solution)/shard_map/all_to_all | solution.py:77
  45.6 0.0 copy-start.1
  45.6 0.1 copy.35
  45.7 0.2 reshape.209
  45.9 0.2 copy.37
  46.1 0.2 copy.36
  46.3 0.2 reshape.206
  46.6 0.0 copy-done.1
  46.6 6.9 %while.18 = (s32[]{:T(128)}, f32[1600,256]{1,0:T(8,128)}, s32[4,1024]{1,0:T(4,128)S(1)}, f32[8,16]{1,0:T(8,128)S(1)}, bf16[1024,256]{1,0:T(8,128)(2,1)S(1)}, /*i...) while((s32[]{:T(128)}, f32[1600,256]{1,0:T(8,128)}, ...), condition=%wide.region_3.4_spmd.clone, body=%wide.region_0.3_spmd.clone.sunk | while | flops 424460288 | bytes 7562477 | solution.py:50
  46.6 0.1 constant_dynamic-slice_fusion.2
  46.7 0.1 convolution_bitcast_fusion.4
  46.9 0.1 convolution_bitcast_fusion.5
  47.0 0.1 select_reduce_fusion.3
  47.1 0.4 multiply_convert_fusion.2
  47.6 1.8 %convolution_add_fusion.2 = f32[1600,256]{1,0:T(8,128)} fusion(bf16[1600,512]{1,0:T(8,128)(2,1)S(1)} %bitcast.46, f32[1600,256]{1,0:T(8,128)} %get-tuple-element.268, pred[]{:T(512)S(6)} %compare.25, bf16[1024,256]{1,0:T(8,128)(2,1)S(1)} %get-tuple-element.283, s32[]{:T(128)S(6)} %select_n.61), kind=kOutput, calls=%fused_computation.1.clone.1 | convolution fusion | flops 420249600 | bytes 5177349 | tf_op jit(solution)/shard_map/while/body/eval_jaxpr/dot_general | solution.py:37
  49.3 0.1 constant_dynamic-slice_fusion.2
  49.4 0.1 convolution_bitcast_fusion.4
  49.6 0.1 convolution_bitcast_fusion.5
  49.7 0.1 select_reduce_fusion.3
  49.9 0.4 multiply_convert_fusion.2
  50.3 3.2 %convolution_add_fusion.2 = f32[1600,256]{1,0:T(8,128)} fusion(bf16[1600,512]{1,0:T(8,128)(2,1)S(1)} %bitcast.46, f32[1600,256]{1,0:T(8,128)} %get-tuple-element.268, pred[]{:T(512)S(6)} %compare.25, bf16[1024,256]{1,0:T(8,128)(2,1)S(1)} %get-tuple-element.283, s32[]{:T(128)S(6)} %select_n.61), kind=kOutput, calls=%fused_computation.1.clone.1 | convolution fusion | flops 420249600 | bytes 5177349 | tf_op jit(solution)/shard_map/while/body/eval_jaxpr/dot_general | solution.py:37
  53.5 1.1 %fusion.19 = (f32[160,256]{1,0:T(8,128)S(1)}, f32[160,256]{1,0:T(8,128)S(1)}, f32[160,256]{1,0:T(8,128)S(1)}) fusion(f32[1600,256]{1,0:T(8,128)} %get-tuple-element.147), kind=kLoop, calls=%fused_computation.39 | loop fusion | bytes 983040 | tf_op jit(solution)/shard_map/slice | solution.py:96
  54.6 5.6 %collective-permute-start = (f32[4,40,256]{2,1,0:T(8,128)S(1)}, f32[4,40,256]{2,1,0:T(8,128)S(1)}, u32[]{:S(2)}, u32[]{:S(2)}) collective-permute-start(f32[4,40,256]{2,1,0:T(8,128)S(1)} %bitcast.58), channel_id=1, source_target_pairs={{8,0},{9,1},{10,2},{11,3},{12,4},{13,5},{14,6},{15,7},{16,8},{17,9... | collective-permute-start | bytes 491528 | tf_op jit(solution)/shard_map/ppermute | solution.py:14
  60.2 4.2 %collective-permute-start.1 = (f32[4,40,256]{2,1,0:T(8,128)S(1)}, f32[4,40,256]{2,1,0:T(8,128)S(1)}, u32[]{:S(2)}, u32[]{:S(2)}) collective-permute-start(f32[4,40,256]{2,1,0:T(8,128)S(1)} %bitcast.57), channel_id=1, source_target_pairs={{0,8},{1,9},{2,10},{3,11},{4,12},{5,13},{6,14},{7,15},{8,16},{9,17... | collective-permute-start | bytes 491528 | tf_op jit(solution)/shard_map/ppermute | solution.py:14
  64.3 8.3 %collective-permute-done = f32[4,40,256]{2,1,0:T(8,128)S(1)} collective-permute-done((f32[4,40,256]{2,1,0:T(8,128)S(1)}, f32[4,40,256]{2,1,0:T(8,128)S(1)}, u32[]{:S(2)}, u32[]{:S(2)}) %collective-permute-start) | collective-permute-done | bytes 163872 | tf_op jit(solution)/shard_map/ppermute | solution.py:14
  72.7 0.7 add_dynamic-update-slice_fusion
  73.4 5.4 %collective-permute-done.1 = f32[4,40,256]{2,1,0:T(8,128)S(1)} collective-permute-done((f32[4,40,256]{2,1,0:T(8,128)S(1)}, f32[4,40,256]{2,1,0:T(8,128)S(1)}, u32[]{:S(2)}, u32[]{:S(2)}) %collective-permute-start.1) | collective-permute-done | bytes 163872 | tf_op jit(solution)/shard_map/ppermute | solution.py:14
  78.8 1.6 %fusion.10 = f32[40,40,256]{2,1,0:T(8,128)} fusion(f32[40,40,256]{2,1,0:T(8,128)} %add_dynamic-update-slice_fusion, f32[4,40,256]{2,1,0:T(8,128)S(1)} %collective-permute-done.1), kind=kLoop, calls=%fused_computation.26 | loop fusion | flops 40960 | bytes 491520 | tf_op jit(solution)/shard_map/scatter-add | solution.py:98
  80.4 1.1 %fusion.18 = (f32[32,4,256]{2,1,0:T(4,128)S(1)}, f32[32,4,256]{2,1,0:T(4,128)S(1)}) fusion(f32[40,40,256]{2,1,0:T(8,128)} %fusion.10), kind=kLoop, calls=%fused_computation.38 | loop fusion | bytes 524288 | tf_op jit(solution)/shard_map/slice | solution.py:102
  81.5 1.9 %collective-permute-start.2 = (f32[32,4,256]{2,1,0:T(4,128)S(1)}, f32[32,4,256]{2,1,0:T(4,128)S(1)}, u32[]{:S(2)}, u32[]{:S(2)}) collective-permute-start(f32[32,4,256]{2,1,0:T(4,128)S(1)} %get-tuple-element.208), channel_id=1, source_target_pairs={{1,0},{2,1},{3,2},{4,3},{5,4},{6,5},{7,6},{8,7},{9,8},{10,9},{11,1... | collective-permute-start | bytes 393224 | tf_op jit(solution)/shard_map/ppermute | solution.py:14
  83.4 1.5 %slice.183 = f32[32,32,256]{2,1,0:T(8,128)S(1)} slice(f32[40,40,256]{2,1,0:T(8,128)} %fusion.10), slice={[4:36], [4:36], [0:256]} | slice | bytes 2097152 | tf_op jit(solution)/shard_map/slice | solution.py:105
  84.9 2.4 %collective-permute-start.3 = (f32[32,4,256]{2,1,0:T(4,128)S(1)}, f32[32,4,256]{2,1,0:T(4,128)S(1)}, u32[]{:S(2)}, u32[]{:S(2)}) collective-permute-start(f32[32,4,256]{2,1,0:T(4,128)S(1)} %get-tuple-element.207), channel_id=1, source_target_pairs={{0,1},{1,2},{2,3},{3,4},{4,5},{5,6},{6,7},{7,8},{8,9},{9,10},{10,1... | collective-permute-start | bytes 393224 | tf_op jit(solution)/shard_map/ppermute | solution.py:14
  87.3 0.0 collective-permute-done.2
  87.3 1.0 %fusion.13 = f32[32,32,256]{2,1,0:T(8,128)S(1)} fusion(f32[32,32,256]{2,1,0:T(8,128)S(1)} %slice.183, f32[40,40,256]{2,1,0:T(8,128)} %fusion.10, f32[32,4,256]{2,1,0:T(4,128)S(1)} %collective-permute-done.2, pred[]{:T(512)S(6)} %lt.23), kind=kLoop, calls=%fused_computation.32 | loop fusion | flops 65536 | bytes 393217 | tf_op jit(solution)/shard_map/scatter-add | solution.py:106
  88.3 1.0 %copy.48 = f32[1,32,32,256]{3,2,1,0:T(8,128)} copy(f32[1,32,32,256]{3,2,1,0:T(8,128)S(1)} %bitcast.48) | data formatting | bytes 2097152
  89.3 4.0 %collective-permute-done.3 = f32[32,4,256]{2,1,0:T(4,128)S(1)} collective-permute-done((f32[32,4,256]{2,1,0:T(4,128)S(1)}, f32[32,4,256]{2,1,0:T(4,128)S(1)}, u32[]{:S(2)}, u32[]{:S(2)}) %collective-permute-start.3) | collective-permute-done | bytes 131104 | tf_op jit(solution)/shard_map/ppermute | solution.py:14
  93.3 0.7 fusion.12
  (8 shorter events, 0.1 us)
Async XLA Ops:
  0.0 3.7 %copy-start = (bf16[1024,256]{1,0:T(8,128)(2,1)S(1)}, bf16[1024,256]{1,0:T(8,128)(2,1)}, u32[]{:S(2)}) copy-start(bf16[1024,256]{1,0:T(8,128)(2,1)} %param.15) | copy-start | bytes 1572868
  8.4 35.0 %all-to-all-start = ((bf16[128,2,1040]{2,1,0:T(2,128)(2,1)}), bf16[128,2,1040]{2,1,0:T(2,128)(2,1)S(1)}, u32[]{:S(2)}, u32[]{:S(2)}) async-start(bf16[128,2,1040]{2,1,0:T(2,128)(2,1)} %reshape.210), calls=%async_computation | async-start | bytes 1179648 | tf_op jit(solution)/shard_map/all_to_all | solution.py:77
  45.6 1.0 %copy-start.1 = (f32[8,16]{1,0:T(8,128)S(1)}, f32[8,16]{1,0:T(8,128)}, u32[]{:S(2)}) copy-start(f32[8,16]{1,0:T(8,128)} %param.19) | copy-start | bytes 1540
  54.6 18.1 %collective-permute-start = (f32[4,40,256]{2,1,0:T(8,128)S(1)}, f32[4,40,256]{2,1,0:T(8,128)S(1)}, u32[]{:S(2)}, u32[]{:S(2)}) collective-permute-start(f32[4,40,256]{2,1,0:T(8,128)S(1)} %bitcast.58), channel_id=1, source_target_pairs={{8,0},{9,1},{10,2},{11,3},{12,4},{13,5},{14,6},{15,7},{16,8},{17,9... | collective-permute-start | bytes 491528 | tf_op jit(solution)/shard_map/ppermute | solution.py:14
  60.2 18.6 %collective-permute-start.1 = (f32[4,40,256]{2,1,0:T(8,128)S(1)}, f32[4,40,256]{2,1,0:T(8,128)S(1)}, u32[]{:S(2)}, u32[]{:S(2)}) collective-permute-start(f32[4,40,256]{2,1,0:T(8,128)S(1)} %bitcast.57), channel_id=1, source_target_pairs={{0,8},{1,9},{2,10},{3,11},{4,12},{5,13},{6,14},{7,15},{8,16},{9,17... | collective-permute-start | bytes 491528 | tf_op jit(solution)/shard_map/ppermute | solution.py:14
  81.5 5.8 %collective-permute-start.2 = (f32[32,4,256]{2,1,0:T(4,128)S(1)}, f32[32,4,256]{2,1,0:T(4,128)S(1)}, u32[]{:S(2)}, u32[]{:S(2)}) collective-permute-start(f32[32,4,256]{2,1,0:T(4,128)S(1)} %get-tuple-element.208), channel_id=1, source_target_pairs={{1,0},{2,1},{3,2},{4,3},{5,4},{6,5},{7,6},{8,7},{9,8},{10,9},{11,1... | collective-permute-start | bytes 393224 | tf_op jit(solution)/shard_map/ppermute | solution.py:14
  84.9 8.4 %collective-permute-start.3 = (f32[32,4,256]{2,1,0:T(4,128)S(1)}, f32[32,4,256]{2,1,0:T(4,128)S(1)}, u32[]{:S(2)}, u32[]{:S(2)}) collective-permute-start(f32[32,4,256]{2,1,0:T(4,128)S(1)} %get-tuple-element.207), channel_id=1, source_target_pairs={{0,1},{1,2},{2,3},{3,4},{4,5},{5,6},{6,7},{7,8},{8,9},{9,10},{10,1... | collective-permute-start | bytes 393224 | tf_op jit(solution)/shard_map/ppermute | solution.py:14

commit v2 on v1

--- a/solution.py
+++ b/solution.py
@@ -57,31 +57,31 @@
     padded_side = TS + 8
     slot_total = tile_count * slot_cap
     block_size = min(512, slot_total)
+    meta_lanes = 128
 
-    listed = send_list.reshape(-1)
+    listed = send_list.transpose(1, 0).reshape(-1)
     row_ids = jnp.arange(rows_dev, dtype=jnp.int32)
     chosen = (listed[:, None] == row_ids[None, :]).astype(jnp.bfloat16)
     outgoing = jnp.dot(chosen, visibilities, preferred_element_type=jnp.float32)
     outgoing = outgoing.astype(jnp.bfloat16)
     meta_src = jnp.concatenate([pixels, offsets], 0).astype(jnp.bfloat16)
     slot_meta = lax.dot_general(
-        chosen, meta_src, (((1,), (1,)), ((), ())), preferred_element_type=jnp.float32
-    ).astype(jnp.bfloat16)
+        meta_src, chosen, (((1,), (1,)), ((), ())), preferred_element_type=jnp.float32
+    )
+    slot_meta = slot_meta.reshape(META, slot_cap, tile_count).transpose(2, 1, 0)
+    slot_meta = slot_meta.reshape(tile_count, slot_cap * META).astype(jnp.bfloat16)
+    slot_meta = jnp.pad(slot_meta, ((0, 0), (0, meta_lanes - slot_cap * META)))
     packed = jnp.concatenate(
-        [
-            outgoing.reshape(tile_count, slot_cap * components),
-            slot_meta.reshape(tile_count, slot_cap * META),
-        ],
+        [outgoing[k * tile_count : (k + 1) * tile_count] for k in range(slot_cap)] + [slot_meta],
         1,
     )
     arrived = lax.all_to_all(packed, "tile", split_axis=0, concat_axis=0, tiled=True)
-    arrived_rows = arrived[:, : slot_cap * components].reshape(slot_total, components)
-    meta_rows = (
-        arrived[:, slot_cap * components :]
-        .reshape(slot_total, META)
-        .astype(jnp.int32)
-        .transpose(1, 0)
+    arrived_rows = jnp.concatenate(
+        [arrived[:, k * components : (k + 1) * components] for k in range(slot_cap)], 0
     )
+    meta_rows = arrived[:, slot_cap * components : slot_cap * components + slot_cap * META]
+    meta_rows = meta_rows.astype(jnp.int32).reshape(tile_count, slot_cap, META)
+    meta_rows = meta_rows.transpose(2, 1, 0).reshape(META, slot_total)
     padded_grid = grid_blocks(
         arrived_rows,
         meta_rows,
@@ -92,19 +92,19 @@
     )
     grid = padded_grid.reshape(padded_side, padded_side, components)
 
-    from_below = passed_along(grid[0:4], "tile", -TILES_Y)
-    from_above = passed_along(grid[TS + 4 : TS + 8], "tile", TILES_Y)
-    grid = grid.at[TS : TS + 4].add(from_below)
-    grid = grid.at[4:8].add(from_above)
+    from_below = passed_along(grid[0:4].astype(jnp.bfloat16), "tile", -TILES_Y)
+    from_above = passed_along(grid[TS + 4 : TS + 7].astype(jnp.bfloat16), "tile", TILES_Y)
+    grid = grid.at[TS : TS + 4].add(from_below.astype(jnp.float32))
+    grid = grid.at[4:7].add(from_above.astype(jnp.float32))
     tile_row = lax.axis_index("tile") % TILES_Y
     inner = grid[4 : TS + 4]
     from_next = passed_along(inner[:, 0:4], "tile", -1)
-    from_prev = passed_along(inner[:, TS + 4 : TS + 8], "tile", 1)
+    from_prev = passed_along(inner[:, TS + 4 : TS + 7], "tile", 1)
     from_next = jnp.where(tile_row + 1 < TILES_Y, from_next, 0.0)
     from_prev = jnp.where(tile_row >= 1, from_prev, 0.0)
     result = inner[:, 4 : TS + 4]
     result = result.at[:, TS - 4 : TS].add(from_next)
-    result = result.at[:, 0:4].add(from_prev)
+    result = result.at[:, 0:3].add(from_prev)
     return result[None]
 
 

time: 94.5 us -> 83.7 us (0.89)
  the two profiles are of different devices: /device:TPU:132 before, /device:TPU:66 now
where the time goes in v2:
time: 83.7 us; the launch traced here: 83.3 us
  waiting for transfers between devices  33 us (39%)
  starting transfers between devices  30.7 us (37%)
  matrix products  8.31 us (10%)
  local copies, waits for them, and re-layouts  6.98 us (8%)
  other arithmetic  3.96 us (5%)
    all_to_all x1, waiting for transfers between devices, body(): lax.all_to_all(packed, 'tile', split_axis=0, concat_axis=0, tiled=True)  20.1 us
    all_to_all x1, starting transfers between devices, body(): lax.all_to_all(packed, 'tile', split_axis=0, concat_axis=0, tiled=True)  16.6 us
    ppermute x4, starting transfers between devices, passed_along(): return lax.ppermute(value, axis, pairs)  14.1 us
    ppermute x4, waiting for transfers between devices, passed_along(): return lax.ppermute(value, axis, pairs)  12.9 us
    dot_general x2, matrix products, place_block(): return jnp.dot(weights, block_rows, preferred_element_type=jnp.float32)  4.98 us
    unnamed x34, local copies, waits for them, and re-layouts  4.2 us
    dot_general x1, matrix products, body(): outgoing = jnp.dot(chosen, visibilities, preferred_element_type=jnp.float32)  1.88 us
    scatter-add x1, local copies, waits for them, and re-layouts, body(): result = result.at[:, 0:3].add(from_prev)  1.87 us
  transfers between devices with their start and end apart: 5, of which 4 were waited for; matrix products, arithmetic and copies ran while one was open for 0% of the time, Pallas kernels for 0%

profile of v2, /device:TPU:66, one launch (start us, length us, event | category | flops | bytes accessed | tf_op | source)
XLA Modules:
  0.0 83.3 jit_solution(6646327965783123184)
XLA Ops:
  0.0 0.0 copy-start
  0.0 1.0 %copy-done = bf16[1024,256]{1,0:T(8,128)(2,1)S(1)} copy-done((bf16[1024,256]{1,0:T(8,128)(2,1)S(1)}, bf16[1024,256]{1,0:T(8,128)(2,1)}, u32[]{:S(2)}) %copy-start) | copy-done | bytes 524312
  1.0 0.0 copy-start.4
  1.0 0.0 copy-start.5
  1.0 0.0 copy-start.6
  1.0 1.9 %fusion.8 = bf16[1024,256]{0,1:T(8,128)(2,1)S(1)} fusion(bf16[1024,256]{1,0:T(8,128)(2,1)S(1)} %copy-done, s32[1024]{0:T(1024)} %bitcast.82), kind=kOutput, calls=%fused_computation.22 | convolution fusion | flops 538181632 | bytes 1052672 | tf_op jit(solution)/shard_map/dot_general | solution.py:65
  3.2 0.0 copy-done.4
  3.2 0.0 copy-done.5
  3.2 0.0 copy-done.6
  3.3 0.9 %fusion.9 = bf16[4,1024]{1,0:T(4,128)(2,1)S(1)} fusion(s32[1024]{0:T(1024)S(1)} %bitcast.83, bf16[2,1024]{1,0:T(2,128)(2,1)S(1)} %convert.14, bf16[2,1024]{1,0:T(2,128)(2,1)S(1)} %convert.13), kind=kOutput, calls=%fused_computation.23 | convolution fusion | flops 9457664 | bytes 20480 | tf_op jit(solution)/shard_map/dot_general | solution.py:68
  4.2 0.5 broadcast.111
  4.7 1.0 %reduce.8 = bf16[128,2176]{0,1:T(8,128)(2,1)S(1)} reduce(bf16[128,1,2176]{0,2,1:T(8,128)(2,1)S(1)} %bitcast.72, bf16[]{:T(256)} %broadcast.111), dimensions={1}, to_apply=%copy.18.reduce_sub_computation | reduce | bytes 1114114 | tf_op jit(solution)/shard_map/all_to_all | solution.py:78
  5.8 0.3 copy.26
  6.1 1.4 %reshape.218 = bf16[128,2,1088]{2,1,0:T(2,128)(2,1)} reshape(bf16[128,2176]{1,0:T(8,128)(2,1)S(1)} %copy.26) | data formatting | bytes 1114112
  7.4 16.6 %all-to-all-start = ((bf16[128,2,1088]{2,1,0:T(2,128)(2,1)}), bf16[128,2,1088]{2,1,0:T(2,128)(2,1)S(1)}, u32[]{:S(2)}, u32[]{:S(2)}) async-start(bf16[128,2,1088]{2,1,0:T(2,128)(2,1)} %reshape.218), calls=%async_computation | async-start | bytes 1179648 | tf_op jit(solution)/shard_map/all_to_all | solution.py:78
  24.0 20.1 %all-to-all-done = bf16[128,2,1088]{2,1,0:T(2,128)(2,1)S(1)} async-done(((bf16[128,2,1088]{2,1,0:T(2,128)(2,1)}), bf16[128,2,1088]{2,1,0:T(2,128)(2,1)S(1)}, u32[]{:S(2)}, u32[]{:S(2)}) %all-to-all-start) | async-done | bytes 557088 | tf_op jit(solution)/shard_map/all_to_all | solution.py:78
  44.1 0.6 reshape.219
  44.8 0.0 copy-start.3
  44.8 0.1 copy.25
  45.0 0.1 copy.23
  45.1 0.4 copy-done.3
  45.5 6.8 %while.18 = (s32[]{:T(128)}, f32[1600,256]{1,0:T(8,128)}, s32[4,1024]{1,0:T(4,128)S(1)}, f32[8,16]{1,0:T(8,128)S(1)}, bf16[1024,256]{1,0:T(8,128)(2,1)S(1)}, /*i...) while((s32[]{:T(128)}, f32[1600,256]{1,0:T(8,128)}, ...), condition=%wide.region_3.4_spmd.clone, body=%wide.region_0.3_spmd.clone.sunk | while | flops 424460288 | bytes 7562469 | solution.py:50
  45.5 0.1 constant_dynamic-slice_fusion.2
  45.5 0.1 convolution_bitcast_fusion.4
  45.7 0.1 convolution_bitcast_fusion.5
  45.9 0.1 select_reduce_fusion.3
  46.0 0.4 multiply_convert_fusion.2
  46.4 1.8 %convolution_add_fusion.2 = f32[1600,256]{1,0:T(8,128)} fusion(bf16[1600,512]{1,0:T(8,128)(2,1)S(1)} %bitcast.60, f32[1600,256]{1,0:T(8,128)} %get-tuple-element.243, pred[]{:T(512)S(6)} %compare.26, bf16[1024,256]{1,0:T(8,128)(2,1)S(1)} %get-tuple-element.258, s32[]{:T(128)S(6)} %select_n.63), kind=kOutput, calls=%fused_computation.1.clone.1 | convolution fusion | flops 420249600 | bytes 5177349 | tf_op jit(solution)/shard_map/while/body/eval_jaxpr/dot_general | solution.py:37
  48.2 0.1 constant_dynamic-slice_fusion.2
  48.3 0.1 convolution_bitcast_fusion.4
  48.4 0.1 convolution_bitcast_fusion.5
  48.6 0.1 select_reduce_fusion.3
  48.7 0.4 multiply_convert_fusion.2
  49.1 3.2 %convolution_add_fusion.2 = f32[1600,256]{1,0:T(8,128)} fusion(bf16[1600,512]{1,0:T(8,128)(2,1)S(1)} %bitcast.60, f32[1600,256]{1,0:T(8,128)} %get-tuple-element.243, pred[]{:T(512)S(6)} %compare.26, bf16[1024,256]{1,0:T(8,128)(2,1)S(1)} %get-tuple-element.258, s32[]{:T(128)S(6)} %select_n.63), kind=kOutput, calls=%fused_computation.1.clone.1 | convolution fusion | flops 420249600 | bytes 5177349 | tf_op jit(solution)/shard_map/while/body/eval_jaxpr/dot_general | solution.py:37
  52.3 0.0 copy-start.1
  52.3 1.6 %convert.15 = bf16[1600,256]{1,0:T(8,128)(2,1)S(1)} convert(f32[1600,256]{1,0:T(8,128)} %get-tuple-element.147) | non-fusion elementwise | flops 409600 | bytes 2457600 | tf_op jit(solution)/shard_map/convert.4
  54.0 5.7 %collective-permute-start = (bf16[4,40,256]{2,1,0:T(8,128)(2,1)S(1)}, bf16[4,40,256]{2,1,0:T(8,128)(2,1)S(1)}, u32[]{:S(2)}, u32[]{:S(2)}) collective-permute-start(bf16[4,40,256]{2,1,0:T(8,128)(2,1)S(1)} %bitcast.79), channel_id=1, source_target_pairs={{8,0},{9,1},{10,2},{11,3},{12,4},{13,5},{14,6},{15,7},{16,8},{17,9... | collective-permute-start | bytes 245768 | tf_op jit(solution)/shard_map/ppermute | solution.py:14
  59.7 0.0 copy-done.1
  59.7 4.0 %collective-permute-start.1 = (bf16[3,40,256]{2,1,0:T(8,128)(2,1)S(1)}, bf16[3,40,256]{2,1,0:T(8,128)(2,1)S(1)}, u32[]{:S(2)}, u32[]{:S(2)}) collective-permute-start(bf16[3,40,256]{2,1,0:T(8,128)(2,1)S(1)} %bitcast.80), channel_id=1, source_target_pairs={{0,8},{1,9},{2,10},{3,11},{4,12},{5,13},{6,14},{7,15},{8,16},{9,17... | collective-permute-start | bytes 184328 | tf_op jit(solution)/shard_map/ppermute | solution.py:14
  63.8 2.2 %collective-permute-done = bf16[4,40,256]{2,1,0:T(8,128)(2,1)S(1)} collective-permute-done((bf16[4,40,256]{2,1,0:T(8,128)(2,1)S(1)}, bf16[4,40,256]{2,1,0:T(8,128)(2,1)S(1)}, u32[]{:S(2)}, u32[]{:S(2)}) %collective-permute-start) | collective-permute-done | bytes 81952 | tf_op jit(solution)/shard_map/ppermute | solution.py:14
  66.0 4.8 %collective-permute-done.1 = bf16[3,40,256]{2,1,0:T(8,128)(2,1)S(1)} collective-permute-done((bf16[3,40,256]{2,1,0:T(8,128)(2,1)S(1)}, bf16[3,40,256]{2,1,0:T(8,128)(2,1)S(1)}, u32[]{:S(2)}, u32[]{:S(2)}) %collective-permute-start.1) | collective-permute-done | bytes 61472 | tf_op jit(solution)/shard_map/ppermute | solution.py:14
  70.8 1.9 %collective-permute-start.2 = (f32[32,4,256]{2,1,0:T(4,128)S(1)}, f32[32,4,256]{2,1,0:T(4,128)S(1)}, u32[]{:S(2)}, u32[]{:S(2)}) collective-permute-start(f32[32,4,256]{2,1,0:T(4,128)S(1)} %slice.258), channel_id=1, source_target_pairs={{1,0},{2,1},{3,2},{4,3},{5,4},{6,5},{7,6},{8,7},{9,8},{10,9},{11,1... | collective-permute-start | bytes 393224 | tf_op jit(solution)/shard_map/ppermute | solution.py:14
  72.8 0.1 slice.256
  73.0 2.4 %collective-permute-start.3 = (f32[32,3,256]{2,1,0:T(4,128)S(1)}, f32[32,3,256]{2,1,0:T(4,128)S(1)}, u32[]{:S(2)}, u32[]{:S(2)}) collective-permute-start(f32[32,3,256]{2,1,0:T(4,128)S(1)} %slice.260), channel_id=1, source_target_pairs={{0,1},{1,2},{2,3},{3,4},{4,5},{5,6},{6,7},{7,8},{8,9},{9,10},{10,1... | collective-permute-start | bytes 294920 | tf_op jit(solution)/shard_map/ppermute | solution.py:14
  75.4 0.0 collective-permute-done.2
  75.4 0.1 fusion.11
  75.5 0.0 copy-start.2
  75.5 5.9 %collective-permute-done.3 = f32[32,3,256]{2,1,0:T(4,128)S(1)} collective-permute-done((f32[32,3,256]{2,1,0:T(4,128)S(1)}, f32[32,3,256]{2,1,0:T(4,128)S(1)}, u32[]{:S(2)}, u32[]{:S(2)}) %collective-permute-start.3) | collective-permute-done | bytes 98336 | tf_op jit(solution)/shard_map/ppermute | solution.py:14
  81.4 0.0 copy-done.2
  81.4 1.9 %scatter-add.19 = f32[1,32,32,256]{3,2,1,0:T(8,128)} dynamic-update-slice(f32[1,32,32,256]{3,2,1,0:T(8,128)} %bitcast.71, f32[1,32,3,256]{3,2,1,0:T(4,128)S(1)} %fusion.10, s32[]{:T(128)} %constant.160.clone.1, s32[]{:T(128)} %constant.160.clone.1, s32[]{:T(128)} %constant.160.clone.1, s32[]{:T(128)} %constant.160.clone.1) | dynamic-update-slice | bytes 196612 | tf_op jit(solution)/shard_map/scatter-add | solution.py:107
  (33 shorter events, 0.5 us)
Async XLA Ops:
  0.0 1.0 %copy-start = (bf16[1024,256]{1,0:T(8,128)(2,1)S(1)}, bf16[1024,256]{1,0:T(8,128)(2,1)}, u32[]{:S(2)}) copy-start(bf16[1024,256]{1,0:T(8,128)(2,1)} %param.15) | copy-start | bytes 1572868
  1.0 2.2 %copy-start.4 = (s32[2,1024]{1,0:T(2,128)S(1)}, s32[2,1024]{1,0:T(2,128)}, u32[]{:S(2)}) copy-start(s32[2,1024]{1,0:T(2,128)} %param.17) | copy-start | bytes 24580
  1.0 2.2 %copy-start.5 = (s32[2,1024]{1,0:T(2,128)S(1)}, s32[2,1024]{1,0:T(2,128)}, u32[]{:S(2)}) copy-start(s32[2,1024]{1,0:T(2,128)} %param.18) | copy-start | bytes 24580
  1.0 2.2 %copy-start.6 = (s32[128,8]{0,1:T(8,128)S(1)}, s32[128,8]{0,1:T(8,128)}, u32[]{:S(2)}) copy-start(s32[128,8]{0,1:T(8,128)} %param.16) | copy-start | bytes 12292
  7.4 36.7 %all-to-all-start = ((bf16[128,2,1088]{2,1,0:T(2,128)(2,1)}), bf16[128,2,1088]{2,1,0:T(2,128)(2,1)S(1)}, u32[]{:S(2)}, u32[]{:S(2)}) async-start(bf16[128,2,1088]{2,1,0:T(2,128)(2,1)} %reshape.218), calls=%async_computation | async-start | bytes 1179648 | tf_op jit(solution)/shard_map/all_to_all | solution.py:78
  44.8 0.7 copy-start.3
  52.3 7.4 %copy-start.1 = (f32[1600,256]{1,0:T(8,128)S(1)}, f32[1600,256]{1,0:T(8,128)}, u32[]{:S(2)}) copy-start(f32[1600,256]{1,0:T(8,128)} %get-tuple-element.147) | copy-start | bytes 4915204
  54.0 12.0 %collective-permute-start = (bf16[4,40,256]{2,1,0:T(8,128)(2,1)S(1)}, bf16[4,40,256]{2,1,0:T(8,128)(2,1)S(1)}, u32[]{:S(2)}, u32[]{:S(2)}) collective-permute-start(bf16[4,40,256]{2,1,0:T(8,128)(2,1)S(1)} %bitcast.79), channel_id=1, source_target_pairs={{8,0},{9,1},{10,2},{11,3},{12,4},{13,5},{14,6},{15,7},{16,8},{17,9... | collective-permute-start | bytes 245768 | tf_op jit(solution)/shard_map/ppermute | solution.py:14
  59.7 11.0 %collective-permute-start.1 = (bf16[3,40,256]{2,1,0:T(8,128)(2,1)S(1)}, bf16[3,40,256]{2,1,0:T(8,128)(2,1)S(1)}, u32[]{:S(2)}, u32[]{:S(2)}) collective-permute-start(bf16[3,40,256]{2,1,0:T(8,128)(2,1)S(1)} %bitcast.80), channel_id=1, source_target_pairs={{0,8},{1,9},{2,10},{3,11},{4,12},{5,13},{6,14},{7,15},{8,16},{9,17... | collective-permute-start | bytes 184328 | tf_op jit(solution)/shard_map/ppermute | solution.py:14
  70.8 4.5 %collective-permute-start.2 = (f32[32,4,256]{2,1,0:T(4,128)S(1)}, f32[32,4,256]{2,1,0:T(4,128)S(1)}, u32[]{:S(2)}, u32[]{:S(2)}) collective-permute-start(f32[32,4,256]{2,1,0:T(4,128)S(1)} %slice.258), channel_id=1, source_target_pairs={{1,0},{2,1},{3,2},{4,3},{5,4},{6,5},{7,6},{8,7},{9,8},{10,9},{11,1... | collective-permute-start | bytes 393224 | tf_op jit(solution)/shard_map/ppermute | solution.py:14
  73.0 8.4 %collective-permute-start.3 = (f32[32,3,256]{2,1,0:T(4,128)S(1)}, f32[32,3,256]{2,1,0:T(4,128)S(1)}, u32[]{:S(2)}, u32[]{:S(2)}) collective-permute-start(f32[32,3,256]{2,1,0:T(4,128)S(1)} %slice.260), channel_id=1, source_target_pairs={{0,1},{1,2},{2,3},{3,4},{4,5},{5,6},{6,7},{7,8},{8,9},{9,10},{10,1... | collective-permute-start | bytes 294920 | tf_op jit(solution)/shard_map/ppermute | solution.py:14
  75.5 6.0 %copy-start.2 = (f32[32,32,256]{2,1,0:T(8,128)}, f32[32,32,256]{2,1,0:T(8,128)S(1)}, u32[]{:S(2)}) copy-start(f32[32,32,256]{2,1,0:T(8,128)S(1)} %fusion.11) | copy-start | bytes 3145732

commit v3 on v2

v3 whole, which is shorter than its diff:
```python
import jax
import jax.numpy as jnp
from jax import lax
from jax.sharding import PartitionSpec as P

TS = 32
TILES_Y = 8
META = 4


def passed_along(value, axis, by):
    count = lax.axis_size(axis)
    pairs = [(i, i + by) for i in range(count) if 0 <= i + by < count]
    return lax.ppermute(value, axis, pairs)


def spread(kernel, pixel, padded_side):
    cell_index = jnp.arange(padded_side, dtype=jnp.int32)[:, None] - pixel[None, :]
    tap_index = jnp.arange(kernel.shape[0], dtype=jnp.int32)[:, None, None]
    return jnp.sum(jnp.where(cell_index[None] == tap_index, kernel[:, None, :], 0.0), axis=0)


def kernel_of(taper, offset):
    levels = jnp.arange(taper.shape[1], dtype=jnp.int32)[:, None]
    select = (levels == offset[None, :]).astype(jnp.float32)
    return jnp.dot(taper, select, precision=lax.Precision.HIGHEST, preferred_element_type=jnp.float32)


def place_rows(spread_u, spread_v, slot_rows):
    weights = (spread_u[:, None, :] * spread_v[None, :, :]).astype(jnp.bfloat16)
    weights = weights.reshape(spread_u.shape[0] * spread_v.shape[0], -1)
    cells = jnp.dot(weights, slot_rows, preferred_element_type=jnp.float32)
    return cells.reshape(spread_u.shape[0], spread_v.shape[0], -1)


def body(visibilities, send_list, pixels, offsets, taper):
    tile_count = lax.axis_size("tile")
    slot_cap = send_list.shape[1]
    rows_dev, components = visibilities.shape
    padded_side = TS + 8
    slot_total = tile_count * slot_cap
    halves = 2
    per_half = slot_cap // halves
    half_lanes = per_half * components + 128

    listed = send_list.transpose(1, 0).reshape(-1)
    row_ids = jnp.arange(rows_dev, dtype=jnp.int32)
    chosen = (listed[:, None] == row_ids[None, :]).astype(jnp.bfloat16)
    outgoing = jnp.dot(chosen, visibilities, preferred_element_type=jnp.float32)
    outgoing = outgoing.astype(jnp.bfloat16)
    meta_src = jnp.concatenate([pixels, offsets], 0).astype(jnp.bfloat16)
    slot_meta = lax.dot_general(
        meta_src, chosen, (((1,), (1,)), ((), ())), preferred_element_type=jnp.float32
    )
    slot_meta = slot_meta.reshape(META, slot_cap, tile_count).transpose(2, 1, 0)
    slot_meta = slot_meta.reshape(tile_count, slot_cap * META).astype(jnp.bfloat16)
    pad = half_lanes - per_half * components
    tails = [
        jnp.pad(slot_meta, ((0, 0), (0, pad - slot_cap * META))),
        jnp.zeros((tile_count, pad), jnp.bfloat16),
    ]
    packed = jnp.stack(
        [
            jnp.concatenate(
                [
                    outgoing[(h * per_half + j) * tile_count : (h * per_half + j + 1) * tile_count]
                    for j in range(per_half)
                ]
                + [tails[h]],
                1,
            )
            for h in range(halves)
        ],
        1,
    )
    arrived = lax.all_to_all(packed, "tile", split_axis=0, concat_axis=0, tiled=True)
    arrived_rows = jnp.concatenate(
        [
            arrived[:, h, j * components : (j + 1) * components]
            for h in range(halves)
            for j in range(per_half)
        ],
        0,
    )
    meta_rows = arrived[:, 0, per_half * components : per_half * components + slot_cap * META]
    meta_rows = meta_rows.astype(jnp.int32).reshape(tile_count, slot_cap, META)
    meta_rows = meta_rows.transpose(2, 1, 0).reshape(META, slot_total)

    spread_u = spread(kernel_of(taper, meta_rows[2]), meta_rows[0], padded_side)
    spread_v = spread(kernel_of(taper, meta_rows[3]), meta_rows[1], padded_side)
    low = place_rows(spread_u[0:4], spread_v, arrived_rows)
    high = place_rows(spread_u[TS + 4 : TS + 7], spread_v, arrived_rows)

    from_below = passed_along(low.astype(jnp.bfloat16), "tile", -TILES_Y)
    from_above = passed_along(high.astype(jnp.bfloat16), "tile", TILES_Y)
    inner = place_rows(spread_u[4 : TS + 4], spread_v, arrived_rows)
    inner = inner.at[TS - 4 : TS].add(from_below.astype(jnp.float32))
    inner = inner.at[0:3].add(from_above.astype(jnp.float32))
    tile_row = lax.axis_index("tile") % TILES_Y
    from_next = passed_along(inner[:, 0:4], "tile", -1)
    from_prev = passed_along(inner[:, TS + 4 : TS + 7], "tile", 1)
    from_next = jnp.where(tile_row + 1 < TILES_Y, from_next, 0.0)
    from_prev = jnp.where(tile_row >= 1, from_prev, 0.0)
    result = inner[:, 4 : TS + 4]
    result = result.at[:, TS - 4 : TS].add(from_next)
    result = result.at[:, 0:3].add(from_prev)
    return result[None]


def solution(mesh):
    placed = (
        P("tile", "chan"),
        P(("chan", "tile"), None),
        P(None, ("chan", "tile")),
        P(None, ("chan", "tile")),
        P(),
    )
    return jax.shard_map(
        body, mesh=mesh, in_specs=placed, out_specs=P("tile", None, None, "chan"), check_vma=False
    )
```

time: 83.7 us -> 73.8 us (0.88)
  the two profiles are of different devices: /device:TPU:66 before, /device:TPU:68 now
where the time goes in v3:
time: 73.8 us; the launch traced here: 73.5 us
  blocking collectives  36.5 us (49%)
  starting transfers between devices  16.8 us (23%)
  waiting for transfers between devices  9.88 us (13%)
  local copies, waits for them, and re-layouts  4.95 us (7%)
  matrix products  4.48 us (6%)
    all_to_all x1, blocking collectives, body(): lax.all_to_all(packed, 'tile', split_axis=0, concat_axis=0, tiled=True)  36.5 us
    ppermute x4, starting transfers between devices, passed_along(): return lax.ppermute(value, axis, pairs)  16.8 us
    ppermute x4, waiting for transfers between devices, passed_along(): return lax.ppermute(value, axis, pairs)  9.88 us
    dot_general x1, matrix products, body(): outgoing = jnp.dot(chosen, visibilities, preferred_element_type=jnp.float32)  1.88 us
    scatter-add x1, local copies, waits for them, and re-layouts, body(): result = result.at[:, 0:3].add(from_prev)  1.87 us
  transfers between devices with their start and end apart: 4, of which 3 were waited for; matrix products, arithmetic and copies ran while one was open for 2% of the time, Pallas kernels for 0%

profile of v3, /device:TPU:68, one launch (start us, length us, event | category | flops | bytes accessed | tf_op | source)
XLA Modules:
  0.0 73.5 jit_solution(4780113452383217518)
XLA Ops:
  0.0 0.0 copy-start
  0.0 1.0 %copy-done = bf16[1024,256]{1,0:T(8,128)(2,1)S(1)} copy-done((bf16[1024,256]{1,0:T(8,128)(2,1)S(1)}, bf16[1024,256]{1,0:T(8,128)(2,1)}, u32[]{:S(2)}) %copy-start) | copy-done | bytes 524312
  1.0 0.0 copy-start.4
  1.0 0.0 copy-start.5
  1.0 0.0 copy-start.6
  1.0 1.9 %fusion.7 = bf16[1024,256]{0,1:T(8,128)(2,1)S(1)} fusion(bf16[1024,256]{1,0:T(8,128)(2,1)S(1)} %copy-done, s32[1024]{0:T(1024)} %bitcast.76), kind=kOutput, calls=%fused_computation.13 | convolution fusion | flops 538181632 | bytes 1052672 | tf_op jit(solution)/shard_map/dot_general | solution.py:49
  3.0 0.0 copy-done.4
  3.0 0.0 copy-done.5
  3.1 0.0 copy-done.6
  3.1 0.9 %fusion.8 = bf16[4,1024]{1,0:T(4,128)(2,1)S(1)} fusion(s32[1024]{0:T(1024)S(1)} %bitcast.77, bf16[2,1024]{1,0:T(2,128)(2,1)S(1)} %convert.9, bf16[2,1024]{1,0:T(2,128)(2,1)S(1)} %convert.8), kind=kOutput, calls=%fused_computation.18 | convolution fusion | flops 9457664 | bytes 20480 | tf_op jit(solution)/shard_map/dot_general | solution.py:52
  4.1 0.1 pad_maximum_fusion
  4.1 0.0 copy-start.3
  4.2 0.7 copy.32
  4.8 36.5 %all_to_all.5 = bf16[128,2,1152]{2,1,0:T(2,128)(2,1)S(1)} all-to-all(bf16[128,2,1152]{2,1,0:T(2,128)(2,1)S(1)} %copy.32), channel_id=1, replica_groups=mesh['chan'=4,'tile'=128] {'tile'}, dimensions={0} | all-to-all | bytes 1179648 | tf_op jit(solution)/shard_map/all_to_all | solution.py:76
  41.4 0.1 copy.42
  41.5 0.0 copy-done.3
  41.5 0.1 convolution_bitcast_fusion.1
  41.7 0.1 select_reduce_fusion.1
  41.8 0.0 copy-start.2
  41.9 0.8 %fusion.34 = (bf16[128,1,256]{2,1,0:T(2,128)(2,1)S(1)}, bf16[128,1,256]{2,1,0:T(2,128)(2,1)S(1)}, bf16[128,1,256]{2,1,0:T(2,128)(2,1)S(1)}, bf16[128,1,256]{2,1,...) fusion(bf16[128,2,1152]{2,1,0:T(2,128)(2,1)S(1)} %all_to_all.5), kind=kLoop, calls=%fused_computation.74 | loop fusion | bytes 1048576 | tf_op jit(solution)/shard_map/slice | solution.py:79
  42.6 0.0 copy-done.2
  42.7 0.0 slice-start
  42.7 0.1 convolution_bitcast_fusion
  43.0 0.1 select_reduce_fusion
  43.1 0.2 convolution_convert_fusion.1
  43.4 4.8 %collective-permute-start.1 = (bf16[3,40,256]{2,1,0:T(8,128)(2,1)S(1)}, bf16[3,40,256]{2,1,0:T(8,128)(2,1)S(1)}, u32[]{:S(2)}, u32[]{:S(2)}) collective-permute-start(bf16[3,40,256]{2,1,0:T(8,128)(2,1)S(1)} %convolution_convert_fusion.1), channel_id=1, source_target_pairs={{0,8},{1,9},{2,10},{3,11},{4,12},{5,13},{6,14},{7,15},{8,16},{9,17... | collective-permute-start | bytes 184328 | tf_op jit(solution)/shard_map/ppermute | solution.py:14
  48.2 0.0 slice-done
  48.2 0.3 convolution_convert_fusion
  48.4 5.8 %collective-permute-start = (bf16[4,40,256]{2,1,0:T(8,128)(2,1)S(1)}, bf16[4,40,256]{2,1,0:T(8,128)(2,1)S(1)}, u32[]{:S(2)}, u32[]{:S(2)}) collective-permute-start(bf16[4,40,256]{2,1,0:T(8,128)(2,1)S(1)} %convolution_convert_fusion), channel_id=1, source_target_pairs={{8,0},{9,1},{10,2},{11,3},{12,4},{13,5},{14,6},{15,7},{16,8},{17,9... | collective-permute-start | bytes 245768 | tf_op jit(solution)/shard_map/ppermute | solution.py:14
  54.3 0.9 %fusion.2 = f32[32,40,256]{2,1,0:T(8,128)S(1)} fusion(f32[40,1024]{1,0:T(8,128)S(1)} %select_reduce_fusion, f32[32,1024]{1,0:T(8,128)S(1)} %slice.224, bf16[1024,256]{1,0:T(8,128)(2,1)S(1)} %fusion.20), kind=kOutput, calls=%fused_computation.4 | convolution fusion | flops 673710080 | bytes 2129920 | tf_op jit(solution)/shard_map/dot_general | solution.py:32
  55.2 3.5 %collective-permute-done = bf16[4,40,256]{2,1,0:T(8,128)(2,1)S(1)} collective-permute-done((bf16[4,40,256]{2,1,0:T(8,128)(2,1)S(1)}, bf16[4,40,256]{2,1,0:T(8,128)(2,1)S(1)}, u32[]{:S(2)}, u32[]{:S(2)}) %collective-permute-start) | collective-permute-done | bytes 81952 | tf_op jit(solution)/shard_map/ppermute | solution.py:14
  58.7 0.0 collective-permute-done.1
  58.8 4.2 %collective-permute-start.2 = (f32[32,4,256]{2,1,0:T(4,128)S(1)}, f32[32,4,256]{2,1,0:T(4,128)S(1)}, u32[]{:S(2)}, u32[]{:S(2)}) collective-permute-start(f32[32,4,256]{2,1,0:T(4,128)S(1)} %slice.241), channel_id=1, source_target_pairs={{1,0},{2,1},{3,2},{4,3},{5,4},{6,5},{7,6},{8,7},{9,8},{10,9},{11,1... | collective-permute-start | bytes 393224 | tf_op jit(solution)/shard_map/ppermute | solution.py:14
  63.0 0.1 slice.239
  63.2 1.9 %collective-permute-start.3 = (f32[32,3,256]{2,1,0:T(4,128)S(1)}, f32[32,3,256]{2,1,0:T(4,128)S(1)}, u32[]{:S(2)}, u32[]{:S(2)}) collective-permute-start(f32[32,3,256]{2,1,0:T(4,128)S(1)} %slice.243), channel_id=1, source_target_pairs={{0,1},{1,2},{2,3},{3,4},{4,5},{5,6},{6,7},{7,8},{8,9},{9,10},{10,1... | collective-permute-start | bytes 294920 | tf_op jit(solution)/shard_map/ppermute | solution.py:14
  65.1 0.4 collective-permute-done.2
  65.5 0.1 fusion.18
  65.5 0.0 copy-start.1
  65.5 6.0 %collective-permute-done.3 = f32[32,3,256]{2,1,0:T(4,128)S(1)} collective-permute-done((f32[32,3,256]{2,1,0:T(4,128)S(1)}, f32[32,3,256]{2,1,0:T(4,128)S(1)}, u32[]{:S(2)}, u32[]{:S(2)}) %collective-permute-start.3) | collective-permute-done | bytes 98336 | tf_op jit(solution)/shard_map/ppermute | solution.py:14
  71.6 0.0 copy-done.1
  71.6 1.9 %scatter-add.19 = f32[1,32,32,256]{3,2,1,0:T(8,128)} dynamic-update-slice(f32[1,32,32,256]{3,2,1,0:T(8,128)} %bitcast.67, f32[1,32,3,256]{3,2,1,0:T(4,128)S(1)} %fusion.17, s32[]{:T(128)} %constant.126.clone.1, s32[]{:T(128)} %constant.126.clone.1, s32[]{:T(128)} %constant.126.clone.1, s32[]{:T(128)} %constant.126.clone.1) | dynamic-update-slice | bytes 196612 | tf_op jit(solution)/shard_map/scatter-add | solution.py:106
  (27 shorter events, 0.5 us)
Async XLA Ops:
  0.0 1.0 %copy-start = (bf16[1024,256]{1,0:T(8,128)(2,1)S(1)}, bf16[1024,256]{1,0:T(8,128)(2,1)}, u32[]{:S(2)}) copy-start(bf16[1024,256]{1,0:T(8,128)(2,1)} %param.13) | copy-start | bytes 1572868
  1.0 1.9 %copy-start.4 = (s32[2,1024]{1,0:T(2,128)S(1)}, s32[2,1024]{1,0:T(2,128)}, u32[]{:S(2)}) copy-start(s32[2,1024]{1,0:T(2,128)} %param.15) | copy-start | bytes 24580
  1.0 2.0 %copy-start.5 = (s32[2,1024]{1,0:T(2,128)S(1)}, s32[2,1024]{1,0:T(2,128)}, u32[]{:S(2)}) copy-start(s32[2,1024]{1,0:T(2,128)} %param.16) | copy-start | bytes 24580
  1.0 2.1 %copy-start.6 = (s32[128,8]{0,1:T(8,128)S(1)}, s32[128,8]{0,1:T(8,128)}, u32[]{:S(2)}) copy-start(s32[128,8]{0,1:T(8,128)} %param.14) | copy-start | bytes 12292
  4.1 37.4 %copy-start.3 = (f32[8,16]{1,0:T(8,128)S(1)}, f32[8,16]{1,0:T(8,128)}, u32[]{:S(2)}) copy-start(f32[8,16]{1,0:T(8,128)} %param.17) | copy-start | bytes 1540
  41.8 0.8 %copy-start.2 = (f32[40,1024]{1,0:T(8,128)}, f32[40,1024]{1,0:T(8,128)S(1)}, u32[]{:S(2)}) copy-start(f32[40,1024]{1,0:T(8,128)S(1)} %select_reduce_fusion.1) | copy-start | bytes 491524
  42.7 5.5 %slice-start = ((f32[40,1024]{1,0:T(8,128)}), f32[4,1024]{1,0:T(4,128)S(1)}, s32[]{:S(2)}) async-start(f32[40,1024]{1,0:T(8,128)} %copy-done.2), calls=%async_computation.1 | async-start | bytes 32768 | tf_op jit(solution)/shard_map/slice | solution.py:91
  43.4 15.4 %collective-permute-start.1 = (bf16[3,40,256]{2,1,0:T(8,128)(2,1)S(1)}, bf16[3,40,256]{2,1,0:T(8,128)(2,1)S(1)}, u32[]{:S(2)}, u32[]{:S(2)}) collective-permute-start(bf16[3,40,256]{2,1,0:T(8,128)(2,1)S(1)} %convolution_convert_fusion.1), channel_id=1, source_target_pairs={{0,8},{1,9},{2,10},{3,11},{4,12},{5,13},{6,14},{7,15},{8,16},{9,17... | collective-permute-start | bytes 184328 | tf_op jit(solution)/shard_map/ppermute | solution.py:14
  48.4 10.2 %collective-permute-start = (bf16[4,40,256]{2,1,0:T(8,128)(2,1)S(1)}, bf16[4,40,256]{2,1,0:T(8,128)(2,1)S(1)}, u32[]{:S(2)}, u32[]{:S(2)}) collective-permute-start(bf16[4,40,256]{2,1,0:T(8,128)(2,1)S(1)} %convolution_convert_fusion), channel_id=1, source_target_pairs={{8,0},{9,1},{10,2},{11,3},{12,4},{13,5},{14,6},{15,7},{16,8},{17,9... | collective-permute-start | bytes 245768 | tf_op jit(solution)/shard_map/ppermute | solution.py:14
  58.8 6.7 %collective-permute-start.2 = (f32[32,4,256]{2,1,0:T(4,128)S(1)}, f32[32,4,256]{2,1,0:T(4,128)S(1)}, u32[]{:S(2)}, u32[]{:S(2)}) collective-permute-start(f32[32,4,256]{2,1,0:T(4,128)S(1)} %slice.241), channel_id=1, source_target_pairs={{1,0},{2,1},{3,2},{4,3},{5,4},{6,5},{7,6},{8,7},{9,8},{10,9},{11,1... | collective-permute-start | bytes 393224 | tf_op jit(solution)/shard_map/ppermute | solution.py:14
  63.2 8.4 %collective-permute-start.3 = (f32[32,3,256]{2,1,0:T(4,128)S(1)}, f32[32,3,256]{2,1,0:T(4,128)S(1)}, u32[]{:S(2)}, u32[]{:S(2)}) collective-permute-start(f32[32,3,256]{2,1,0:T(4,128)S(1)} %slice.243), channel_id=1, source_target_pairs={{0,1},{1,2},{2,3},{3,4},{4,5},{5,6},{6,7},{7,8},{8,9},{9,10},{10,1... | collective-permute-start | bytes 294920 | tf_op jit(solution)/shard_map/ppermute | solution.py:14
  65.5 6.1 %copy-start.1 = (f32[32,32,256]{2,1,0:T(8,128)}, f32[32,32,256]{2,1,0:T(8,128)S(1)}, u32[]{:S(2)}) copy-start(f32[32,32,256]{2,1,0:T(8,128)S(1)} %fusion.18) | copy-start | bytes 3145732

commit v4 on v3

--- a/solution.py
+++ b/solution.py
@@ -88,22 +88,32 @@
 
     spread_u = spread(kernel_of(taper, meta_rows[2]), meta_rows[0], padded_side)
     spread_v = spread(kernel_of(taper, meta_rows[3]), meta_rows[1], padded_side)
-    low = place_rows(spread_u[0:4], spread_v, arrived_rows)
-    high = place_rows(spread_u[TS + 4 : TS + 7], spread_v, arrived_rows)
-
-    from_below = passed_along(low.astype(jnp.bfloat16), "tile", -TILES_Y)
-    from_above = passed_along(high.astype(jnp.bfloat16), "tile", TILES_Y)
-    inner = place_rows(spread_u[4 : TS + 4], spread_v, arrived_rows)
-    inner = inner.at[TS - 4 : TS].add(from_below.astype(jnp.float32))
-    inner = inner.at[0:3].add(from_above.astype(jnp.float32))
+    source = {-1: (TS + 4, 3), 0: (4, TS), 1: (0, 4)}
+    target = {-1: 0, 0: 0, 1: TS - 4}
     tile_row = lax.axis_index("tile") % TILES_Y
-    from_next = passed_along(inner[:, 0:4], "tile", -1)
-    from_prev = passed_along(inner[:, TS + 4 : TS + 7], "tile", 1)
-    from_next = jnp.where(tile_row + 1 < TILES_Y, from_next, 0.0)
-    from_prev = jnp.where(tile_row >= 1, from_prev, 0.0)
-    result = inner[:, 4 : TS + 4]
-    result = result.at[:, TS - 4 : TS].add(from_next)
-    result = result.at[:, 0:3].add(from_prev)
+    pieces = {}
+    for step_x in (-1, 0, 1):
+        for step_y in (-1, 0, 1):
+            if step_x == 0 and step_y == 0:
+                continue
+            rows_from, rows_span = source[step_x]
+            cols_from, cols_span = source[step_y]
+            piece = place_rows(
+                spread_u[rows_from : rows_from + rows_span],
+                spread_v[cols_from : cols_from + cols_span],
+                arrived_rows,
+            )
+            if step_x != 0:
+                piece = piece.astype(jnp.bfloat16)
+            pieces[step_x, step_y] = passed_along(piece, "tile", -(step_x * TILES_Y + step_y))
+    result = place_rows(spread_u[4 : TS + 4], spread_v[4 : TS + 4], arrived_rows)
+    for (step_x, step_y), incoming in pieces.items():
+        inside = (tile_row + step_y >= 0) & (tile_row + step_y < TILES_Y)
+        incoming = jnp.where(inside, incoming.astype(jnp.float32), 0.0)
+        rows_at, cols_at = target[step_x], target[step_y]
+        result = result.at[
+            rows_at : rows_at + incoming.shape[0], cols_at : cols_at + incoming.shape[1]
+        ].add(incoming)
     return result[None]
 
 

time: 73.8 us -> 103 us (1.40)
  the two profiles are of different devices: /device:TPU:68 before, /device:TPU:66 now
where the time goes in v4:
time: 103 us; the launch traced here: 102 us
  starting transfers between devices  48 us (47%)
  waiting for transfers between devices  35.5 us (34%)
  local copies, waits for them, and re-layouts  8.21 us (8%)
  matrix products  6.3 us (6%)
  other arithmetic  3.85 us (4%)
    ppermute x8, starting transfers between devices, passed_along(): return lax.ppermute(value, axis, pairs)  31.4 us
    all_to_all x1, waiting for transfers between devices, body(): lax.all_to_all(packed, 'tile', split_axis=0, concat_axis=0, tiled=True)  18.7 us
    ppermute x8, waiting for transfers between devices, passed_along(): return lax.ppermute(value, axis, pairs)  16.8 us
    all_to_all x1, starting transfers between devices, body(): lax.all_to_all(packed, 'tile', split_axis=0, concat_axis=0, tiled=True)  16.6 us
    scatter-add x4, local copies, waits for them, and re-layouts, body(): result = result.at[rows_at:rows_at + incoming.shape[0], cols_at:cols_at +...  3.47 us
    dot_general x9, matrix products, place_rows(): cells = jnp.dot(weights, slot_rows, preferred_element_type=jnp.float32)  3.22 us
    another operation x5, other arithmetic  2.68 us
  transfers between devices with their start and end apart: 9, of which 4 were waited for; matrix products, arithmetic and copies ran while one was open for 7% of the time, Pallas kernels for 0%

profile of v4, /device:TPU:66, one launch (start us, length us, event | category | flops | bytes accessed | tf_op | source)
XLA Modules:
  0.0 102.4 jit_solution(12335664980422614940)
XLA Ops:
  0.0 0.0 copy-start
  0.0 0.0 copy-start.2
  0.0 0.0 copy-start.3
  0.0 1.0 %copy-done = bf16[1024,256]{1,0:T(8,128)(2,1)S(1)} copy-done((bf16[1024,256]{1,0:T(8,128)(2,1)S(1)}, bf16[1024,256]{1,0:T(8,128)(2,1)}, u32[]{:S(2)}) %copy-start) | copy-done | bytes 524312
  1.0 0.0 copy-start.5
  1.0 1.9 %fusion.6 = bf16[1024,256]{0,1:T(8,128)(2,1)S(1)} fusion(bf16[1024,256]{1,0:T(8,128)(2,1)S(1)} %copy-done, s32[1024]{0:T(1024)} %bitcast.94), kind=kOutput, calls=%fused_computation.12 | convolution fusion | flops 538181632 | bytes 1052672 | tf_op jit(solution)/shard_map/dot_general | solution.py:49
  3.0 0.0 copy-done.2
  3.0 0.0 copy-done.3
  3.1 0.0 copy-done.5
  3.1 0.9 fusion.7
  4.0 0.0 copy-start.4
  4.1 0.0 copy-start.1
  4.1 0.1 pad_maximum_fusion
  4.1 1.7 %copy.61 = bf16[128,2,1152]{2,1,0:T(2,128)(2,1)} copy(bf16[128,2,1152]{0,2,1:T(8,128)(2,1)S(1)} %pad_maximum_fusion) | data formatting | bytes 1179648 | tf_op jit(solution)/shard_map/stack | solution.py:62
  5.9 16.6 %all-to-all-start = ((bf16[128,2,1152]{2,1,0:T(2,128)(2,1)}), bf16[128,2,1152]{2,1,0:T(2,128)(2,1)S(1)}, u32[]{:S(2)}, u32[]{:S(2)}) async-start(bf16[128,2,1152]{2,1,0:T(2,128)(2,1)} %copy.61), calls=%async_computation | async-start | bytes 1179648 | tf_op jit(solution)/shard_map/all_to_all | solution.py:76
  22.5 0.6 fusion.55
  23.1 0.0 copy-done.4
  23.1 0.8 and_reduce_fusion
  23.9 18.7 %all-to-all-done = bf16[128,2,1152]{2,1,0:T(2,128)(2,1)S(1)} async-done(((bf16[128,2,1152]{2,1,0:T(2,128)(2,1)}), bf16[128,2,1152]{2,1,0:T(2,128)(2,1)S(1)}, u32[]{:S(2)}, u32[]{:S(2)}) %all-to-all-start) | async-done | bytes 589856 | tf_op jit(solution)/shard_map/all_to_all | solution.py:76
  42.6 0.1 copy.87
  42.8 0.0 copy-done.1
  42.8 0.1 convolution_bitcast_fusion
  42.9 0.1 select_reduce_fusion
  43.1 0.1 convolution_bitcast_fusion.1
  43.3 0.1 select_reduce_fusion.1
  43.4 0.8 fusion.53
  44.4 0.2 convolution_convert_fusion.2
  44.6 0.2 fusion.12
  44.8 0.2 fusion.14
  45.1 0.2 fusion.9
  45.3 0.2 fusion.17
  45.6 0.5 multiply_convert_fusion
  46.1 0.2 convolution_convert_fusion
  46.3 3.9 %collective-permute-start.7 = (bf16[4,4,256]{2,0,1:T(4,128)(2,1)S(1)}, bf16[4,4,256]{2,0,1:T(4,128)(2,1)S(1)}, u32[]{:S(2)}, u32[]{:S(2)}) collective-permute-start(bf16[4,4,256]{2,0,1:T(4,128)(2,1)S(1)} %convolution_convert_fusion), channel_id=1, source_target_pairs={{9,0},{10,1},{11,2},{12,3},{13,4},{14,5},{15,6},{16,7},{17,8},{18,... | collective-permute-start | bytes 24584 | tf_op jit(solution)/shard_map/ppermute | solution.py:14
  50.3 0.1 copy.130
  50.3 3.1 %collective-permute-start.6 = (bf16[4,32,256]{2,0,1:T(4,128)(2,1)S(1)}, bf16[4,32,256]{2,0,1:T(4,128)(2,1)S(1)}, u32[]{:S(2)}, u32[]{:S(2)}) collective-permute-start(bf16[4,32,256]{2,0,1:T(4,128)(2,1)S(1)} %copy.130), channel_id=1, source_target_pairs={{8,0},{9,1},{10,2},{11,3},{12,4},{13,5},{14,6},{15,7},{16,8},{17,9... | collective-permute-start | bytes 196616 | tf_op jit(solution)/shard_map/ppermute | solution.py:14
  53.4 5.2 %collective-permute-start.5 = (bf16[4,3,256]{2,0,1:T(4,128)(2,1)S(1)}, bf16[4,3,256]{2,0,1:T(4,128)(2,1)S(1)}, u32[]{:S(2)}, u32[]{:S(2)}) collective-permute-start(bf16[4,3,256]{2,0,1:T(4,128)(2,1)S(1)} %convolution_convert_fusion.2), channel_id=1, source_target_pairs={{7,0},{8,1},{9,2},{10,3},{11,4},{12,5},{13,6},{14,7},{15,8},{16,9}... | collective-permute-start | bytes 18440 | tf_op jit(solution)/shard_map/ppermute | solution.py:14
  58.6 1.9 %collective-permute-start.4 = (f32[32,4,256]{2,0,1:T(8,128)S(1)}, f32[32,4,256]{2,0,1:T(8,128)S(1)}, u32[]{:S(2)}, u32[]{:S(2)}) collective-permute-start(f32[32,4,256]{2,0,1:T(8,128)S(1)} %fusion.12), channel_id=1, source_target_pairs={{1,0},{2,1},{3,2},{4,3},{5,4},{6,5},{7,6},{8,7},{9,8},{10,9},{11,1... | collective-permute-start | bytes 393224 | tf_op jit(solution)/shard_map/ppermute | solution.py:14
  60.5 0.2 convolution_convert_fusion.3
  60.7 7.7 %collective-permute-start = (bf16[3,3,256]{2,0,1:T(4,128)(2,1)S(1)}, bf16[3,3,256]{2,0,1:T(4,128)(2,1)S(1)}, u32[]{:S(2)}, u32[]{:S(2)}) collective-permute-start(bf16[3,3,256]{2,0,1:T(4,128)(2,1)S(1)} %convolution_convert_fusion.3), channel_id=1, source_target_pairs={{0,9},{1,10},{2,11},{3,12},{4,13},{5,14},{6,15},{7,16},{8,17},{9,1... | collective-permute-start | bytes 13832 | tf_op jit(solution)/shard_map/ppermute | solution.py:14
  68.4 1.5 %fusion.2 = f32[32,32,256]{2,0,1:T(8,128)S(1)} fusion(bf16[32,32,1024]{2,1,0:T(8,128)(2,1)S(1)} %multiply_convert_fusion, bf16[1024,256]{1,0:T(8,128)(2,1)S(1)} %fusion.31), kind=kOutput, calls=%fused_computation.4 | convolution fusion | flops 536870912 | bytes 3670016 | tf_op jit(solution)/shard_map/dot_general | solution.py:32
  69.9 0.2 convolution_convert_fusion.1
  70.1 0.0 collective-permute-done
  70.1 5.8 %collective-permute-start.1 = (bf16[3,32,256]{2,0,1:T(4,128)(2,1)S(1)}, bf16[3,32,256]{2,0,1:T(4,128)(2,1)S(1)}, u32[]{:S(2)}, u32[]{:S(2)}) collective-permute-start(bf16[3,32,256]{2,0,1:T(4,128)(2,1)S(1)} %copy.131), channel_id=1, source_target_pairs={{0,8},{1,9},{2,10},{3,11},{4,12},{5,13},{6,14},{7,15},{8,16},{9,17... | collective-permute-start | bytes 147464 | tf_op jit(solution)/shard_map/ppermute | solution.py:14
  76.0 0.2 scatter-add.26
  76.2 6.5 %collective-permute-done.1 = bf16[3,32,256]{2,0,1:T(4,128)(2,1)S(1)} collective-permute-done((bf16[3,32,256]{2,0,1:T(4,128)(2,1)S(1)}, bf16[3,32,256]{2,0,1:T(4,128)(2,1)S(1)}, u32[]{:S(2)}, u32[]{:S(2)}) %collective-permute-start.1) | collective-permute-done | bytes 49184 | tf_op jit(solution)/shard_map/ppermute | solution.py:14
  82.7 1.9 %collective-permute-start.2 = (bf16[3,4,256]{2,0,1:T(4,128)(2,1)S(1)}, bf16[3,4,256]{2,0,1:T(4,128)(2,1)S(1)}, u32[]{:S(2)}, u32[]{:S(2)}) collective-permute-start(bf16[3,4,256]{2,0,1:T(4,128)(2,1)S(1)} %convolution_convert_fusion.1), channel_id=1, source_target_pairs={{0,7},{1,8},{2,9},{3,10},{4,11},{5,12},{6,13},{7,14},{8,15},{9,16}... | collective-permute-start | bytes 18440 | tf_op jit(solution)/shard_map/ppermute | solution.py:14
  84.7 0.3 scatter-add.29
  85.0 7.4 %collective-permute-done.2 = bf16[3,4,256]{2,0,1:T(4,128)(2,1)S(1)} collective-permute-done((bf16[3,4,256]{2,0,1:T(4,128)(2,1)S(1)}, bf16[3,4,256]{2,0,1:T(4,128)(2,1)S(1)}, u32[]{:S(2)}, u32[]{:S(2)}) %collective-permute-start.2) | collective-permute-done | bytes 6176 | tf_op jit(solution)/shard_map/ppermute | solution.py:14
  92.5 1.9 %collective-permute-start.3 = (f32[32,3,256]{2,0,1:T(8,128)S(1)}, f32[32,3,256]{2,0,1:T(8,128)S(1)}, u32[]{:S(2)}, u32[]{:S(2)}) collective-permute-start(f32[32,3,256]{2,0,1:T(8,128)S(1)} %fusion.14), channel_id=1, source_target_pairs={{0,1},{1,2},{2,3},{3,4},{4,5},{5,6},{6,7},{7,8},{8,9},{9,10},{10,1... | collective-permute-start | bytes 294920 | tf_op jit(solution)/shard_map/ppermute | solution.py:14
  94.4 1.9 %add_select_fusion = f32[3,4,256]{2,0,1:T(4,128)S(1)} fusion(bf16[3,4,256]{2,0,1:T(4,128)(2,1)S(1)} %collective-permute-done.2, f32[32,32,256]{2,0,1:T(8,128)S(1)} %scatter-add.29, s32[]{:T(128)} %bitcast.25, s32[]{:T(128)} %bitcast.26, pred[]{:T(512)S(6)} %and.51, pred[]{:T(512)} %and_reduce_fusion), kind=kLoop, calls=%fused_computation.96 | loop fusion | flops 12288 | bytes 30730 | tf_op jit(solution)/shard_map/select.10
  96.3 1.3 %scatter-add.30 = f32[32,32,256]{2,0,1:T(8,128)S(1)} dynamic-update-slice(f32[32,32,256]{2,0,1:T(8,128)S(1)} %scatter-add.29, f32[3,4,256]{2,0,1:T(4,128)S(1)} %add_select_fusion, s32[]{:T(128)} %bitcast.25, s32[]{:T(128)} %bitcast.26, s32[]{:T(128)} %constant.240.clone.1) | dynamic-update-slice | bytes 24580 | tf_op jit(solution)/shard_map/scatter-add | solution.py:116
  97.6 2.9 %collective-permute-done.3 = f32[32,3,256]{2,0,1:T(8,128)S(1)} collective-permute-done((f32[32,3,256]{2,0,1:T(8,128)S(1)}, f32[32,3,256]{2,0,1:T(8,128)S(1)}, u32[]{:S(2)}, u32[]{:S(2)}) %collective-permute-start.3) | collective-permute-done | bytes 98336 | tf_op jit(solution)/shard_map/ppermute | solution.py:14
  100.5 0.0 collective-permute-done.4
  100.6 0.0 collective-permute-done.5
  100.6 0.1 copy.153
  100.7 0.0 collective-permute-done.6
  100.7 0.1 bitcast_dynamic-update-slice_fusion
  100.8 0.0 collective-permute-done.7
  100.8 1.6 %copy.78 = f32[1,32,32,256]{3,2,1,0:T(8,128)} copy(f32[1,32,32,256]{3,1,2,0:T(8,128)S(1)} %fusion.47) | data formatting | bytes 2097152 | tf_op jit(solution)/shard_map/scatter-add | solution.py:116
  (37 shorter events, 0.6 us)
Async XLA Ops:
  0.0 1.0 %copy-start = (bf16[1024,256]{1,0:T(8,128)(2,1)S(1)}, bf16[1024,256]{1,0:T(8,128)(2,1)}, u32[]{:S(2)}) copy-start(bf16[1024,256]{1,0:T(8,128)(2,1)} %param.21) | copy-start | bytes 1572868
  0.0 3.0 %copy-start.2 = (s32[2,1024]{1,0:T(2,128)S(1)}, s32[2,1024]{1,0:T(2,128)}, u32[]{:S(2)}) copy-start(s32[2,1024]{1,0:T(2,128)} %param.23) | copy-start | bytes 24580
  0.0 3.0 %copy-start.3 = (s32[2,1024]{1,0:T(2,128)S(1)}, s32[2,1024]{1,0:T(2,128)}, u32[]{:S(2)}) copy-start(s32[2,1024]{1,0:T(2,128)} %param.24) | copy-start | bytes 24580
  1.0 2.1 %copy-start.5 = (s32[128,8]{0,1:T(8,128)S(1)}, s32[128,8]{0,1:T(8,128)}, u32[]{:S(2)}) copy-start(s32[128,8]{0,1:T(8,128)} %param.22) | copy-start | bytes 12292
  4.0 19.0 %copy-start.4 = (s32[3]{0:T(128)S(1)}, s32[3]{0:T(128)}, u32[]{:S(2)}) copy-start(s32[3]{0:T(128)} %constant.246.clone.1) | copy-start | bytes 40
  4.1 38.7 %copy-start.1 = (f32[8,16]{1,0:T(8,128)S(1)}, f32[8,16]{1,0:T(8,128)}, u32[]{:S(2)}) copy-start(f32[8,16]{1,0:T(8,128)} %param.25) | copy-start | bytes 1540
  5.9 36.7 %all-to-all-start = ((bf16[128,2,1152]{2,1,0:T(2,128)(2,1)}), bf16[128,2,1152]{2,1,0:T(2,128)(2,1)S(1)}, u32[]{:S(2)}, u32[]{:S(2)}) async-start(bf16[128,2,1152]{2,1,0:T(2,128)(2,1)} %copy.61), calls=%async_computation | async-start | bytes 1179648 | tf_op jit(solution)/shard_map/all_to_all | solution.py:76
  46.3 54.5 %collective-permute-start.7 = (bf16[4,4,256]{2,0,1:T(4,128)(2,1)S(1)}, bf16[4,4,256]{2,0,1:T(4,128)(2,1)S(1)}, u32[]{:S(2)}, u32[]{:S(2)}) collective-permute-start(bf16[4,4,256]{2,0,1:T(4,128)(2,1)S(1)} %convolution_convert_fusion), channel_id=1, source_target_pairs={{9,0},{10,1},{11,2},{12,3},{13,4},{14,5},{15,6},{16,7},{17,8},{18,... | collective-permute-start | bytes 24584 | tf_op jit(solution)/shard_map/ppermute | solution.py:14
  50.3 50.4 %collective-permute-start.6 = (bf16[4,32,256]{2,0,1:T(4,128)(2,1)S(1)}, bf16[4,32,256]{2,0,1:T(4,128)(2,1)S(1)}, u32[]{:S(2)}, u32[]{:S(2)}) collective-permute-start(bf16[4,32,256]{2,0,1:T(4,128)(2,1)S(1)} %copy.130), channel_id=1, source_target_pairs={{8,0},{9,1},{10,2},{11,3},{12,4},{13,5},{14,6},{15,7},{16,8},{17,9... | collective-permute-start | bytes 196616 | tf_op jit(solution)/shard_map/ppermute | solution.py:14
  53.4 47.2 %collective-permute-start.5 = (bf16[4,3,256]{2,0,1:T(4,128)(2,1)S(1)}, bf16[4,3,256]{2,0,1:T(4,128)(2,1)S(1)}, u32[]{:S(2)}, u32[]{:S(2)}) collective-permute-start(bf16[4,3,256]{2,0,1:T(4,128)(2,1)S(1)} %convolution_convert_fusion.2), channel_id=1, source_target_pairs={{7,0},{8,1},{9,2},{10,3},{11,4},{12,5},{13,6},{14,7},{15,8},{16,9}... | collective-permute-start | bytes 18440 | tf_op jit(solution)/shard_map/ppermute | solution.py:14
  58.6 42.0 %collective-permute-start.4 = (f32[32,4,256]{2,0,1:T(8,128)S(1)}, f32[32,4,256]{2,0,1:T(8,128)S(1)}, u32[]{:S(2)}, u32[]{:S(2)}) collective-permute-start(f32[32,4,256]{2,0,1:T(8,128)S(1)} %fusion.12), channel_id=1, source_target_pairs={{1,0},{2,1},{3,2},{4,3},{5,4},{6,5},{7,6},{8,7},{9,8},{10,9},{11,1... | collective-permute-start | bytes 393224 | tf_op jit(solution)/shard_map/ppermute | solution.py:14
  60.7 9.4 %collective-permute-start = (bf16[3,3,256]{2,0,1:T(4,128)(2,1)S(1)}, bf16[3,3,256]{2,0,1:T(4,128)(2,1)S(1)}, u32[]{:S(2)}, u32[]{:S(2)}) collective-permute-start(bf16[3,3,256]{2,0,1:T(4,128)(2,1)S(1)} %convolution_convert_fusion.3), channel_id=1, source_target_pairs={{0,9},{1,10},{2,11},{3,12},{4,13},{5,14},{6,15},{7,16},{8,17},{9,1... | collective-permute-start | bytes 13832 | tf_op jit(solution)/shard_map/ppermute | solution.py:14
  70.1 12.6 %collective-permute-start.1 = (bf16[3,32,256]{2,0,1:T(4,128)(2,1)S(1)}, bf16[3,32,256]{2,0,1:T(4,128)(2,1)S(1)}, u32[]{:S(2)}, u32[]{:S(2)}) collective-permute-start(bf16[3,32,256]{2,0,1:T(4,128)(2,1)S(1)} %copy.131), channel_id=1, source_target_pairs={{0,8},{1,9},{2,10},{3,11},{4,12},{5,13},{6,14},{7,15},{8,16},{9,17... | collective-permute-start | bytes 147464 | tf_op jit(solution)/shard_map/ppermute | solution.py:14
  82.7 9.8 %collective-permute-start.2 = (bf16[3,4,256]{2,0,1:T(4,128)(2,1)S(1)}, bf16[3,4,256]{2,0,1:T(4,128)(2,1)S(1)}, u32[]{:S(2)}, u32[]{:S(2)}) collective-permute-start(bf16[3,4,256]{2,0,1:T(4,128)(2,1)S(1)} %convolution_convert_fusion.1), channel_id=1, source_target_pairs={{0,7},{1,8},{2,9},{3,10},{4,11},{5,12},{6,13},{7,14},{8,15},{9,16}... | collective-permute-start | bytes 18440 | tf_op jit(solution)/shard_map/ppermute | solution.py:14
  92.5 8.0 %collective-permute-start.3 = (f32[32,3,256]{2,0,1:T(8,128)S(1)}, f32[32,3,256]{2,0,1:T(8,128)S(1)}, u32[]{:S(2)}, u32[]{:S(2)}) collective-permute-start(f32[32,3,256]{2,0,1:T(8,128)S(1)} %fusion.14), channel_id=1, source_target_pairs={{0,1},{1,2},{2,3},{3,4},{4,5},{5,6},{6,7},{7,8},{8,9},{9,10},{10,1... | collective-permute-start | bytes 294920 | tf_op jit(solution)/shard_map/ppermute | solution.py:14

commit v5 on v3

--- a/solution.py
+++ b/solution.py
@@ -90,20 +90,35 @@
     spread_v = spread(kernel_of(taper, meta_rows[3]), meta_rows[1], padded_side)
     low = place_rows(spread_u[0:4], spread_v, arrived_rows)
     high = place_rows(spread_u[TS + 4 : TS + 7], spread_v, arrived_rows)
+    edge_lo = place_rows(spread_u[4 : TS + 4], spread_v[0:4], arrived_rows)
+    edge_hi = place_rows(spread_u[4 : TS + 4], spread_v[TS + 4 : TS + 7], arrived_rows)
 
+    tile_row = lax.axis_index("tile") % TILES_Y
     from_below = passed_along(low.astype(jnp.bfloat16), "tile", -TILES_Y)
     from_above = passed_along(high.astype(jnp.bfloat16), "tile", TILES_Y)
-    inner = place_rows(spread_u[4 : TS + 4], spread_v, arrived_rows)
-    inner = inner.at[TS - 4 : TS].add(from_below.astype(jnp.float32))
-    inner = inner.at[0:3].add(from_above.astype(jnp.float32))
-    tile_row = lax.axis_index("tile") % TILES_Y
-    from_next = passed_along(inner[:, 0:4], "tile", -1)
-    from_prev = passed_along(inner[:, TS + 4 : TS + 7], "tile", 1)
-    from_next = jnp.where(tile_row + 1 < TILES_Y, from_next, 0.0)
-    from_prev = jnp.where(tile_row >= 1, from_prev, 0.0)
-    result = inner[:, 4 : TS + 4]
+    from_next = passed_along(edge_lo, "tile", -1)
+    from_prev = passed_along(edge_hi, "tile", 1)
+    result = place_rows(spread_u[4 : TS + 4], spread_v[4 : TS + 4], arrived_rows)
+    corner_lo = jnp.concatenate([from_below[:, 0:4], from_above[:, 0:4]], 0)
+    corner_hi = jnp.concatenate([from_below[:, TS + 4 : TS + 7], from_above[:, TS + 4 : TS + 7]], 0)
+    corner_next = passed_along(corner_lo, "tile", -1).astype(jnp.float32)
+    corner_prev = passed_along(corner_hi, "tile", 1).astype(jnp.float32)
+    has_next = tile_row + 1 < TILES_Y
+    has_prev = tile_row >= 1
+    from_next = jnp.where(has_next, from_next, 0.0)
+    from_prev = jnp.where(has_prev, from_prev, 0.0)
+    corner_next = jnp.where(has_next, corner_next, 0.0)
+    corner_prev = jnp.where(has_prev, corner_prev, 0.0)
+    from_below = from_below[:, 4 : TS + 4].astype(jnp.float32)
+    from_above = from_above[:, 4 : TS + 4].astype(jnp.float32)
+    result = result.at[TS - 4 : TS].add(from_below)
+    result = result.at[0:3].add(from_above)
     result = result.at[:, TS - 4 : TS].add(from_next)
     result = result.at[:, 0:3].add(from_prev)
+    result = result.at[TS - 4 : TS, TS - 4 : TS].add(corner_next[0:4])
+    result = result.at[0:3, TS - 4 : TS].add(corner_next[4:7])
+    result = result.at[TS - 4 : TS, 0:3].add(corner_prev[0:4])
+    result = result.at[0:3, 0:3].add(corner_prev[4:7])
     return result[None]
 
 

time: 73.8 us -> 83.3 us (1.13)
  the two profiles are of different devices: /device:TPU:68 before, /device:TPU:57 now
where the time goes in v5:
time: 83.3 us; the launch traced here: 82.7 us
  starting transfers between devices  42.1 us (51%)
  waiting for transfers between devices  22.5 us (27%)
  local copies, waits for them, and re-layouts  9.5 us (11%)
  matrix products  4.69 us (6%)
  other arithmetic  3.36 us (4%)
    ppermute x6, starting transfers between devices, passed_along(): return lax.ppermute(value, axis, pairs)  25 us
    all_to_all x1, waiting for transfers between devices, body(): lax.all_to_all(packed, 'tile', split_axis=0, concat_axis=0, tiled=True)  17.3 us
    all_to_all x1, starting transfers between devices, body(): lax.all_to_all(packed, 'tile', split_axis=0, concat_axis=0, tiled=True)  17.1 us
    ppermute x6, waiting for transfers between devices, passed_along(): return lax.ppermute(value, axis, pairs)  5.12 us
    unnamed x28, local copies, waits for them, and re-layouts  2.79 us
    another operation x5, other arithmetic  2.73 us
    dot_general x1, matrix products, body(): outgoing = jnp.dot(chosen, visibilities, preferred_element_type=jnp.float32)  1.84 us
    another operation x1, local copies, waits for them, and re-layouts, body(): jnp.stack([jnp.concatenate([outgoing[(h * per_half + j) * tile_count:(h *...  1.73 us
  transfers between devices with their start and end apart: 7, of which 2 were waited for; matrix products, arithmetic and copies ran while one was open for 4% of the time, Pallas kernels for 0%

profile of v5, /device:TPU:57, one launch (start us, length us, event | category | flops | bytes accessed | tf_op | source)
XLA Modules:
  0.0 82.7 jit_solution(1919020971644717825)
XLA Ops:
  0.0 0.0 copy-start
  0.0 1.0 %copy-done = bf16[1024,256]{1,0:T(8,128)(2,1)S(1)} copy-done((bf16[1024,256]{1,0:T(8,128)(2,1)S(1)}, bf16[1024,256]{1,0:T(8,128)(2,1)}, u32[]{:S(2)}) %copy-start) | copy-done | bytes 524312
  1.0 0.0 copy-start.4
  1.0 0.0 copy-start.5
  1.0 1.8 %fusion.7 = bf16[1024,256]{0,1:T(8,128)(2,1)S(1)} fusion(bf16[1024,256]{1,0:T(8,128)(2,1)S(1)} %copy-done, s32[1024]{0:T(1024)} %bitcast.82), kind=kOutput, calls=%fused_computation.13 | convolution fusion | flops 538181632 | bytes 1052672 | tf_op jit(solution)/shard_map/dot_general | solution.py:49
  2.9 0.0 copy-start.7
  2.9 0.0 copy-done.4
  3.0 0.0 copy-done.5
  3.1 0.5 copy-done.7
  3.6 0.9 %fusion.8 = bf16[4,1024]{1,0:T(4,128)(2,1)S(1)} fusion(s32[1024]{0:T(1024)S(1)} %bitcast.83, bf16[2,1024]{1,0:T(2,128)(2,1)S(1)} %convert.9, bf16[2,1024]{1,0:T(2,128)(2,1)S(1)} %convert.8), kind=kOutput, calls=%fused_computation.18 | convolution fusion | flops 9457664 | bytes 20480 | tf_op jit(solution)/shard_map/dot_general | solution.py:52
  4.5 0.1 pad_maximum_fusion
  4.6 0.0 copy-start.6
  4.6 1.7 %copy.40 = bf16[128,2,1152]{2,1,0:T(2,128)(2,1)} copy(bf16[128,2,1152]{0,2,1:T(8,128)(2,1)S(1)} %pad_maximum_fusion) | data formatting | bytes 1179648 | tf_op jit(solution)/shard_map/stack | solution.py:62
  6.3 0.0 copy-start.3
  6.3 17.1 %all-to-all-start = ((bf16[128,2,1152]{2,1,0:T(2,128)(2,1)}), bf16[128,2,1152]{2,1,0:T(2,128)(2,1)S(1)}, u32[]{:S(2)}, u32[]{:S(2)}) async-start(bf16[128,2,1152]{2,1,0:T(2,128)(2,1)} %copy.40), calls=%async_computation | async-start | bytes 1179648 | tf_op jit(solution)/shard_map/all_to_all | solution.py:76
  23.5 0.6 fusion.45
  24.1 0.0 copy-done.6
  24.1 0.8 and_reduce_fusion
  24.8 17.3 %all-to-all-done = bf16[128,2,1152]{2,1,0:T(2,128)(2,1)S(1)} async-done(((bf16[128,2,1152]{2,1,0:T(2,128)(2,1)}), bf16[128,2,1152]{2,1,0:T(2,128)(2,1)S(1)}, u32[]{:S(2)}, u32[]{:S(2)}) %all-to-all-start) | async-done | bytes 589856 | tf_op jit(solution)/shard_map/all_to_all | solution.py:76
  42.2 0.1 copy.52
  42.4 0.0 copy-done.3
  42.4 0.1 convolution_bitcast_fusion.1
  42.5 0.1 select_reduce_fusion.1
  42.7 0.0 copy-start.1
  42.7 0.1 convolution_bitcast_fusion
  42.9 0.1 select_reduce_fusion
  43.1 0.8 fusion.43
  43.8 0.0 copy-done.1
  43.9 0.0 slice-start
  44.0 0.2 convolution_convert_fusion.1
  44.3 6.2 %collective-permute-start.1 = (bf16[3,40,256]{2,1,0:T(8,128)(2,1)S(1)}, bf16[3,40,256]{2,1,0:T(8,128)(2,1)S(1)}, u32[]{:S(2)}, u32[]{:S(2)}) collective-permute-start(bf16[3,40,256]{2,1,0:T(8,128)(2,1)S(1)} %convolution_convert_fusion.1), channel_id=1, source_target_pairs={{0,8},{1,9},{2,10},{3,11},{4,12},{5,13},{6,14},{7,15},{8,16},{9,17... | collective-permute-start | bytes 184328 | tf_op jit(solution)/shard_map/ppermute | solution.py:14
  50.5 0.0 slice-done
  50.5 0.3 convolution_convert_fusion
  50.7 3.0 %collective-permute-start = (bf16[4,40,256]{2,1,0:T(8,128)(2,1)S(1)}, bf16[4,40,256]{2,1,0:T(8,128)(2,1)S(1)}, u32[]{:S(2)}, u32[]{:S(2)}) collective-permute-start(bf16[4,40,256]{2,1,0:T(8,128)(2,1)S(1)} %convolution_convert_fusion), channel_id=1, source_target_pairs={{8,0},{9,1},{10,2},{11,3},{12,4},{13,5},{14,6},{15,7},{16,8},{17,9... | collective-permute-start | bytes 245768 | tf_op jit(solution)/shard_map/ppermute | solution.py:14
  53.7 0.2 fusion.9
  54.0 0.1 copy.51
  54.0 6.2 %collective-permute-start.3 = (f32[32,3,256]{2,1,0:T(4,128)S(1)}, f32[32,3,256]{2,1,0:T(4,128)S(1)}, u32[]{:S(2)}, u32[]{:S(2)}) collective-permute-start(f32[32,3,256]{2,1,0:T(4,128)S(1)} %copy.51), channel_id=1, source_target_pairs={{0,1},{1,2},{2,3},{3,4},{4,5},{5,6},{6,7},{7,8},{8,9},{9,10},{10,1... | collective-permute-start | bytes 294920 | tf_op jit(solution)/shard_map/ppermute | solution.py:14
  60.3 0.2 fusion.11
  60.5 0.1 copy.50
  60.6 1.9 %collective-permute-start.2 = (f32[32,4,256]{2,1,0:T(4,128)S(1)}, f32[32,4,256]{2,1,0:T(4,128)S(1)}, u32[]{:S(2)}, u32[]{:S(2)}) collective-permute-start(f32[32,4,256]{2,1,0:T(4,128)S(1)} %copy.50), channel_id=1, source_target_pairs={{1,0},{2,1},{3,2},{4,3},{5,4},{6,5},{7,6},{8,7},{9,8},{10,9},{11,1... | collective-permute-start | bytes 393224 | tf_op jit(solution)/shard_map/ppermute | solution.py:14
  62.5 0.7 fusion.2
  63.2 0.0 collective-permute-done.1
  63.3 0.0 collective-permute-done
  63.3 5.8 %collective-permute-start.5 = (bf16[7,3,256]{2,1,0:T(4,128)(2,1)S(1)}, bf16[7,3,256]{2,1,0:T(4,128)(2,1)S(1)}, u32[]{:S(2)}, u32[]{:S(2)}) collective-permute-start(bf16[7,3,256]{2,1,0:T(4,128)(2,1)S(1)} %pad_maximum_fusion.2), channel_id=1, source_target_pairs={{0,1},{1,2},{2,3},{3,4},{4,5},{5,6},{6,7},{7,8},{8,9},{9,10},{10,1... | collective-permute-start | bytes 32264 | tf_op jit(solution)/shard_map/ppermute | solution.py:14
  69.1 1.9 %collective-permute-start.4 = (bf16[7,4,256]{2,1,0:T(4,128)(2,1)S(1)}, bf16[7,4,256]{2,1,0:T(4,128)(2,1)S(1)}, u32[]{:S(2)}, u32[]{:S(2)}) collective-permute-start(bf16[7,4,256]{2,1,0:T(4,128)(2,1)S(1)} %pad_maximum_fusion.1), channel_id=1, source_target_pairs={{1,0},{2,1},{3,2},{4,3},{5,4},{6,5},{7,6},{8,7},{9,8},{10,9},{11,1... | collective-permute-start | bytes 43016 | tf_op jit(solution)/shard_map/ppermute | solution.py:14
  71.1 0.0 collective-permute-done.5
  71.2 5.1 %collective-permute-done.4 = bf16[7,4,256]{2,1,0:T(4,128)(2,1)S(1)} collective-permute-done((bf16[7,4,256]{2,1,0:T(4,128)(2,1)S(1)}, bf16[7,4,256]{2,1,0:T(4,128)(2,1)S(1)}, u32[]{:S(2)}, u32[]{:S(2)}) %collective-permute-start.4) | collective-permute-done | bytes 14368 | tf_op jit(solution)/shard_map/ppermute | solution.py:14
  76.3 0.0 collective-permute-done.2
  76.3 0.1 fusion.24
  76.4 0.0 collective-permute-done.3
  76.4 0.3 scatter-add.31
  76.8 1.9 %add_select_fusion = f32[3,4,256]{2,1,0:T(4,128)S(1)} fusion(f32[7,4,256]{2,1,0:T(4,128)S(1)} %convert_select_fusion.1, f32[32,32,256]{2,1,0:T(8,128)S(1)} %fusion.37, s32[]{:T(128)} %bitcast.25, s32[]{:T(128)} %bitcast.26, pred[]{:T(512)} %and_reduce_fusion), kind=kLoop, calls=%fused_computation.80 | loop fusion | flops 6144 | bytes 36873 | tf_op jit(solution)/shard_map/select.13
  78.7 1.4 %scatter-add.35 = f32[32,32,256]{2,1,0:T(8,128)S(1)} dynamic-update-slice(f32[32,32,256]{2,1,0:T(8,128)S(1)} %fusion.37, f32[3,4,256]{2,1,0:T(4,128)S(1)} %add_select_fusion, s32[]{:T(128)} %bitcast.25, s32[]{:T(128)} %bitcast.26, s32[]{:T(128)} %constant.238.clone.1) | dynamic-update-slice | bytes 24580 | tf_op jit(solution)/shard_map/scatter-add | solution.py:119
  80.2 0.2 scatter-add.36
  80.3 0.0 copy-start.2
  80.4 0.9 %copy-done.2 = f32[32,32,256]{2,1,0:T(8,128)} copy-done((f32[32,32,256]{2,1,0:T(8,128)}, f32[32,32,256]{2,1,0:T(8,128)S(1)}, u32[]{:S(2)}) %copy-start.2) | copy-done | bytes 1048600
  81.3 1.4 %scatter-add.39 = f32[1,32,32,256]{3,2,1,0:T(8,128)} dynamic-update-slice(f32[1,32,32,256]{3,2,1,0:T(8,128)} %bitcast.75, f32[1,3,3,256]{3,2,1,0:T(4,128)S(1)} %fusion.38, s32[]{:T(128)} %constant.238.clone.1, s32[]{:T(128)} %constant.238.clone.1, s32[]{:T(128)} %constant.238.clone.1, s32[]{:T(128)} %constant.238.clone.1) | dynamic-update-slice | bytes 18436 | tf_op jit(solution)/shard_map/scatter-add | solution.py:121
  (40 shorter events, 0.6 us)
Async XLA Ops:
  0.0 1.0 %copy-start = (bf16[1024,256]{1,0:T(8,128)(2,1)S(1)}, bf16[1024,256]{1,0:T(8,128)(2,1)}, u32[]{:S(2)}) copy-start(bf16[1024,256]{1,0:T(8,128)(2,1)} %param.21) | copy-start | bytes 1572868
  1.0 1.9 %copy-start.4 = (s32[2,1024]{1,0:T(2,128)S(1)}, s32[2,1024]{1,0:T(2,128)}, u32[]{:S(2)}) copy-start(s32[2,1024]{1,0:T(2,128)} %param.23) | copy-start | bytes 24580
  1.0 1.9 %copy-start.5 = (s32[2,1024]{1,0:T(2,128)S(1)}, s32[2,1024]{1,0:T(2,128)}, u32[]{:S(2)}) copy-start(s32[2,1024]{1,0:T(2,128)} %param.24) | copy-start | bytes 24580
  2.9 0.7 copy-start.7
  4.6 19.5 %copy-start.6 = (s32[3]{0:T(128)S(1)}, s32[3]{0:T(128)}, u32[]{:S(2)}) copy-start(s32[3]{0:T(128)} %constant.244.clone.1) | copy-start | bytes 40
  6.3 36.1 %copy-start.3 = (f32[8,16]{1,0:T(8,128)S(1)}, f32[8,16]{1,0:T(8,128)}, u32[]{:S(2)}) copy-start(f32[8,16]{1,0:T(8,128)} %param.25) | copy-start | bytes 1540
  6.3 35.9 %all-to-all-start = ((bf16[128,2,1152]{2,1,0:T(2,128)(2,1)}), bf16[128,2,1152]{2,1,0:T(2,128)(2,1)S(1)}, u32[]{:S(2)}, u32[]{:S(2)}) async-start(bf16[128,2,1152]{2,1,0:T(2,128)(2,1)} %copy.40), calls=%async_computation | async-start | bytes 1179648 | tf_op jit(solution)/shard_map/all_to_all | solution.py:76
  42.7 1.2 %copy-start.1 = (f32[40,1024]{1,0:T(8,128)}, f32[40,1024]{1,0:T(8,128)S(1)}, u32[]{:S(2)}) copy-start(f32[40,1024]{1,0:T(8,128)S(1)} %select_reduce_fusion.1) | copy-start | bytes 491524
  43.9 6.6 %slice-start = ((f32[40,1024]{1,0:T(8,128)}), f32[4,1024]{1,0:T(4,128)S(1)}, s32[]{:S(2)}) async-start(f32[40,1024]{1,0:T(8,128)} %copy-done.1), calls=%async_computation.1 | async-start | bytes 32768 | tf_op jit(solution)/shard_map/slice | solution.py:91
  44.3 19.0 %collective-permute-start.1 = (bf16[3,40,256]{2,1,0:T(8,128)(2,1)S(1)}, bf16[3,40,256]{2,1,0:T(8,128)(2,1)S(1)}, u32[]{:S(2)}, u32[]{:S(2)}) collective-permute-start(bf16[3,40,256]{2,1,0:T(8,128)(2,1)S(1)} %convolution_convert_fusion.1), channel_id=1, source_target_pairs={{0,8},{1,9},{2,10},{3,11},{4,12},{5,13},{6,14},{7,15},{8,16},{9,17... | collective-permute-start | bytes 184328 | tf_op jit(solution)/shard_map/ppermute | solution.py:14
  50.7 12.5 %collective-permute-start = (bf16[4,40,256]{2,1,0:T(8,128)(2,1)S(1)}, bf16[4,40,256]{2,1,0:T(8,128)(2,1)S(1)}, u32[]{:S(2)}, u32[]{:S(2)}) collective-permute-start(bf16[4,40,256]{2,1,0:T(8,128)(2,1)S(1)} %convolution_convert_fusion), channel_id=1, source_target_pairs={{8,0},{9,1},{10,2},{11,3},{12,4},{13,5},{14,6},{15,7},{16,8},{17,9... | collective-permute-start | bytes 245768 | tf_op jit(solution)/shard_map/ppermute | solution.py:14
  54.0 22.3 %collective-permute-start.3 = (f32[32,3,256]{2,1,0:T(4,128)S(1)}, f32[32,3,256]{2,1,0:T(4,128)S(1)}, u32[]{:S(2)}, u32[]{:S(2)}) collective-permute-start(f32[32,3,256]{2,1,0:T(4,128)S(1)} %copy.51), channel_id=1, source_target_pairs={{0,1},{1,2},{2,3},{3,4},{4,5},{5,6},{6,7},{7,8},{8,9},{9,10},{10,1... | collective-permute-start | bytes 294920 | tf_op jit(solution)/shard_map/ppermute | solution.py:14
  60.6 15.7 %collective-permute-start.2 = (f32[32,4,256]{2,1,0:T(4,128)S(1)}, f32[32,4,256]{2,1,0:T(4,128)S(1)}, u32[]{:S(2)}, u32[]{:S(2)}) collective-permute-start(f32[32,4,256]{2,1,0:T(4,128)S(1)} %copy.50), channel_id=1, source_target_pairs={{1,0},{2,1},{3,2},{4,3},{5,4},{6,5},{7,6},{8,7},{9,8},{10,9},{11,1... | collective-permute-start | bytes 393224 | tf_op jit(solution)/shard_map/ppermute | solution.py:14
  63.3 7.8 %collective-permute-start.5 = (bf16[7,3,256]{2,1,0:T(4,128)(2,1)S(1)}, bf16[7,3,256]{2,1,0:T(4,128)(2,1)S(1)}, u32[]{:S(2)}, u32[]{:S(2)}) collective-permute-start(bf16[7,3,256]{2,1,0:T(4,128)(2,1)S(1)} %pad_maximum_fusion.2), channel_id=1, source_target_pairs={{0,1},{1,2},{2,3},{3,4},{4,5},{5,6},{6,7},{7,8},{8,9},{9,10},{10,1... | collective-permute-start | bytes 32264 | tf_op jit(solution)/shard_map/ppermute | solution.py:14
  69.1 7.1 %collective-permute-start.4 = (bf16[7,4,256]{2,1,0:T(4,128)(2,1)S(1)}, bf16[7,4,256]{2,1,0:T(4,128)(2,1)S(1)}, u32[]{:S(2)}, u32[]{:S(2)}) collective-permute-start(bf16[7,4,256]{2,1,0:T(4,128)(2,1)S(1)} %pad_maximum_fusion.1), channel_id=1, source_target_pairs={{1,0},{2,1},{3,2},{4,3},{5,4},{6,5},{7,6},{8,7},{9,8},{10,9},{11,1... | collective-permute-start | bytes 43016 | tf_op jit(solution)/shard_map/ppermute | solution.py:14
  80.3 1.0 %copy-start.2 = (f32[32,32,256]{2,1,0:T(8,128)}, f32[32,32,256]{2,1,0:T(8,128)S(1)}, u32[]{:S(2)}) copy-start(f32[32,32,256]{2,1,0:T(8,128)S(1)} %scatter-add.36) | copy-start | bytes 3145732

commit v6 on v3

--- a/solution.py
+++ b/solution.py
@@ -97,10 +97,10 @@
     inner = inner.at[TS - 4 : TS].add(from_below.astype(jnp.float32))
     inner = inner.at[0:3].add(from_above.astype(jnp.float32))
     tile_row = lax.axis_index("tile") % TILES_Y
-    from_next = passed_along(inner[:, 0:4], "tile", -1)
-    from_prev = passed_along(inner[:, TS + 4 : TS + 7], "tile", 1)
-    from_next = jnp.where(tile_row + 1 < TILES_Y, from_next, 0.0)
-    from_prev = jnp.where(tile_row >= 1, from_prev, 0.0)
+    from_next = passed_along(inner[:, 0:4].astype(jnp.bfloat16), "tile", -1)
+    from_prev = passed_along(inner[:, TS + 4 : TS + 7].astype(jnp.bfloat16), "tile", 1)
+    from_next = jnp.where(tile_row + 1 < TILES_Y, from_next.astype(jnp.float32), 0.0)
+    from_prev = jnp.where(tile_row >= 1, from_prev.astype(jnp.float32), 0.0)
     result = inner[:, 4 : TS + 4]
     result = result.at[:, TS - 4 : TS].add(from_next)
     result = result.at[:, 0:3].add(from_prev)

time: 73.8 us -> 73.8 us (level)
  other arithmetic: 0.54 us -> 2.05 us
  local copies, waits for them, and re-layouts: 4.95 us -> 4.07 us
    another operation x2 -> x3, other arithmetic: 0.01 us -> 1.53 us
    unnamed x26 -> x22, local copies, waits for them, and re-layouts: 1.35 us -> 0.3 us
  transfers between devices with their start and end apart: 4 -> 4, of which waited for: 3 -> 2; matrix products, arithmetic and copies ran while one was open for 2% -> 2% of each run, Pallas kernels for 0% -> 0%
where the time goes in v6:
time: 73.8 us; the launch traced here: 73.4 us
  blocking collectives  36.5 us (49%)
  starting transfers between devices  16.8 us (23%)
  waiting for transfers between devices  9.16 us (12%)
  matrix products  4.47 us (6%)
  local copies, waits for them, and re-layouts  4.07 us (6%)
  other arithmetic  2.05 us (3%)
    all_to_all x1, blocking collectives, body(): lax.all_to_all(packed, 'tile', split_axis=0, concat_axis=0, tiled=True)  36.5 us
    ppermute x4, starting transfers between devices, passed_along(): return lax.ppermute(value, axis, pairs)  16.8 us
    ppermute x4, waiting for transfers between devices, passed_along(): return lax.ppermute(value, axis, pairs)  9.16 us
    dot_general x1, matrix products, body(): outgoing = jnp.dot(chosen, visibilities, preferred_element_type=jnp.float32)  1.88 us
    scatter-add x1, local copies, waits for them, and re-layouts, body(): result = result.at[:, 0:3].add(from_prev)  1.87 us
    another operation x3, other arithmetic  1.53 us
  transfers between devices with their start and end apart: 4, of which 2 were waited for; matrix products, arithmetic and copies ran while one was open for 2% of the time, Pallas kernels for 0%

profile of v6, /device:TPU:68, one launch (start us, length us, event | category | flops | bytes accessed | tf_op | source)
XLA Modules:
  0.0 73.4 jit_solution(15419901658675985462)
XLA Ops:
  0.0 0.0 copy-start
  0.0 0.8 %convert.12 = bf16[2,1024]{1,0:T(2,128)(2,1)S(1)} convert(s32[2,1024]{1,0:T(2,128)} %param.15) | non-fusion elementwise | flops 2048 | bytes 12288 | tf_op jit(solution)/shard_map/convert.4
  0.8 0.7 convert.13
  1.5 0.0 copy-done
  1.5 0.0 copy-start.4
  1.5 1.9 %fusion.7 = bf16[1024,256]{0,1:T(8,128)(2,1)S(1)} fusion(bf16[1024,256]{1,0:T(8,128)(2,1)S(1)} %copy-done, s32[1024]{0:T(1024)} %bitcast.76), kind=kOutput, calls=%fused_computation.13 | convolution fusion | flops 538181632 | bytes 1052672 | tf_op jit(solution)/shard_map/dot_general | solution.py:49
  3.4 0.0 copy-done.4
  3.4 0.9 %fusion.8 = bf16[4,1024]{1,0:T(4,128)(2,1)S(1)} fusion(s32[1024]{0:T(1024)S(1)} %bitcast.77, bf16[2,1024]{1,0:T(2,128)(2,1)S(1)} %convert.13, bf16[2,1024]{1,0:T(2,128)(2,1)S(1)} %convert.12), kind=kOutput, calls=%fused_computation.18 | convolution fusion | flops 9457664 | bytes 20480 | tf_op jit(solution)/shard_map/dot_general | solution.py:52
  4.4 0.1 pad_maximum_fusion
  4.5 0.0 copy-start.3
  4.5 0.7 copy.32
  5.2 36.5 %all_to_all.5 = bf16[128,2,1152]{2,1,0:T(2,128)(2,1)S(1)} all-to-all(bf16[128,2,1152]{2,1,0:T(2,128)(2,1)S(1)} %copy.32), channel_id=1, replica_groups=mesh['chan'=4,'tile'=128] {'tile'}, dimensions={0} | all-to-all | bytes 1179648 | tf_op jit(solution)/shard_map/all_to_all | solution.py:76
  41.7 0.1 copy.42
  41.9 0.0 copy-done.3
  41.9 0.1 convolution_bitcast_fusion.1
  42.0 0.1 select_reduce_fusion.1
  42.2 0.0 copy-start.2
  42.2 0.1 convolution_bitcast_fusion
  42.4 0.8 %fusion.34 = (bf16[128,1,256]{2,1,0:T(2,128)(2,1)S(1)}, bf16[128,1,256]{2,1,0:T(2,128)(2,1)S(1)}, bf16[128,1,256]{2,1,0:T(2,128)(2,1)S(1)}, bf16[128,1,256]{2,1,...) fusion(bf16[128,2,1152]{2,1,0:T(2,128)(2,1)S(1)} %all_to_all.5), kind=kLoop, calls=%fused_computation.74 | loop fusion | bytes 1048576 | tf_op jit(solution)/shard_map/slice | solution.py:79
  43.2 0.0 copy-done.2
  43.2 0.0 slice-start
  43.2 0.1 select_reduce_fusion
  43.5 0.2 convolution_convert_fusion.1
  43.7 0.2 slice-done
  43.9 0.3 convolution_convert_fusion
  44.2 4.8 %collective-permute-start.1 = (bf16[3,40,256]{2,1,0:T(8,128)(2,1)S(1)}, bf16[3,40,256]{2,1,0:T(8,128)(2,1)S(1)}, u32[]{:S(2)}, u32[]{:S(2)}) collective-permute-start(bf16[3,40,256]{2,1,0:T(8,128)(2,1)S(1)} %convolution_convert_fusion.1), channel_id=1, source_target_pairs={{0,8},{1,9},{2,10},{3,11},{4,12},{5,13},{6,14},{7,15},{8,16},{9,17... | collective-permute-start | bytes 184328 | tf_op jit(solution)/shard_map/ppermute | solution.py:14
  49.0 5.8 %collective-permute-start = (bf16[4,40,256]{2,1,0:T(8,128)(2,1)S(1)}, bf16[4,40,256]{2,1,0:T(8,128)(2,1)S(1)}, u32[]{:S(2)}, u32[]{:S(2)}) collective-permute-start(bf16[4,40,256]{2,1,0:T(8,128)(2,1)S(1)} %convolution_convert_fusion), channel_id=1, source_target_pairs={{8,0},{9,1},{10,2},{11,3},{12,4},{13,5},{14,6},{15,7},{16,8},{17,9... | collective-permute-start | bytes 245768 | tf_op jit(solution)/shard_map/ppermute | solution.py:14
  54.8 0.9 %fusion.2 = f32[32,40,256]{2,1,0:T(8,128)S(1)} fusion(f32[40,1024]{1,0:T(8,128)S(1)} %select_reduce_fusion, f32[32,1024]{1,0:T(8,128)S(1)} %slice.226, bf16[1024,256]{1,0:T(8,128)(2,1)S(1)} %fusion.20), kind=kOutput, calls=%fused_computation.4 | convolution fusion | flops 673710080 | bytes 2129920 | tf_op jit(solution)/shard_map/dot_general | solution.py:32
  55.7 3.5 %collective-permute-done = bf16[4,40,256]{2,1,0:T(8,128)(2,1)S(1)} collective-permute-done((bf16[4,40,256]{2,1,0:T(8,128)(2,1)S(1)}, bf16[4,40,256]{2,1,0:T(8,128)(2,1)S(1)}, u32[]{:S(2)}, u32[]{:S(2)}) %collective-permute-start) | collective-permute-done | bytes 81952 | tf_op jit(solution)/shard_map/ppermute | solution.py:14
  59.2 0.0 collective-permute-done.1
  59.3 0.1 convert.14
  59.4 4.2 %collective-permute-start.2 = (bf16[32,4,256]{2,1,0:T(4,128)(2,1)S(1)}, bf16[32,4,256]{2,1,0:T(4,128)(2,1)S(1)}, u32[]{:S(2)}, u32[]{:S(2)}) collective-permute-start(bf16[32,4,256]{2,1,0:T(4,128)(2,1)S(1)} %slice.243), channel_id=1, source_target_pairs={{1,0},{2,1},{3,2},{4,3},{5,4},{6,5},{7,6},{8,7},{9,8},{10,9},{11,1... | collective-permute-start | bytes 196616 | tf_op jit(solution)/shard_map/ppermute | solution.py:14
  63.6 0.1 slice.241
  63.8 1.9 %collective-permute-start.3 = (bf16[32,3,256]{2,1,0:T(4,128)(2,1)S(1)}, bf16[32,3,256]{2,1,0:T(4,128)(2,1)S(1)}, u32[]{:S(2)}, u32[]{:S(2)}) collective-permute-start(bf16[32,3,256]{2,1,0:T(4,128)(2,1)S(1)} %slice.245), channel_id=1, source_target_pairs={{0,1},{1,2},{2,3},{3,4},{4,5},{5,6},{6,7},{7,8},{8,9},{9,10},{10,1... | collective-permute-start | bytes 147464 | tf_op jit(solution)/shard_map/ppermute | solution.py:14
  65.7 0.0 collective-permute-done.2
  65.7 0.1 fusion.18
  65.8 0.0 copy-start.1
  65.8 5.7 %collective-permute-done.3 = bf16[32,3,256]{2,1,0:T(4,128)(2,1)S(1)} collective-permute-done((bf16[32,3,256]{2,1,0:T(4,128)(2,1)S(1)}, bf16[32,3,256]{2,1,0:T(4,128)(2,1)S(1)}, u32[]{:S(2)}, u32[]{:S(2)}) %collective-permute-start.3) | collective-permute-done | bytes 49184 | tf_op jit(solution)/shard_map/ppermute | solution.py:14
  71.5 0.0 copy-done.1
  71.5 1.9 %scatter-add.19 = f32[1,32,32,256]{3,2,1,0:T(8,128)} dynamic-update-slice(f32[1,32,32,256]{3,2,1,0:T(8,128)} %bitcast.67, f32[1,32,3,256]{3,2,1,0:T(4,128)S(1)} %fusion.17, s32[]{:T(128)} %constant.126.clone.1, s32[]{:T(128)} %constant.126.clone.1, s32[]{:T(128)} %constant.126.clone.1, s32[]{:T(128)} %constant.126.clone.1) | dynamic-update-slice | bytes 196612 | tf_op jit(solution)/shard_map/scatter-add | solution.py:106
  (25 shorter events, 0.5 us)
Async XLA Ops:
  0.0 1.5 %copy-start = (bf16[1024,256]{1,0:T(8,128)(2,1)S(1)}, bf16[1024,256]{1,0:T(8,128)(2,1)}, u32[]{:S(2)}) copy-start(bf16[1024,256]{1,0:T(8,128)(2,1)} %param.13) | copy-start | bytes 1572868
  1.5 1.9 %copy-start.4 = (s32[128,8]{0,1:T(8,128)S(1)}, s32[128,8]{0,1:T(8,128)}, u32[]{:S(2)}) copy-start(s32[128,8]{0,1:T(8,128)} %param.14) | copy-start | bytes 12292
  4.5 37.4 %copy-start.3 = (f32[8,16]{1,0:T(8,128)S(1)}, f32[8,16]{1,0:T(8,128)}, u32[]{:S(2)}) copy-start(f32[8,16]{1,0:T(8,128)} %param.17) | copy-start | bytes 1540
  42.2 1.0 %copy-start.2 = (f32[40,1024]{1,0:T(8,128)}, f32[40,1024]{1,0:T(8,128)S(1)}, u32[]{:S(2)}) copy-start(f32[40,1024]{1,0:T(8,128)S(1)} %select_reduce_fusion.1) | copy-start | bytes 491524
  43.2 0.7 slice-start
  44.2 15.1 %collective-permute-start.1 = (bf16[3,40,256]{2,1,0:T(8,128)(2,1)S(1)}, bf16[3,40,256]{2,1,0:T(8,128)(2,1)S(1)}, u32[]{:S(2)}, u32[]{:S(2)}) collective-permute-start(bf16[3,40,256]{2,1,0:T(8,128)(2,1)S(1)} %convolution_convert_fusion.1), channel_id=1, source_target_pairs={{0,8},{1,9},{2,10},{3,11},{4,12},{5,13},{6,14},{7,15},{8,16},{9,17... | collective-permute-start | bytes 184328 | tf_op jit(solution)/shard_map/ppermute | solution.py:14
  49.0 10.2 %collective-permute-start = (bf16[4,40,256]{2,1,0:T(8,128)(2,1)S(1)}, bf16[4,40,256]{2,1,0:T(8,128)(2,1)S(1)}, u32[]{:S(2)}, u32[]{:S(2)}) collective-permute-start(bf16[4,40,256]{2,1,0:T(8,128)(2,1)S(1)} %convolution_convert_fusion), channel_id=1, source_target_pairs={{8,0},{9,1},{10,2},{11,3},{12,4},{13,5},{14,6},{15,7},{16,8},{17,9... | collective-permute-start | bytes 245768 | tf_op jit(solution)/shard_map/ppermute | solution.py:14
  59.4 6.3 %collective-permute-start.2 = (bf16[32,4,256]{2,1,0:T(4,128)(2,1)S(1)}, bf16[32,4,256]{2,1,0:T(4,128)(2,1)S(1)}, u32[]{:S(2)}, u32[]{:S(2)}) collective-permute-start(bf16[32,4,256]{2,1,0:T(4,128)(2,1)S(1)} %slice.243), channel_id=1, source_target_pairs={{1,0},{2,1},{3,2},{4,3},{5,4},{6,5},{7,6},{8,7},{9,8},{10,9},{11,1... | collective-permute-start | bytes 196616 | tf_op jit(solution)/shard_map/ppermute | solution.py:14
  63.8 7.7 %collective-permute-start.3 = (bf16[32,3,256]{2,1,0:T(4,128)(2,1)S(1)}, bf16[32,3,256]{2,1,0:T(4,128)(2,1)S(1)}, u32[]{:S(2)}, u32[]{:S(2)}) collective-permute-start(bf16[32,3,256]{2,1,0:T(4,128)(2,1)S(1)} %slice.245), channel_id=1, source_target_pairs={{0,1},{1,2},{2,3},{3,4},{4,5},{5,6},{6,7},{7,8},{8,9},{9,10},{10,1... | collective-permute-start | bytes 147464 | tf_op jit(solution)/shard_map/ppermute | solution.py:14
  65.8 5.7 %copy-start.1 = (f32[32,32,256]{2,1,0:T(8,128)}, f32[32,32,256]{2,1,0:T(8,128)S(1)}, u32[]{:S(2)}) copy-start(f32[32,32,256]{2,1,0:T(8,128)S(1)} %fusion.18) | copy-start | bytes 3145732

commit v7 on v3

--- a/solution.py
+++ b/solution.py
@@ -88,22 +88,23 @@
 
     spread_u = spread(kernel_of(taper, meta_rows[2]), meta_rows[0], padded_side)
     spread_v = spread(kernel_of(taper, meta_rows[3]), meta_rows[1], padded_side)
-    low = place_rows(spread_u[0:4], spread_v, arrived_rows)
-    high = place_rows(spread_u[TS + 4 : TS + 7], spread_v, arrived_rows)
+    span = spread_u[0 : TS + 7]
+    edge_lo = place_rows(span, spread_v[0:4], arrived_rows)
+    edge_hi = place_rows(span, spread_v[TS + 4 : TS + 7], arrived_rows)
 
-    from_below = passed_along(low.astype(jnp.bfloat16), "tile", -TILES_Y)
-    from_above = passed_along(high.astype(jnp.bfloat16), "tile", TILES_Y)
-    inner = place_rows(spread_u[4 : TS + 4], spread_v, arrived_rows)
-    inner = inner.at[TS - 4 : TS].add(from_below.astype(jnp.float32))
-    inner = inner.at[0:3].add(from_above.astype(jnp.float32))
     tile_row = lax.axis_index("tile") % TILES_Y
-    from_next = passed_along(inner[:, 0:4], "tile", -1)
-    from_prev = passed_along(inner[:, TS + 4 : TS + 7], "tile", 1)
+    from_next = passed_along(edge_lo, "tile", -1)
+    from_prev = passed_along(edge_hi, "tile", 1)
+    body_cols = place_rows(span, spread_v[4 : TS + 4], arrived_rows)
     from_next = jnp.where(tile_row + 1 < TILES_Y, from_next, 0.0)
     from_prev = jnp.where(tile_row >= 1, from_prev, 0.0)
-    result = inner[:, 4 : TS + 4]
-    result = result.at[:, TS - 4 : TS].add(from_next)
-    result = result.at[:, 0:3].add(from_prev)
+    body_cols = body_cols.at[:, TS - 4 : TS].add(from_next)
+    body_cols = body_cols.at[:, 0:3].add(from_prev)
+    from_below = passed_along(body_cols[0:4].astype(jnp.bfloat16), "tile", -TILES_Y)
+    from_above = passed_along(body_cols[TS + 4 : TS + 7].astype(jnp.bfloat16), "tile", TILES_Y)
+    result = body_cols[4 : TS + 4]
+    result = result.at[TS - 4 : TS].add(from_below.astype(jnp.float32))
+    result = result.at[0:3].add(from_above.astype(jnp.float32))
     return result[None]
 
 

time: 73.8 us -> 78.2 us (1.060)
  blocking collectives: 36.5 us -> 0 us
  waiting for transfers between devices: 9.88 us -> 31.2 us
  starting transfers between devices: 16.8 us -> 31.2 us
  local copies, waits for them, and re-layouts: 4.95 us -> 7.87 us
  other arithmetic: 0.54 us -> 2.74 us
    all_to_all x1 -> x0, blocking collectives: 36.5 us -> none  [body(): lax.all_to_all(packed, 'tile', split_axis=0, concat_axis=0, tiled=True)]
    all_to_all x0 -> x1, waiting for transfers between devices: none -> 20.1 us  [body(): lax.all_to_all(packed, 'tile', split_axis=0, concat_axis=0, tiled=True)]
    all_to_all x0 -> x1, starting transfers between devices: none -> 16.6 us  [body(): lax.all_to_all(packed, 'tile', split_axis=0, concat_axis=0, tiled=True)]
    ppermute x4, starting transfers between devices: 16.8 us -> 14.6 us  [passed_along(): return lax.ppermute(value, axis, pairs)]
    scatter-add x1, local copies, waits for them, and re-layouts: 1.87 us -> 3.52 us  [body(): body_cols = body_cols.at[:, 0:3].add(from_prev)]
    another operation x2 -> x3, other arithmetic: 0.01 us -> 1.55 us
    ppermute x4, waiting for transfers between devices: 9.88 us -> 11.1 us  [passed_along(): return lax.ppermute(value, axis, pairs)]
    another operation x1, local copies, waits for them, and re-layouts: 0.66 us -> 1.73 us  [body(): jnp.stack([jnp.concatenate([outgoing[(h * per_half + j) * tile_count:(h *...]
  transfers between devices with their start and end apart: 4 -> 5, of which waited for: 3 -> 4; matrix products, arithmetic and copies ran while one was open for 2% -> 3% of each run, Pallas kernels for 0% -> 0%
where the time goes in v7:
time: 78.2 us; the launch traced here: 77.8 us
  starting transfers between devices  31.2 us (40%)
  waiting for transfers between devices  31.2 us (40%)
  local copies, waits for them, and re-layouts  7.87 us (10%)
  matrix products  4.41 us (6%)
  other arithmetic  2.74 us (4%)
    all_to_all x1, waiting for transfers between devices, body(): lax.all_to_all(packed, 'tile', split_axis=0, concat_axis=0, tiled=True)  20.1 us
    all_to_all x1, starting transfers between devices, body(): lax.all_to_all(packed, 'tile', split_axis=0, concat_axis=0, tiled=True)  16.6 us
    ppermute x4, starting transfers between devices, passed_along(): return lax.ppermute(value, axis, pairs)  14.6 us
    ppermute x4, waiting for transfers between devices, passed_along(): return lax.ppermute(value, axis, pairs)  11.1 us
    scatter-add x1, local copies, waits for them, and re-layouts, body(): body_cols = body_cols.at[:, 0:3].add(from_prev)  3.52 us
    dot_general x1, matrix products, body(): outgoing = jnp.dot(chosen, visibilities, preferred_element_type=jnp.float32)  1.88 us
    another operation x1, local copies, waits for them, and re-layouts, body(): jnp.stack([jnp.concatenate([outgoing[(h * per_half + j) * tile_count:(h *...  1.73 us
  transfers between devices with their start and end apart: 5, of which 4 were waited for; matrix products, arithmetic and copies ran while one was open for 3% of the time, Pallas kernels for 0%

profile of v7, /device:TPU:68, one launch (start us, length us, event | category | flops | bytes accessed | tf_op | source)
XLA Modules:
  0.0 77.8 jit_solution(1168111344146861456)
XLA Ops:
  0.0 0.0 copy-start
  0.0 0.8 convert.12
  0.8 0.7 convert.13
  1.5 0.0 copy-done
  1.5 0.0 copy-start.3
  1.5 1.9 %fusion.7 = bf16[1024,256]{0,1:T(8,128)(2,1)S(1)} fusion(bf16[1024,256]{1,0:T(8,128)(2,1)S(1)} %copy-done, s32[1024]{0:T(1024)} %bitcast.82), kind=kOutput, calls=%fused_computation.13 | convolution fusion | flops 538181632 | bytes 1052672 | tf_op jit(solution)/shard_map/dot_general | solution.py:49
  3.4 0.0 copy-done.3
  3.4 0.9 %fusion.8 = bf16[4,1024]{1,0:T(4,128)(2,1)S(1)} fusion(s32[1024]{0:T(1024)S(1)} %bitcast.83, bf16[2,1024]{1,0:T(2,128)(2,1)S(1)} %convert.13, bf16[2,1024]{1,0:T(2,128)(2,1)S(1)} %convert.12), kind=kOutput, calls=%fused_computation.16 | convolution fusion | flops 9457664 | bytes 20480 | tf_op jit(solution)/shard_map/dot_general | solution.py:52
  4.4 0.1 pad_maximum_fusion
  4.5 0.0 copy-start.2
  4.5 1.7 %copy.38 = bf16[128,2,1152]{2,1,0:T(2,128)(2,1)} copy(bf16[128,2,1152]{0,2,1:T(8,128)(2,1)S(1)} %pad_maximum_fusion) | data formatting | bytes 1179648 | tf_op jit(solution)/shard_map/stack | solution.py:62
  6.2 16.6 %all-to-all-start = ((bf16[128,2,1152]{2,1,0:T(2,128)(2,1)}), bf16[128,2,1152]{2,1,0:T(2,128)(2,1)S(1)}, u32[]{:S(2)}, u32[]{:S(2)}) async-start(bf16[128,2,1152]{2,1,0:T(2,128)(2,1)} %copy.38), calls=%async_computation | async-start | bytes 1179648 | tf_op jit(solution)/shard_map/all_to_all | solution.py:76
  22.9 20.1 %all-to-all-done = bf16[128,2,1152]{2,1,0:T(2,128)(2,1)S(1)} async-done(((bf16[128,2,1152]{2,1,0:T(2,128)(2,1)}), bf16[128,2,1152]{2,1,0:T(2,128)(2,1)S(1)}, u32[]{:S(2)}, u32[]{:S(2)}) %all-to-all-start) | async-done | bytes 589856 | tf_op jit(solution)/shard_map/all_to_all | solution.py:76
  43.0 0.1 copy.50
  43.2 0.0 copy-done.2
  43.2 0.1 convolution_bitcast_fusion
  43.3 0.1 select_reduce_fusion
  43.4 0.0 copy-start.1
  43.5 0.1 convolution_bitcast_fusion.1
  43.7 0.8 fusion.36
  44.4 0.0 copy-done.1
  44.5 0.1 select_reduce_fusion.1
  44.6 0.0 slice-start
  44.7 0.2 fusion.9
  45.0 0.1 copy.49
  45.1 0.3 slice-done
  45.3 0.3 fusion.11
  45.6 0.1 copy.48
  45.7 2.9 %collective-permute-start = (f32[39,4,256]{2,1,0:T(4,128)S(1)}, f32[39,4,256]{2,1,0:T(4,128)S(1)}, u32[]{:S(2)}, u32[]{:S(2)}) collective-permute-start(f32[39,4,256]{2,1,0:T(4,128)S(1)} %copy.48), channel_id=1, source_target_pairs={{1,0},{2,1},{3,2},{4,3},{5,4},{6,5},{7,6},{8,7},{9,8},{10,9},{11,1... | collective-permute-start | bytes 479240 | tf_op jit(solution)/shard_map/ppermute | solution.py:14
  48.6 1.9 %collective-permute-start.1 = (f32[39,3,256]{2,1,0:T(4,128)S(1)}, f32[39,3,256]{2,1,0:T(4,128)S(1)}, u32[]{:S(2)}, u32[]{:S(2)}) collective-permute-start(f32[39,3,256]{2,1,0:T(4,128)S(1)} %copy.49), channel_id=1, source_target_pairs={{0,1},{1,2},{2,3},{3,4},{4,5},{5,6},{6,7},{7,8},{8,9},{9,10},{10,1... | collective-permute-start | bytes 359432 | tf_op jit(solution)/shard_map/ppermute | solution.py:14
  50.5 0.8 %fusion.2 = f32[39,32,256]{2,1,0:T(8,128)S(1)} fusion(f32[32,1024]{1,0:T(8,128)S(1)} %slice.233, f32[39,1024]{1,0:T(8,128)S(1)} %bitcast.73, bf16[1024,256]{1,0:T(8,128)(2,1)S(1)} %fusion.22), kind=kOutput, calls=%fused_computation.4 | convolution fusion | flops 656867328 | bytes 2093056 | tf_op jit(solution)/shard_map/dot_general | solution.py:32
  51.4 0.0 collective-permute-done
  51.4 0.1 fusion.18
  51.5 5.8 %collective-permute-done.1 = f32[39,3,256]{2,1,0:T(4,128)S(1)} collective-permute-done((f32[39,3,256]{2,1,0:T(4,128)S(1)}, f32[39,3,256]{2,1,0:T(4,128)S(1)}, u32[]{:S(2)}, u32[]{:S(2)}) %collective-permute-start.1) | collective-permute-done | bytes 119840 | tf_op jit(solution)/shard_map/ppermute | solution.py:14
  57.3 0.1 slice_add_fusion
  57.4 3.5 %scatter-add.15 = f32[39,32,256]{2,1,0:T(8,128)S(1)} dynamic-update-slice(f32[39,32,256]{2,1,0:T(8,128)S(1)} %fusion.18, f32[39,3,256]{2,1,0:T(4,128)S(1)} %slice_add_fusion, s32[]{:T(128)} %constant.126.clone.1, s32[]{:T(128)} %constant.126.clone.1, s32[]{:T(128)} %constant.126.clone.1) | dynamic-update-slice | bytes 239620 | tf_op jit(solution)/shard_map/scatter-add | solution.py:102
  60.9 0.1 convert.14
  61.0 4.7 %collective-permute-start.2 = (bf16[4,32,256]{2,1,0:T(8,128)(2,1)S(1)}, bf16[4,32,256]{2,1,0:T(8,128)(2,1)S(1)}, u32[]{:S(2)}, u32[]{:S(2)}) collective-permute-start(bf16[4,32,256]{2,1,0:T(8,128)(2,1)S(1)} %slice.248), channel_id=1, source_target_pairs={{8,0},{9,1},{10,2},{11,3},{12,4},{13,5},{14,6},{15,7},{16,8},{17,9... | collective-permute-start | bytes 196616 | tf_op jit(solution)/shard_map/ppermute | solution.py:14
  65.7 0.1 slice.246
  65.8 5.0 %collective-permute-start.3 = (bf16[3,32,256]{2,1,0:T(8,128)(2,1)S(1)}, bf16[3,32,256]{2,1,0:T(8,128)(2,1)S(1)}, u32[]{:S(2)}, u32[]{:S(2)}) collective-permute-start(bf16[3,32,256]{2,1,0:T(8,128)(2,1)S(1)} %slice.250), channel_id=1, source_target_pairs={{0,8},{1,9},{2,10},{3,11},{4,12},{5,13},{6,14},{7,15},{8,16},{9,17... | collective-permute-start | bytes 147464 | tf_op jit(solution)/shard_map/ppermute | solution.py:14
  70.9 2.0 %collective-permute-done.2 = bf16[4,32,256]{2,1,0:T(8,128)(2,1)S(1)} collective-permute-done((bf16[4,32,256]{2,1,0:T(8,128)(2,1)S(1)}, bf16[4,32,256]{2,1,0:T(8,128)(2,1)S(1)}, u32[]{:S(2)}, u32[]{:S(2)}) %collective-permute-start.2) | collective-permute-done | bytes 65568 | tf_op jit(solution)/shard_map/ppermute | solution.py:14
  72.8 1.0 %copy.101 = f32[1,32,32,256]{3,2,1,0:T(8,128)} copy(f32[1,32,32,256]{3,2,1,0:T(8,128)S(1)} %bitcast.70) | data formatting | bytes 2097152
  73.8 3.3 %collective-permute-done.3 = bf16[3,32,256]{2,1,0:T(8,128)(2,1)S(1)} collective-permute-done((bf16[3,32,256]{2,1,0:T(8,128)(2,1)S(1)}, bf16[3,32,256]{2,1,0:T(8,128)(2,1)S(1)}, u32[]{:S(2)}, u32[]{:S(2)}) %collective-permute-start.3) | collective-permute-done | bytes 49184 | tf_op jit(solution)/shard_map/ppermute | solution.py:14
  77.1 0.7 fusion.21
  (23 shorter events, 0.4 us)
Async XLA Ops:
  0.0 1.5 %copy-start = (bf16[1024,256]{1,0:T(8,128)(2,1)S(1)}, bf16[1024,256]{1,0:T(8,128)(2,1)}, u32[]{:S(2)}) copy-start(bf16[1024,256]{1,0:T(8,128)(2,1)} %param.13) | copy-start | bytes 1572868
  1.5 1.9 %copy-start.3 = (s32[128,8]{0,1:T(8,128)S(1)}, s32[128,8]{0,1:T(8,128)}, u32[]{:S(2)}) copy-start(s32[128,8]{0,1:T(8,128)} %param.14) | copy-start | bytes 12292
  4.5 38.7 %copy-start.2 = (f32[8,16]{1,0:T(8,128)S(1)}, f32[8,16]{1,0:T(8,128)}, u32[]{:S(2)}) copy-start(f32[8,16]{1,0:T(8,128)} %param.17) | copy-start | bytes 1540
  6.2 36.7 %all-to-all-start = ((bf16[128,2,1152]{2,1,0:T(2,128)(2,1)}), bf16[128,2,1152]{2,1,0:T(2,128)(2,1)S(1)}, u32[]{:S(2)}, u32[]{:S(2)}) async-start(bf16[128,2,1152]{2,1,0:T(2,128)(2,1)} %copy.38), calls=%async_computation | async-start | bytes 1179648 | tf_op jit(solution)/shard_map/all_to_all | solution.py:76
  43.4 1.0 %copy-start.1 = (f32[40,1024]{1,0:T(8,128)}, f32[40,1024]{1,0:T(8,128)S(1)}, u32[]{:S(2)}) copy-start(f32[40,1024]{1,0:T(8,128)S(1)} %select_reduce_fusion) | copy-start | bytes 491524
  44.6 0.7 slice-start
  45.7 5.7 %collective-permute-start = (f32[39,4,256]{2,1,0:T(4,128)S(1)}, f32[39,4,256]{2,1,0:T(4,128)S(1)}, u32[]{:S(2)}, u32[]{:S(2)}) collective-permute-start(f32[39,4,256]{2,1,0:T(4,128)S(1)} %copy.48), channel_id=1, source_target_pairs={{1,0},{2,1},{3,2},{4,3},{5,4},{6,5},{7,6},{8,7},{9,8},{10,9},{11,1... | collective-permute-start | bytes 479240 | tf_op jit(solution)/shard_map/ppermute | solution.py:14
  48.6 8.7 %collective-permute-start.1 = (f32[39,3,256]{2,1,0:T(4,128)S(1)}, f32[39,3,256]{2,1,0:T(4,128)S(1)}, u32[]{:S(2)}, u32[]{:S(2)}) collective-permute-start(f32[39,3,256]{2,1,0:T(4,128)S(1)} %copy.49), channel_id=1, source_target_pairs={{0,1},{1,2},{2,3},{3,4},{4,5},{5,6},{6,7},{7,8},{8,9},{9,10},{10,1... | collective-permute-start | bytes 359432 | tf_op jit(solution)/shard_map/ppermute | solution.py:14
  61.0 11.8 %collective-permute-start.2 = (bf16[4,32,256]{2,1,0:T(8,128)(2,1)S(1)}, bf16[4,32,256]{2,1,0:T(8,128)(2,1)S(1)}, u32[]{:S(2)}, u32[]{:S(2)}) collective-permute-start(bf16[4,32,256]{2,1,0:T(8,128)(2,1)S(1)} %slice.248), channel_id=1, source_target_pairs={{8,0},{9,1},{10,2},{11,3},{12,4},{13,5},{14,6},{15,7},{16,8},{17,9... | collective-permute-start | bytes 196616 | tf_op jit(solution)/shard_map/ppermute | solution.py:14
  65.8 11.3 %collective-permute-start.3 = (bf16[3,32,256]{2,1,0:T(8,128)(2,1)S(1)}, bf16[3,32,256]{2,1,0:T(8,128)(2,1)S(1)}, u32[]{:S(2)}, u32[]{:S(2)}) collective-permute-start(bf16[3,32,256]{2,1,0:T(8,128)(2,1)S(1)} %slice.250), channel_id=1, source_target_pairs={{0,8},{1,9},{2,10},{3,11},{4,12},{5,13},{6,14},{7,15},{8,16},{9,17... | collective-permute-start | bytes 147464 | tf_op jit(solution)/shard_map/ppermute | solution.py:14

commit v8 on v3

--- a/solution.py
+++ b/solution.py
@@ -101,9 +101,11 @@
     from_prev = passed_along(inner[:, TS + 4 : TS + 7], "tile", 1)
     from_next = jnp.where(tile_row + 1 < TILES_Y, from_next, 0.0)
     from_prev = jnp.where(tile_row >= 1, from_prev, 0.0)
-    result = inner[:, 4 : TS + 4]
-    result = result.at[:, TS - 4 : TS].add(from_next)
-    result = result.at[:, 0:3].add(from_prev)
+    result = (
+        inner[:, 4 : TS + 4]
+        + jnp.pad(from_next, ((0, 0), (TS - 4, 0), (0, 0)))
+        + jnp.pad(from_prev, ((0, 0), (0, TS - 3), (0, 0)))
+    )
     return result[None]
 
 

time: 73.8 us -> 73.8 us (level)
  the two profiles are of different devices: /device:TPU:68 before, /device:TPU:29 now
where the time goes in v8:
time: 73.8 us; the launch traced here: 73.5 us
  blocking collectives  36.4 us (49%)
  starting transfers between devices  15.2 us (21%)
  waiting for transfers between devices  12.5 us (17%)
  matrix products  4.48 us (6%)
  local copies, waits for them, and re-layouts  2.93 us (4%)
  other arithmetic  1.63 us (2%)
    all_to_all x1, blocking collectives, body(): lax.all_to_all(packed, 'tile', split_axis=0, concat_axis=0, tiled=True)  36.4 us
    ppermute x4, starting transfers between devices, passed_along(): return lax.ppermute(value, axis, pairs)  15.2 us
    ppermute x4, waiting for transfers between devices, passed_along(): return lax.ppermute(value, axis, pairs)  12.5 us
    dot_general x1, matrix products, body(): outgoing = jnp.dot(chosen, visibilities, preferred_element_type=jnp.float32)  1.88 us
  transfers between devices with their start and end apart: 4, of which 2 were waited for; matrix products, arithmetic and copies ran while one was open for 2% of the time, Pallas kernels for 0%

profile of v8, /device:TPU:29, one launch (start us, length us, event | category | flops | bytes accessed | tf_op | source)
XLA Modules:
  0.0 73.5 jit_solution(13317700735222056837)
XLA Ops:
  0.0 0.0 copy-start
  0.0 1.0 %copy-done = bf16[1024,256]{1,0:T(8,128)(2,1)S(1)} copy-done((bf16[1024,256]{1,0:T(8,128)(2,1)S(1)}, bf16[1024,256]{1,0:T(8,128)(2,1)}, u32[]{:S(2)}) %copy-start) | copy-done | bytes 524312
  1.0 0.0 copy-start.3
  1.0 0.0 copy-start.4
  1.0 0.0 copy-start.5
  1.0 1.9 %fusion.7 = bf16[1024,256]{0,1:T(8,128)(2,1)S(1)} fusion(bf16[1024,256]{1,0:T(8,128)(2,1)S(1)} %copy-done, s32[1024]{0:T(1024)} %bitcast.74), kind=kOutput, calls=%fused_computation.13 | convolution fusion | flops 538181632 | bytes 1052672 | tf_op jit(solution)/shard_map/dot_general | solution.py:49
  3.0 0.0 copy-done.3
  3.0 0.0 copy-done.4
  3.1 0.0 copy-done.5
  3.1 0.9 %fusion.8 = bf16[4,1024]{1,0:T(4,128)(2,1)S(1)} fusion(s32[1024]{0:T(1024)S(1)} %bitcast.75, bf16[2,1024]{1,0:T(2,128)(2,1)S(1)} %convert.9, bf16[2,1024]{1,0:T(2,128)(2,1)S(1)} %convert.8), kind=kOutput, calls=%fused_computation.18 | convolution fusion | flops 9457664 | bytes 20480 | tf_op jit(solution)/shard_map/dot_general | solution.py:52
  4.1 0.1 pad_maximum_fusion
  4.1 0.0 copy-start.2
  4.1 0.7 copy.32
  4.8 36.4 %all_to_all.5 = bf16[128,2,1152]{2,1,0:T(2,128)(2,1)S(1)} all-to-all(bf16[128,2,1152]{2,1,0:T(2,128)(2,1)S(1)} %copy.32), channel_id=1, replica_groups=mesh['chan'=4,'tile'=128] {'tile'}, dimensions={0} | all-to-all | bytes 1179648 | tf_op jit(solution)/shard_map/all_to_all | solution.py:76
  41.3 0.1 copy.42
  41.4 0.0 copy-done.2
  41.4 0.1 convolution_bitcast_fusion.1
  41.6 0.1 select_reduce_fusion.1
  41.7 0.0 copy-start.1
  41.8 0.8 %fusion.34 = (bf16[128,1,256]{2,1,0:T(2,128)(2,1)S(1)}, bf16[128,1,256]{2,1,0:T(2,128)(2,1)S(1)}, bf16[128,1,256]{2,1,0:T(2,128)(2,1)S(1)}, bf16[128,1,256]{2,1,...) fusion(bf16[128,2,1152]{2,1,0:T(2,128)(2,1)S(1)} %all_to_all.5), kind=kLoop, calls=%fused_computation.75 | loop fusion | bytes 1048576 | tf_op jit(solution)/shard_map/slice | solution.py:79
  42.5 0.0 copy-done.1
  42.6 0.0 slice-start
  42.6 0.1 convolution_bitcast_fusion
  42.9 0.1 select_reduce_fusion
  43.0 0.2 convolution_convert_fusion.1
  43.3 3.9 %collective-permute-start.1 = (bf16[3,40,256]{2,1,0:T(8,128)(2,1)S(1)}, bf16[3,40,256]{2,1,0:T(8,128)(2,1)S(1)}, u32[]{:S(2)}, u32[]{:S(2)}) collective-permute-start(bf16[3,40,256]{2,1,0:T(8,128)(2,1)S(1)} %convolution_convert_fusion.1), channel_id=1, source_target_pairs={{0,8},{1,9},{2,10},{3,11},{4,12},{5,13},{6,14},{7,15},{8,16},{9,17... | collective-permute-start | bytes 184328 | tf_op jit(solution)/shard_map/ppermute | solution.py:14
  47.1 0.0 slice-done
  47.1 0.3 convolution_convert_fusion
  47.4 1.3 %collective-permute-start = (bf16[4,40,256]{2,1,0:T(8,128)(2,1)S(1)}, bf16[4,40,256]{2,1,0:T(8,128)(2,1)S(1)}, u32[]{:S(2)}, u32[]{:S(2)}) collective-permute-start(bf16[4,40,256]{2,1,0:T(8,128)(2,1)S(1)} %convolution_convert_fusion), channel_id=1, source_target_pairs={{8,0},{9,1},{10,2},{11,3},{12,4},{13,5},{14,6},{15,7},{16,8},{17,9... | collective-permute-start | bytes 245768 | tf_op jit(solution)/shard_map/ppermute | solution.py:14
  48.7 0.9 %fusion.2 = f32[32,40,256]{2,1,0:T(8,128)S(1)} fusion(f32[40,1024]{1,0:T(8,128)S(1)} %select_reduce_fusion, f32[32,1024]{1,0:T(8,128)S(1)} %slice.173, bf16[1024,256]{1,0:T(8,128)(2,1)S(1)} %fusion.20), kind=kOutput, calls=%fused_computation.4 | convolution fusion | flops 673710080 | bytes 2129920 | tf_op jit(solution)/shard_map/dot_general | solution.py:32
  49.6 6.9 %collective-permute-done = bf16[4,40,256]{2,1,0:T(8,128)(2,1)S(1)} collective-permute-done((bf16[4,40,256]{2,1,0:T(8,128)(2,1)S(1)}, bf16[4,40,256]{2,1,0:T(8,128)(2,1)S(1)}, u32[]{:S(2)}, u32[]{:S(2)}) %collective-permute-start) | collective-permute-done | bytes 81952 | tf_op jit(solution)/shard_map/ppermute | solution.py:14
  56.6 0.0 collective-permute-done.1
  56.7 8.1 %collective-permute-start.3 = (f32[32,3,256]{2,1,0:T(4,128)S(1)}, f32[32,3,256]{2,1,0:T(4,128)S(1)}, u32[]{:S(2)}, u32[]{:S(2)}) collective-permute-start(f32[32,3,256]{2,1,0:T(4,128)S(1)} %slice.190), channel_id=1, source_target_pairs={{0,1},{1,2},{2,3},{3,4},{4,5},{5,6},{6,7},{7,8},{8,9},{9,10},{10,1... | collective-permute-start | bytes 294920 | tf_op jit(solution)/shard_map/ppermute | solution.py:14
  64.8 1.9 %collective-permute-start.2 = (f32[32,4,256]{2,1,0:T(4,128)S(1)}, f32[32,4,256]{2,1,0:T(4,128)S(1)}, u32[]{:S(2)}, u32[]{:S(2)}) collective-permute-start(f32[32,4,256]{2,1,0:T(4,128)S(1)} %slice.189), channel_id=1, source_target_pairs={{1,0},{2,1},{3,2},{4,3},{5,4},{6,5},{7,6},{8,7},{9,8},{10,9},{11,1... | collective-permute-start | bytes 393224 | tf_op jit(solution)/shard_map/ppermute | solution.py:14
  66.7 0.0 collective-permute-done.3
  66.8 5.5 %collective-permute-done.2 = f32[32,4,256]{2,1,0:T(4,128)S(1)} collective-permute-done((f32[32,4,256]{2,1,0:T(4,128)S(1)}, f32[32,4,256]{2,1,0:T(4,128)S(1)}, u32[]{:S(2)}, u32[]{:S(2)}) %collective-permute-start.2) | collective-permute-done | bytes 131104 | tf_op jit(solution)/shard_map/ppermute | solution.py:14
  72.3 1.1 %fusion.10 = f32[1,32,32,256]{3,2,1,0:T(8,128)} fusion(f32[32,40,256]{2,1,0:T(8,128)S(1)} %fusion.19, f32[32,3,256]{2,1,0:T(4,128)S(1)} %broadcast_select_fusion, f32[32,4,256]{2,1,0:T(4,128)S(1)} %broadcast_select_fusion.1), kind=kLoop, calls=%fused_computation.21 | loop fusion | flops 524288 | bytes 2326528 | tf_op jit(solution)/shard_map/broadcast_in_dim | solution.py:109
  (28 shorter events, 0.5 us)
Async XLA Ops:
  0.0 1.0 %copy-start = (bf16[1024,256]{1,0:T(8,128)(2,1)S(1)}, bf16[1024,256]{1,0:T(8,128)(2,1)}, u32[]{:S(2)}) copy-start(bf16[1024,256]{1,0:T(8,128)(2,1)} %param.9) | copy-start | bytes 1572868
  1.0 1.9 %copy-start.3 = (s32[2,1024]{1,0:T(2,128)S(1)}, s32[2,1024]{1,0:T(2,128)}, u32[]{:S(2)}) copy-start(s32[2,1024]{1,0:T(2,128)} %param.11) | copy-start | bytes 24580
  1.0 1.9 %copy-start.4 = (s32[2,1024]{1,0:T(2,128)S(1)}, s32[2,1024]{1,0:T(2,128)}, u32[]{:S(2)}) copy-start(s32[2,1024]{1,0:T(2,128)} %param.12) | copy-start | bytes 24580
  1.0 2.1 %copy-start.5 = (s32[128,8]{0,1:T(8,128)S(1)}, s32[128,8]{0,1:T(8,128)}, u32[]{:S(2)}) copy-start(s32[128,8]{0,1:T(8,128)} %param.10) | copy-start | bytes 12292
  4.1 37.3 %copy-start.2 = (f32[8,16]{1,0:T(8,128)S(1)}, f32[8,16]{1,0:T(8,128)}, u32[]{:S(2)}) copy-start(f32[8,16]{1,0:T(8,128)} %param.13) | copy-start | bytes 1540
  41.7 0.8 %copy-start.1 = (f32[40,1024]{1,0:T(8,128)}, f32[40,1024]{1,0:T(8,128)S(1)}, u32[]{:S(2)}) copy-start(f32[40,1024]{1,0:T(8,128)S(1)} %select_reduce_fusion.1) | copy-start | bytes 491524
  42.6 4.6 %slice-start = ((f32[40,1024]{1,0:T(8,128)}), f32[4,1024]{1,0:T(4,128)S(1)}, s32[]{:S(2)}) async-start(f32[40,1024]{1,0:T(8,128)} %copy-done.1), calls=%async_computation.1 | async-start | bytes 32768 | tf_op jit(solution)/shard_map/slice | solution.py:91
  43.3 13.3 %collective-permute-start.1 = (bf16[3,40,256]{2,1,0:T(8,128)(2,1)S(1)}, bf16[3,40,256]{2,1,0:T(8,128)(2,1)S(1)}, u32[]{:S(2)}, u32[]{:S(2)}) collective-permute-start(bf16[3,40,256]{2,1,0:T(8,128)(2,1)S(1)} %convolution_convert_fusion.1), channel_id=1, source_target_pairs={{0,8},{1,9},{2,10},{3,11},{4,12},{5,13},{6,14},{7,15},{8,16},{9,17... | collective-permute-start | bytes 184328 | tf_op jit(solution)/shard_map/ppermute | solution.py:14
  47.4 9.1 %collective-permute-start = (bf16[4,40,256]{2,1,0:T(8,128)(2,1)S(1)}, bf16[4,40,256]{2,1,0:T(8,128)(2,1)S(1)}, u32[]{:S(2)}, u32[]{:S(2)}) collective-permute-start(bf16[4,40,256]{2,1,0:T(8,128)(2,1)S(1)} %convolution_convert_fusion), channel_id=1, source_target_pairs={{8,0},{9,1},{10,2},{11,3},{12,4},{13,5},{14,6},{15,7},{16,8},{17,9... | collective-permute-start | bytes 245768 | tf_op jit(solution)/shard_map/ppermute | solution.py:14
  56.7 10.1 %collective-permute-start.3 = (f32[32,3,256]{2,1,0:T(4,128)S(1)}, f32[32,3,256]{2,1,0:T(4,128)S(1)}, u32[]{:S(2)}, u32[]{:S(2)}) collective-permute-start(f32[32,3,256]{2,1,0:T(4,128)S(1)} %slice.190), channel_id=1, source_target_pairs={{0,1},{1,2},{2,3},{3,4},{4,5},{5,6},{6,7},{7,8},{8,9},{9,10},{10,1... | collective-permute-start | bytes 294920 | tf_op jit(solution)/shard_map/ppermute | solution.py:14
  64.8 7.5 %collective-permute-start.2 = (f32[32,4,256]{2,1,0:T(4,128)S(1)}, f32[32,4,256]{2,1,0:T(4,128)S(1)}, u32[]{:S(2)}, u32[]{:S(2)}) collective-permute-start(f32[32,4,256]{2,1,0:T(4,128)S(1)} %slice.189), channel_id=1, source_target_pairs={{1,0},{2,1},{3,2},{4,3},{5,4},{6,5},{7,6},{8,7},{9,8},{10,9},{11,1... | collective-permute-start | bytes 393224 | tf_op jit(solution)/shard_map/ppermute | solution.py:14

commit v9 on v8

--- a/solution.py
+++ b/solution.py
@@ -46,12 +46,13 @@
     listed = send_list.transpose(1, 0).reshape(-1)
     row_ids = jnp.arange(rows_dev, dtype=jnp.int32)
     chosen = (listed[:, None] == row_ids[None, :]).astype(jnp.bfloat16)
-    outgoing = jnp.dot(chosen, visibilities, preferred_element_type=jnp.float32)
-    outgoing = outgoing.astype(jnp.bfloat16)
     meta_src = jnp.concatenate([pixels, offsets], 0).astype(jnp.bfloat16)
     slot_meta = lax.dot_general(
         meta_src, chosen, (((1,), (1,)), ((), ())), preferred_element_type=jnp.float32
     )
+    slot_meta, visibilities = lax.optimization_barrier((slot_meta, visibilities))
+    outgoing = jnp.dot(chosen, visibilities, preferred_element_type=jnp.float32)
+    outgoing = outgoing.astype(jnp.bfloat16)
     slot_meta = slot_meta.reshape(META, slot_cap, tile_count).transpose(2, 1, 0)
     slot_meta = slot_meta.reshape(tile_count, slot_cap * META).astype(jnp.bfloat16)
     pad = half_lanes - per_half * components

time: 73.8 us -> 74.9 us (1.015)
  the two profiles are of different devices: /device:TPU:29 before, /device:TPU:27 now
where the time goes in v9:
time: 74.9 us; the launch traced here: 74.5 us
  blocking collectives  36.4 us (49%)
  starting transfers between devices  15.2 us (20%)
  waiting for transfers between devices  12.5 us (17%)
  matrix products  5.11 us (7%)
  other arithmetic  3.08 us (4%)
  local copies, waits for them, and re-layouts  1.89 us (3%)
    all_to_all x1, blocking collectives, body(): lax.all_to_all(packed, 'tile', split_axis=0, concat_axis=0, tiled=True)  36.4 us
    ppermute x4, starting transfers between devices, passed_along(): return lax.ppermute(value, axis, pairs)  15.2 us
    ppermute x4, waiting for transfers between devices, passed_along(): return lax.ppermute(value, axis, pairs)  12.5 us
    dot_general x1, matrix products, body(): outgoing = jnp.dot(chosen, visibilities, preferred_element_type=jnp.float32)  1.82 us
    dot_general x1, matrix products, body(): lax.dot_general(meta_src, chosen, (((1,), (1,)), ((), ())), preferred_ele...  1.6 us
  transfers between devices with their start and end apart: 4, of which 2 were waited for; matrix products, arithmetic and copies ran while one was open for 2% of the time, Pallas kernels for 0%

profile of v9, /device:TPU:27, one launch (start us, length us, event | category | flops | bytes accessed | tf_op | source)
XLA Modules:
  0.0 74.5 jit_solution(8449932791528456543)
XLA Ops:
  0.0 0.0 copy-start
  0.0 0.8 %convert.8 = bf16[2,1024]{1,0:T(2,128)(2,1)S(1)} convert(s32[2,1024]{1,0:T(2,128)} %param.11) | non-fusion elementwise | flops 2048 | bytes 12288 | tf_op jit(solution)/shard_map/convert.2
  0.8 0.7 convert.9
  1.5 1.6 %fusion.1 = bf16[4,1024]{1,0:T(4,128)(2,1)S(1)} fusion(s32[1024]{0:T(1024)} %bitcast.81, bf16[2,1024]{1,0:T(2,128)(2,1)S(1)} %convert.9, bf16[2,1024]{1,0:T(2,128)(2,1)S(1)} %convert.8), kind=kOutput, calls=%fused_computation.3 | convolution fusion | flops 9453568 | bytes 20480 | tf_op jit(solution)/shard_map/dot_general | solution.py:50
  3.1 0.0 copy-done
  3.1 1.8 %fusion.7 = bf16[1024,256]{0,1:T(8,128)(2,1)S(1)} fusion(bf16[1024,256]{1,0:T(8,128)(2,1)S(1)} %copy-done, s32[1024]{0:T(1024)} %bitcast.82), kind=kOutput, calls=%fused_computation.13 | convolution fusion | flops 538181632 | bytes 1052672 | tf_op jit(solution)/shard_map/dot_general | solution.py:54
  5.1 0.1 pad_maximum_fusion
  5.1 0.0 copy-start.2
  5.2 0.7 copy.32
  5.8 36.4 %all_to_all.5 = bf16[128,2,1152]{2,1,0:T(2,128)(2,1)S(1)} all-to-all(bf16[128,2,1152]{2,1,0:T(2,128)(2,1)S(1)} %copy.32), channel_id=1, replica_groups=mesh['chan'=4,'tile'=128] {'tile'}, dimensions={0} | all-to-all | bytes 1179648 | tf_op jit(solution)/shard_map/all_to_all | solution.py:77
  42.3 0.1 copy.42
  42.4 0.0 copy-done.2
  42.4 0.1 convolution_bitcast_fusion.1
  42.6 0.1 select_reduce_fusion.1
  42.7 0.0 copy-start.1
  42.8 0.8 %fusion.33 = (bf16[128,1,256]{2,1,0:T(2,128)(2,1)S(1)}, bf16[128,1,256]{2,1,0:T(2,128)(2,1)S(1)}, bf16[128,1,256]{2,1,0:T(2,128)(2,1)S(1)}, bf16[128,1,256]{2,1,...) fusion(bf16[128,2,1152]{2,1,0:T(2,128)(2,1)S(1)} %all_to_all.5), kind=kLoop, calls=%fused_computation.76 | loop fusion | bytes 1048576 | tf_op jit(solution)/shard_map/slice | solution.py:80
  43.6 0.0 copy-done.1
  43.6 0.0 slice-start
  43.6 0.1 convolution_bitcast_fusion
  43.9 0.1 select_reduce_fusion
  44.0 0.2 convolution_convert_fusion.1
  44.3 3.9 %collective-permute-start.1 = (bf16[3,40,256]{2,1,0:T(8,128)(2,1)S(1)}, bf16[3,40,256]{2,1,0:T(8,128)(2,1)S(1)}, u32[]{:S(2)}, u32[]{:S(2)}) collective-permute-start(bf16[3,40,256]{2,1,0:T(8,128)(2,1)S(1)} %convolution_convert_fusion.1), channel_id=1, source_target_pairs={{0,8},{1,9},{2,10},{3,11},{4,12},{5,13},{6,14},{7,15},{8,16},{9,17... | collective-permute-start | bytes 184328 | tf_op jit(solution)/shard_map/ppermute | solution.py:14
  48.1 0.0 slice-done
  48.2 0.3 convolution_convert_fusion
  48.4 1.3 %collective-permute-start = (bf16[4,40,256]{2,1,0:T(8,128)(2,1)S(1)}, bf16[4,40,256]{2,1,0:T(8,128)(2,1)S(1)}, u32[]{:S(2)}, u32[]{:S(2)}) collective-permute-start(bf16[4,40,256]{2,1,0:T(8,128)(2,1)S(1)} %convolution_convert_fusion), channel_id=1, source_target_pairs={{8,0},{9,1},{10,2},{11,3},{12,4},{13,5},{14,6},{15,7},{16,8},{17,9... | collective-permute-start | bytes 245768 | tf_op jit(solution)/shard_map/ppermute | solution.py:14
  49.7 0.9 %fusion.2 = f32[32,40,256]{2,1,0:T(8,128)S(1)} fusion(f32[40,1024]{1,0:T(8,128)S(1)} %select_reduce_fusion, f32[32,1024]{1,0:T(8,128)S(1)} %slice.173, bf16[1024,256]{1,0:T(8,128)(2,1)S(1)} %fusion.19), kind=kOutput, calls=%fused_computation.4 | convolution fusion | flops 673710080 | bytes 2129920 | tf_op jit(solution)/shard_map/dot_general | solution.py:32
  50.6 6.9 %collective-permute-done = bf16[4,40,256]{2,1,0:T(8,128)(2,1)S(1)} collective-permute-done((bf16[4,40,256]{2,1,0:T(8,128)(2,1)S(1)}, bf16[4,40,256]{2,1,0:T(8,128)(2,1)S(1)}, u32[]{:S(2)}, u32[]{:S(2)}) %collective-permute-start) | collective-permute-done | bytes 81952 | tf_op jit(solution)/shard_map/ppermute | solution.py:14
  57.6 0.0 collective-permute-done.1
  57.7 8.1 %collective-permute-start.3 = (f32[32,3,256]{2,1,0:T(4,128)S(1)}, f32[32,3,256]{2,1,0:T(4,128)S(1)}, u32[]{:S(2)}, u32[]{:S(2)}) collective-permute-start(f32[32,3,256]{2,1,0:T(4,128)S(1)} %slice.190), channel_id=1, source_target_pairs={{0,1},{1,2},{2,3},{3,4},{4,5},{5,6},{6,7},{7,8},{8,9},{9,10},{10,1... | collective-permute-start | bytes 294920 | tf_op jit(solution)/shard_map/ppermute | solution.py:14
  65.8 1.9 %collective-permute-start.2 = (f32[32,4,256]{2,1,0:T(4,128)S(1)}, f32[32,4,256]{2,1,0:T(4,128)S(1)}, u32[]{:S(2)}, u32[]{:S(2)}) collective-permute-start(f32[32,4,256]{2,1,0:T(4,128)S(1)} %slice.189), channel_id=1, source_target_pairs={{1,0},{2,1},{3,2},{4,3},{5,4},{6,5},{7,6},{8,7},{9,8},{10,9},{11,1... | collective-permute-start | bytes 393224 | tf_op jit(solution)/shard_map/ppermute | solution.py:14
  67.7 0.0 collective-permute-done.3
  67.8 5.5 %collective-permute-done.2 = f32[32,4,256]{2,1,0:T(4,128)S(1)} collective-permute-done((f32[32,4,256]{2,1,0:T(4,128)S(1)}, f32[32,4,256]{2,1,0:T(4,128)S(1)}, u32[]{:S(2)}, u32[]{:S(2)}) %collective-permute-start.2) | collective-permute-done | bytes 131104 | tf_op jit(solution)/shard_map/ppermute | solution.py:14
  73.3 1.1 %fusion.9 = f32[1,32,32,256]{3,2,1,0:T(8,128)} fusion(f32[32,40,256]{2,1,0:T(8,128)S(1)} %fusion.18, f32[32,3,256]{2,1,0:T(4,128)S(1)} %broadcast_select_fusion, f32[32,4,256]{2,1,0:T(4,128)S(1)} %broadcast_select_fusion.1), kind=kLoop, calls=%fused_computation.20 | loop fusion | flops 524288 | bytes 2326528 | tf_op jit(solution)/shard_map/broadcast_in_dim | solution.py:110
  (28 shorter events, 0.5 us)
Async XLA Ops:
  0.0 3.1 %copy-start = (bf16[1024,256]{1,0:T(8,128)(2,1)S(1)}, bf16[1024,256]{1,0:T(8,128)(2,1)}, u32[]{:S(2)}) copy-start(bf16[1024,256]{1,0:T(8,128)(2,1)} %param.9) | copy-start | bytes 1572868
  5.1 37.3 %copy-start.2 = (f32[8,16]{1,0:T(8,128)S(1)}, f32[8,16]{1,0:T(8,128)}, u32[]{:S(2)}) copy-start(f32[8,16]{1,0:T(8,128)} %param.13) | copy-start | bytes 1540
  42.7 0.8 %copy-start.1 = (f32[40,1024]{1,0:T(8,128)}, f32[40,1024]{1,0:T(8,128)S(1)}, u32[]{:S(2)}) copy-start(f32[40,1024]{1,0:T(8,128)S(1)} %select_reduce_fusion.1) | copy-start | bytes 491524
  43.6 4.6 %slice-start = ((f32[40,1024]{1,0:T(8,128)}), f32[4,1024]{1,0:T(4,128)S(1)}, s32[]{:S(2)}) async-start(f32[40,1024]{1,0:T(8,128)} %copy-done.1), calls=%async_computation.1 | async-start | bytes 32768 | tf_op jit(solution)/shard_map/slice | solution.py:92
  44.3 13.3 %collective-permute-start.1 = (bf16[3,40,256]{2,1,0:T(8,128)(2,1)S(1)}, bf16[3,40,256]{2,1,0:T(8,128)(2,1)S(1)}, u32[]{:S(2)}, u32[]{:S(2)}) collective-permute-start(bf16[3,40,256]{2,1,0:T(8,128)(2,1)S(1)} %convolution_convert_fusion.1), channel_id=1, source_target_pairs={{0,8},{1,9},{2,10},{3,11},{4,12},{5,13},{6,14},{7,15},{8,16},{9,17... | collective-permute-start | bytes 184328 | tf_op jit(solution)/shard_map/ppermute | solution.py:14
  48.4 9.1 %collective-permute-start = (bf16[4,40,256]{2,1,0:T(8,128)(2,1)S(1)}, bf16[4,40,256]{2,1,0:T(8,128)(2,1)S(1)}, u32[]{:S(2)}, u32[]{:S(2)}) collective-permute-start(bf16[4,40,256]{2,1,0:T(8,128)(2,1)S(1)} %convolution_convert_fusion), channel_id=1, source_target_pairs={{8,0},{9,1},{10,2},{11,3},{12,4},{13,5},{14,6},{15,7},{16,8},{17,9... | collective-permute-start | bytes 245768 | tf_op jit(solution)/shard_map/ppermute | solution.py:14
  57.7 10.1 %collective-permute-start.3 = (f32[32,3,256]{2,1,0:T(4,128)S(1)}, f32[32,3,256]{2,1,0:T(4,128)S(1)}, u32[]{:S(2)}, u32[]{:S(2)}) collective-permute-start(f32[32,3,256]{2,1,0:T(4,128)S(1)} %slice.190), channel_id=1, source_target_pairs={{0,1},{1,2},{2,3},{3,4},{4,5},{5,6},{6,7},{7,8},{8,9},{9,10},{10,1... | collective-permute-start | bytes 294920 | tf_op jit(solution)/shard_map/ppermute | solution.py:14
  65.8 7.5 %collective-permute-start.2 = (f32[32,4,256]{2,1,0:T(4,128)S(1)}, f32[32,4,256]{2,1,0:T(4,128)S(1)}, u32[]{:S(2)}, u32[]{:S(2)}) collective-permute-start(f32[32,4,256]{2,1,0:T(4,128)S(1)} %slice.189), channel_id=1, source_target_pairs={{1,0},{2,1},{3,2},{4,3},{5,4},{6,5},{7,6},{8,7},{9,8},{10,9},{11,1... | collective-permute-start | bytes 393224 | tf_op jit(solution)/shard_map/ppermute | solution.py:14
